TPU v7x, 256 devices: a whole 4x4x8 slice. The times are simulated.
256 devices in a mesh: frame: 16 (over z_lo, y), tensor: 8 (over z_hi, x), dp: 2 (over core).
Axes of the slice: x: 4, y: 4, z: 8 (z_hi: 2, z_lo: 4; z = z_hi * 4 + z_lo), core: 2. Of those that a mesh axis runs over, the one named last changes fastest.
Arguments:
- q_proj: bfloat16 [16384, 3072], P(('dp', 'frame'), 'tensor'), parts along dimension 0
- k_proj: bfloat16 [16384, 3072], P(('dp', 'frame'), 'tensor'), parts along dimension 0
- v_proj: bfloat16 [16384, 3072], P(('dp', 'frame'), 'tensor'), parts along dimension 0, may hold values from -6 to 6
- gain_q: float32 [3072], P('tensor'), may hold values from 0.5 to 6
- gain_k: float32 [3072], P('tensor'), may hold values from 0.5 to 6
- tiles: int32 [128, 12], P('dp'), parts along dimension 0, may hold values from 0 to 63, as said below
Outputs:
- attended: bfloat16 [16384, 3072], P(('dp', 'frame'), 'tensor'), parts along dimension 0
There are 2 independent parts, one for each index of `dp`. A program takes and returns all parts, laid end to end along the dimension named above; an argument that names none is the same for every part. Nothing has to cross between parts.
Inputs may be any that keep to these rules, and one draw needn't show every extreme that they name: `tiles`: row q lists 12 distinct key blocks: q first; then 8 blocks whose slab (group of 4 consecutive blocks, one frame slab) is at most 2 slabs from the slab of q; then 3 blocks that are each the first block of a slab more than 2 slabs away. Farther groups are listed less often.
All inputs are finite; a program needn't handle non-finite values.
Results may differ from a plain program's by a relative error of at most 0.007.
The roundings to bfloat16 on the way count: a program that leaves them out, or rounds other values in their place, can miss the bound.
Values may be sent and summed in bfloat16 or wider, within the bound.
No kernel may reach another device: no remote copies, remote signals or barrier semaphores. Data moves between devices by JAX's collectives and lax.ppermute only.
A program may use at most 128 MiB of HBM per device.

v0:
```python
import functools
import math

import jax
import jax.numpy as jnp
from jax import lax
from jax.experimental import pallas as pl
from jax.experimental.pallas import tpu as pltpu
from jax.sharding import PartitionSpec as P


HD = 128
BLK = 128
NEAR = 2

EPS = 1e-06


def attn_kernel(idx_ref, q_ref, k_ref, v_ref, o_ref, s_ref, *, heads, slots):
    i = pl.program_id(0)
    scale = 1.0 / math.sqrt(HD)
    for h in range(heads):
        cols = pl.ds(h * HD, HD)
        qh = q_ref[:, cols]
        top = None
        for j in range(slots):
            kb = idx_ref[i, j]
            kh = k_ref[kb, :, cols]
            s = lax.dot_general(
                qh, kh, (((1,), (1,)), ((), ())), preferred_element_type=jnp.float32
            ) * scale
            s_ref[j] = s
            part = jnp.max(s, axis=1, keepdims=True)
            top = part if top is None else jnp.maximum(top, part)
        total = None
        acc = None
        for j in range(slots):
            kb = idx_ref[i, j]
            w = jnp.exp(s_ref[j] - top)
            part = jnp.sum(w, axis=1, keepdims=True)
            total = part if total is None else total + part
            prod = jnp.dot(
                w.astype(jnp.bfloat16), v_ref[kb, :, cols], preferred_element_type=jnp.float32
            )
            acc = prod if acc is None else acc + prod
        o_ref[:, cols] = (acc / total).astype(o_ref.dtype)


def sparse_attend(idx, qn, k_bank, v_bank):
    tok_rows, width = qn.shape
    heads = width // HD
    q_blocks = tok_rows // BLK
    slots = idx.shape[1]
    n_bank = k_bank.shape[0]
    kernel = functools.partial(attn_kernel, heads=heads, slots=slots)
    grid_spec = pltpu.PrefetchScalarGridSpec(
        num_scalar_prefetch=1,
        grid=(q_blocks,),
        in_specs=[
            pl.BlockSpec((BLK, width), lambda i, idx_ref: (i, 0)),
            pl.BlockSpec((n_bank, BLK, width), lambda i, idx_ref: (0, 0, 0)),
            pl.BlockSpec((n_bank, BLK, width), lambda i, idx_ref: (0, 0, 0)),
        ],
        out_specs=pl.BlockSpec((BLK, width), lambda i, idx_ref: (i, 0)),
        scratch_shapes=[pltpu.VMEM((slots, BLK, BLK), jnp.float32)],
    )
    flops = 4 * q_blocks * slots * heads * BLK * BLK * HD
    return pl.pallas_call(
        kernel,
        grid_spec=grid_spec,
        out_shape=jax.ShapeDtypeStruct((tok_rows, width), jnp.bfloat16),
        compiler_params=pltpu.CompilerParams(vmem_limit_bytes=48 * 1024 * 1024),
        cost_estimate=pl.CostEstimate(
            flops=flops,
            transcendentals=q_blocks * slots * heads * BLK * BLK,
            bytes_accessed=2 * (2 * tok_rows * width + 2 * n_bank * BLK * width),
        ),
    )(idx, qn, k_bank, v_bank)


def xor_gather(piece, n_frame, frame_pos):
    held = piece[None]
    bit = 1
    while bit < n_frame:
        perm = [(i, i ^ bit) for i in range(n_frame)]
        got = lax.ppermute(held, "frame", perm)
        upper = (frame_pos // bit) % 2 == 1
        held = jnp.where(
            upper, jnp.concatenate([got, held], axis=0), jnp.concatenate([held, got], axis=0)
        )
        bit *= 2
    return held


def body(q_proj, k_proj, v_proj, gain_q, gain_k, tiles, *, n_frame):
    tok_rows, width = q_proj.shape
    blocks = tok_rows // BLK
    frame_pos = lax.axis_index("frame")
    full_width = width * lax.axis_size("tensor")
    offsets = list(range(-NEAR, NEAR + 1))
    perms = {
        d: [(i, i - d) for i in range(n_frame) if 0 <= i - d < n_frame] for d in offsets if d != 0
    }

    kv_raw = jnp.stack([k_proj, v_proj])
    first = lax.all_gather(kv_raw[:, :BLK], "frame", axis=1, tiled=False)
    tail = kv_raw[:, BLK:]
    near = {0: tail}
    for d in perms:
        near[d] = lax.ppermute(tail, "frame", perms[d])

    q_wide = q_proj.astype(jnp.float32)
    k_wide = k_proj.astype(jnp.float32)
    row_sums = lax.psum(
        (jnp.sum(q_wide * q_wide, axis=1), jnp.sum(k_wide * k_wide, axis=1)), "tensor"
    )
    q_norm = (q_wide * lax.rsqrt(row_sums[0] / full_width + EPS)[:, None] * gain_q).astype(
        jnp.bfloat16
    )
    k_sum = row_sums[1]
    sum_tail = k_sum[BLK:]
    near_sum = {0: sum_tail}
    for d in perms:
        near_sum[d] = lax.ppermute(sum_tail, "frame", perms[d])
    first_sum = xor_gather(k_sum[:BLK], n_frame, frame_pos)

    bank_sum = jnp.concatenate(
        [near_sum[d].reshape(blocks - 1, BLK) for d in offsets] + [first_sum], axis=0
    )
    k_scale = lax.rsqrt(bank_sum / full_width + EPS)[:, :, None]
    k_raw = jnp.concatenate(
        [near[d][0].reshape(blocks - 1, BLK, width) for d in offsets] + [first[0]], axis=0
    )
    k_bank = (k_raw.astype(jnp.float32) * k_scale * gain_k).astype(jnp.bfloat16)
    v_bank = jnp.concatenate(
        [near[d][1].reshape(blocks - 1, BLK, width) for d in offsets] + [first[1]], axis=0
    )
    n_near = len(offsets) * (blocks - 1)

    q_tiles = lax.dynamic_slice_in_dim(tiles, frame_pos * blocks, blocks, 0)
    key_slab = q_tiles // blocks
    within = q_tiles % blocks
    dist = key_slab - frame_pos
    near_ok = (jnp.abs(dist) <= NEAR) & (within > 0)
    idx = jnp.where(
        near_ok,
        (dist + NEAR) * (blocks - 1) + within - 1,
        n_near + key_slab,
    )
    idx = jnp.clip(idx, 0, n_near + n_frame - 1).astype(jnp.int32)
    return sparse_attend(idx, q_norm, k_bank, v_bank)


def solution(mesh):
    return jax.shard_map(
        functools.partial(body, n_frame=mesh.shape["frame"]),
        mesh=mesh,
        in_specs=(
            P(("dp", "frame"), "tensor"),
            P(("dp", "frame"), "tensor"),
            P(("dp", "frame"), "tensor"),
            P("tensor"),
            P("tensor"),
            P("dp", None),
        ),
        out_specs=P(("dp", "frame"), "tensor"),
        check_vma=False,
    )
```

profile of v0, /device:TPU:50, one launch (start us, length us, event | category | flops | bytes accessed | tf_op | source)
XLA Modules:
  0.0 157.9 jit_solution(8084977896615544724)
XLA Ops:
  6.6 1.8 %pad_maximum_fusion = bf16[2,128,384]{2,1,0:T(8,128)(2,1)} fusion(bf16[1,512,384]{2,1,0:T(8,128)(2,1)} %bitcast.27, bf16[1,512,384]{2,1,0:T(8,128)(2,1)} %bitcast.24), kind=kLoop, calls=%fused_computation.10 | loop fusion | flops 393216 | bytes 983040 | tf_op jit(solution)/shard_map/stack | solution.py:105
  8.4 1.1 multiply_reduce_fusion
  9.5 1.1 fusion
  10.7 25.6 %all-reduce = (f32[512]{0:T(512)S(1)}, f32[512]{0:T(512)S(1)}) all-reduce(f32[512]{0:T(512)S(1)} %fusion, f32[512]{0:T(512)S(1)} %multiply_reduce_fusion), channel_id=1, replica_groups=mesh['frame'=16,'tensor'=8,'dp'=2] {'tensor'}, use_global_device_ids=true, to_apply=%region_1.0 | all-reduce | flops 1024 | bytes 8192 | tf_op jit(solution)/shard_map/psum | solution.py:114
  36.2 2.3 %collective-permute-start.6 = (f32[384]{0:T(512)S(1)}, f32[384]{0:T(512)S(1)}, u32[]{:S(2)}, u32[]{:S(2)}) collective-permute-start(f32[384]{0:T(512)S(1)} %get-tuple-element.18), channel_id=1, source_target_pairs={{16,0},{32,16},{48,32},{64,48},{80,64},{96,80},{112,96},{128,112},... | collective-permute-start | bytes 4616 | tf_op jit(solution)/shard_map/ppermute | solution.py:124
  38.6 5.5 %collective-permute-start.7 = (f32[384]{0:T(512)S(1)}, f32[384]{0:T(512)S(1)}, u32[]{:S(2)}, u32[]{:S(2)}) collective-permute-start(f32[384]{0:T(512)S(1)} %get-tuple-element.18), channel_id=1, source_target_pairs={{32,0},{48,16},{64,32},{80,48},{96,64},{112,80},{128,96},{144,112}... | collective-permute-start | bytes 4616 | tf_op jit(solution)/shard_map/ppermute | solution.py:124
  44.1 2.8 %collective-permute-start.4 = (f32[384]{0:T(512)S(1)}, f32[384]{0:T(512)S(1)}, u32[]{:S(2)}, u32[]{:S(2)}) collective-permute-start(f32[384]{0:T(512)S(1)} %get-tuple-element.18), channel_id=1, source_target_pairs={{0,32},{16,48},{32,64},{48,80},{64,96},{80,112},{96,128},{112,144}... | collective-permute-start | bytes 4616 | tf_op jit(solution)/shard_map/ppermute | solution.py:124
  46.9 1.7 %collective-permute-start.8 = (f32[1,128]{1,0:T(1,128)S(1)}, f32[1,128]{1,0:T(1,128)S(1)}, u32[]{:S(2)}, u32[]{:S(2)}) collective-permute-start(f32[1,128]{1,0:T(1,128)S(1)} %slice_bitcast_fusion), channel_id=1, source_target_pairs={{0,16},{16,0},{32,48},{48,32},{64,80},{80,64},{96,112},{112,96},{1... | collective-permute-start | bytes 1544 | tf_op jit(solution)/shard_map/ppermute | solution.py:86
  48.5 1.9 %fusion.3 = bf16[2,384,384]{2,1,0:T(8,128)(2,1)} fusion(bf16[1,512,384]{2,1,0:T(8,128)(2,1)} %bitcast.25, bf16[1,512,384]{2,1,0:T(8,128)(2,1)} %bitcast.28), kind=kLoop, calls=%fused_computation.9 | loop fusion | flops 294912 | bytes 1376256 | tf_op jit(solution)/shard_map/stack | solution.py:105
  50.5 3.4 %collective-permute-start = (bf16[2,384,384]{2,1,0:T(8,128)(2,1)}, bf16[2,384,384]{2,1,0:T(8,128)(2,1)S(1)}, u32[]{:S(2)}, u32[]{:S(2)}) collective-permute-start(bf16[2,384,384]{2,1,0:T(8,128)(2,1)} %fusion.3), channel_id=1, source_target_pairs={{0,32},{16,48},{32,64},{48,80},{64,96},{80,112},{96,128},{112,144}... | collective-permute-start | bytes 1769480 | tf_op jit(solution)/shard_map/ppermute | solution.py:110
  54.2 2.1 %collective-permute-start.9 = (f32[2,128]{1,0:T(2,128)S(1)}, f32[2,128]{1,0:T(2,128)S(1)}, u32[]{:S(2)}, u32[]{:S(2)}) collective-permute-start(f32[2,128]{1,0:T(2,128)S(1)} %maximum_select_fusion.3), channel_id=1, source_target_pairs={{0,32},{16,48},{32,0},{48,16},{64,96},{80,112},{96,64},{112,80},{1... | collective-permute-start | bytes 3080 | tf_op jit(solution)/shard_map/ppermute | solution.py:86
  56.3 16.0 %collective-permute-done.9 = f32[2,128]{1,0:T(2,128)S(1)} collective-permute-done((f32[2,128]{1,0:T(2,128)S(1)}, f32[2,128]{1,0:T(2,128)S(1)}, u32[]{:S(2)}, u32[]{:S(2)}) %collective-permute-start.9) | collective-permute-done | bytes 1056 | tf_op jit(solution)/shard_map/ppermute | solution.py:86
  72.8 3.2 %collective-permute-done.10 = f32[4,128]{1,0:T(4,128)S(1)} collective-permute-done((f32[4,128]{1,0:T(4,128)S(1)}, f32[4,128]{1,0:T(4,128)S(1)}, u32[]{:S(2)}, u32[]{:S(2)}) %collective-permute-start.10) | collective-permute-done | bytes 2080 | tf_op jit(solution)/shard_map/ppermute | solution.py:86
  76.1 0.7 slice.85
  76.9 0.8 slice.91
  77.6 2.9 %collective-permute-done.11 = f32[8,128]{1,0:T(8,128)S(1)} collective-permute-done((f32[8,128]{1,0:T(8,128)S(1)}, f32[8,128]{1,0:T(8,128)S(1)}, u32[]{:S(2)}, u32[]{:S(2)}) %collective-permute-start.11) | collective-permute-done | bytes 4128 | tf_op jit(solution)/shard_map/ppermute | solution.py:86
  80.5 2.8 %collective-permute-start.5 = (f32[384]{0:T(512)S(1)}, f32[384]{0:T(512)S(1)}, u32[]{:S(2)}, u32[]{:S(2)}) collective-permute-start(f32[384]{0:T(512)S(1)} %get-tuple-element.18), channel_id=1, source_target_pairs={{0,16},{16,32},{32,48},{48,64},{64,80},{80,96},{96,112},{112,128},... | collective-permute-start | bytes 4616 | tf_op jit(solution)/shard_map/ppermute | solution.py:124
  83.4 3.4 %collective-permute-start.1 = (bf16[2,384,384]{2,1,0:T(8,128)(2,1)}, bf16[2,384,384]{2,1,0:T(8,128)(2,1)}, u32[]{:S(2)}, u32[]{:S(2)}) collective-permute-start(bf16[2,384,384]{2,1,0:T(8,128)(2,1)} %fusion.3), channel_id=1, source_target_pairs={{0,16},{16,32},{32,48},{48,64},{64,80},{80,96},{96,112},{112,128},... | collective-permute-start | bytes 1769480 | tf_op jit(solution)/shard_map/ppermute | solution.py:110
  86.8 2.4 %collective-permute-start.2 = (bf16[2,384,384]{2,1,0:T(8,128)(2,1)}, bf16[2,384,384]{2,1,0:T(8,128)(2,1)}, u32[]{:S(2)}, u32[]{:S(2)}) collective-permute-start(bf16[2,384,384]{2,1,0:T(8,128)(2,1)} %fusion.3), channel_id=1, source_target_pairs={{16,0},{32,16},{48,32},{64,48},{80,64},{96,80},{112,96},{128,112},... | collective-permute-start | bytes 1769480 | tf_op jit(solution)/shard_map/ppermute | solution.py:110
  89.2 6.4 %collective-permute-start.3 = (bf16[2,384,384]{2,1,0:T(8,128)(2,1)}, bf16[2,384,384]{2,1,0:T(8,128)(2,1)}, u32[]{:S(2)}, u32[]{:S(2)}) collective-permute-start(bf16[2,384,384]{2,1,0:T(8,128)(2,1)} %fusion.3), channel_id=1, source_target_pairs={{32,0},{48,16},{64,32},{80,48},{96,64},{112,80},{128,96},{144,112}... | collective-permute-start | bytes 1769480 | tf_op jit(solution)/shard_map/ppermute | solution.py:110
  96.1 8.1 %collective-permute-done.1 = bf16[2,384,384]{2,1,0:T(8,128)(2,1)} collective-permute-done((bf16[2,384,384]{2,1,0:T(8,128)(2,1)}, bf16[2,384,384]{2,1,0:T(8,128)(2,1)}, u32[]{:S(2)}, u32[]{:S(2)}) %collective-permute-start.1) | collective-permute-done | bytes 589856 | tf_op jit(solution)/shard_map/ppermute | solution.py:110
  104.3 1.1 fusion.10
  105.5 2.6 %collective-permute-done.2 = bf16[2,384,384]{2,1,0:T(8,128)(2,1)} collective-permute-done((bf16[2,384,384]{2,1,0:T(8,128)(2,1)}, bf16[2,384,384]{2,1,0:T(8,128)(2,1)}, u32[]{:S(2)}, u32[]{:S(2)}) %collective-permute-start.2) | collective-permute-done | bytes 589856 | tf_op jit(solution)/shard_map/ppermute | solution.py:110
  108.1 1.1 fusion.9
  109.3 22.6 %collective-permute-done.3 = bf16[2,384,384]{2,1,0:T(8,128)(2,1)} collective-permute-done((bf16[2,384,384]{2,1,0:T(8,128)(2,1)}, bf16[2,384,384]{2,1,0:T(8,128)(2,1)}, u32[]{:S(2)}, u32[]{:S(2)}) %collective-permute-start.3) | collective-permute-done | bytes 589856 | tf_op jit(solution)/shard_map/ppermute | solution.py:110
  131.9 1.1 fusion.8
  133.2 1.5 copy-done.3
  134.8 2.3 %fusion.7 = (bf16[1,2048,384]{2,1,0:T(8,128)(2,1)S(1)}, bf16[1,2048,384]{2,1,0:T(8,128)(2,1)S(1)}) fusion(bf16[2,2048,384]{2,1,0:T(8,128)(2,1)} %all-gather.3.cloned.1.call-done), kind=kLoop, calls=%fused_computation.43 | loop fusion | bytes 6291456 | tf_op jit(solution)/shard_map/slice | solution.py:136
  137.1 0.4 copy-done.4
  138.3 0.9 multiply_convert_fusion.k_ref
  139.2 0.7 copy-done.2
  139.9 11.1 %shard_map.64 = bf16[512,384]{1,0:T(8,128)(2,1)} custom-call(s32[4,12]{1,0:T(4,128)S(1)} %select_clamp_fusion.idx_ref, bf16[512,384]{1,0:T(8,128)(2,1)S(1)} %fusion.2.q_ref, bf16[31,128,384]{2,1,0:T(8,128)(2,1)S(1)} %multiply_convert_fusion.k_ref, bf16[31,128,384]{2,1,0:T(8,128)(2,1)} %copy-done.2), custom_call_target="tpu_custom_call" | custom-call | flops 1207959552 | bytes 6881280 | tf_op jit(solution)/shard_map/pallas_call | solution.py:68
  (56 shorter events, 2.4 us)
Async XLA Ops:
  6.5 66.1 %copy-start = (s32[64,12]{0,1:T(8,128)S(1)}, s32[64,12]{0,1:T(8,128)}, u32[]{:S(2)}) copy-start(s32[64,12]{0,1:T(8,128)} %param.11) | copy-start | bytes 9220
  6.5 69.6 %copy-start.1 = (bf16[512,384]{1,0:T(8,128)(2,1)S(1)}, bf16[512,384]{1,0:T(8,128)(2,1)}, u32[]{:S(2)}) copy-start(bf16[512,384]{1,0:T(8,128)(2,1)} %param.7) | copy-start | bytes 1179652
  6.5 70.3 %copy-start.5 = (bf16[512,384]{1,0:T(8,128)(2,1)S(1)}, bf16[512,384]{1,0:T(8,128)(2,1)}, u32[]{:S(2)}) copy-start(bf16[512,384]{1,0:T(8,128)(2,1)} %param.8) | copy-start | bytes 1179652
  6.5 47.4 %copy-start.6 = (bf16[512,384]{1,0:T(8,128)(2,1)S(1)}, bf16[512,384]{1,0:T(8,128)(2,1)}, u32[]{:S(2)}) copy-start(bf16[512,384]{1,0:T(8,128)(2,1)} %param.6) | copy-start | bytes 1179652
  6.5 47.4 %copy-start.9 = (f32[384]{0:T(512)S(1)}, f32[384]{0:T(512)}, u32[]{:S(2)}) copy-start(f32[384]{0:T(512)} %param.9) | copy-start | bytes 4612
  6.5 128.2 %all-gather.3.cloned.1.call-start = ((), (), s32[]{:S(2)}) async-start(), calls=%async_computation | async-start | bytes 3342336 | tf_op jit(solution)/shard_map/all_gather | solution.py:106
  36.2 47.1 %collective-permute-start.6 = (f32[384]{0:T(512)S(1)}, f32[384]{0:T(512)S(1)}, u32[]{:S(2)}, u32[]{:S(2)}) collective-permute-start(f32[384]{0:T(512)S(1)} %get-tuple-element.18), channel_id=1, source_target_pairs={{16,0},{32,16},{48,32},{64,48},{80,64},{96,80},{112,96},{128,112},... | collective-permute-start | bytes 4616 | tf_op jit(solution)/shard_map/ppermute | solution.py:124
  38.6 48.2 %collective-permute-start.7 = (f32[384]{0:T(512)S(1)}, f32[384]{0:T(512)S(1)}, u32[]{:S(2)}, u32[]{:S(2)}) collective-permute-start(f32[384]{0:T(512)S(1)} %get-tuple-element.18), channel_id=1, source_target_pairs={{32,0},{48,16},{64,32},{80,48},{96,64},{112,80},{128,96},{144,112}... | collective-permute-start | bytes 4616 | tf_op jit(solution)/shard_map/ppermute | solution.py:124
  44.1 45.1 %collective-permute-start.4 = (f32[384]{0:T(512)S(1)}, f32[384]{0:T(512)S(1)}, u32[]{:S(2)}, u32[]{:S(2)}) collective-permute-start(f32[384]{0:T(512)S(1)} %get-tuple-element.18), channel_id=1, source_target_pairs={{0,32},{16,48},{32,64},{48,80},{64,96},{80,112},{96,128},{112,144}... | collective-permute-start | bytes 4616 | tf_op jit(solution)/shard_map/ppermute | solution.py:124
  46.9 7.3 %collective-permute-start.8 = (f32[1,128]{1,0:T(1,128)S(1)}, f32[1,128]{1,0:T(1,128)S(1)}, u32[]{:S(2)}, u32[]{:S(2)}) collective-permute-start(f32[1,128]{1,0:T(1,128)S(1)} %slice_bitcast_fusion), channel_id=1, source_target_pairs={{0,16},{16,0},{32,48},{48,32},{64,80},{80,64},{96,112},{112,96},{1... | collective-permute-start | bytes 1544 | tf_op jit(solution)/shard_map/ppermute | solution.py:86
  50.5 45.5 %collective-permute-start = (bf16[2,384,384]{2,1,0:T(8,128)(2,1)}, bf16[2,384,384]{2,1,0:T(8,128)(2,1)S(1)}, u32[]{:S(2)}, u32[]{:S(2)}) collective-permute-start(bf16[2,384,384]{2,1,0:T(8,128)(2,1)} %fusion.3), channel_id=1, source_target_pairs={{0,32},{16,48},{32,64},{48,80},{64,96},{80,112},{96,128},{112,144}... | collective-permute-start | bytes 1769480 | tf_op jit(solution)/shard_map/ppermute | solution.py:110
  54.2 18.1 %collective-permute-start.9 = (f32[2,128]{1,0:T(2,128)S(1)}, f32[2,128]{1,0:T(2,128)S(1)}, u32[]{:S(2)}, u32[]{:S(2)}) collective-permute-start(f32[2,128]{1,0:T(2,128)S(1)} %maximum_select_fusion.3), channel_id=1, source_target_pairs={{0,32},{16,48},{32,0},{48,16},{64,96},{80,112},{96,64},{112,80},{1... | collective-permute-start | bytes 3080 | tf_op jit(solution)/shard_map/ppermute | solution.py:86
  72.3 3.7 %collective-permute-start.10 = (f32[4,128]{1,0:T(4,128)S(1)}, f32[4,128]{1,0:T(4,128)S(1)}, u32[]{:S(2)}, u32[]{:S(2)}) collective-permute-start(f32[4,128]{1,0:T(4,128)S(1)} %maximum_select_fusion.2), channel_id=1, source_target_pairs={{0,64},{16,80},{32,96},{48,112},{64,0},{80,16},{96,32},{112,48},{1... | collective-permute-start | bytes 6152 | tf_op jit(solution)/shard_map/ppermute | solution.py:86
  76.0 4.6 %collective-permute-start.11 = (f32[8,128]{1,0:T(8,128)S(1)}, f32[8,128]{1,0:T(8,128)S(1)}, u32[]{:S(2)}, u32[]{:S(2)}) collective-permute-start(f32[8,128]{1,0:T(8,128)S(1)} %maximum_select_fusion.1), channel_id=1, source_target_pairs={{0,128},{16,144},{32,160},{48,176},{64,192},{80,208},{96,224},{112... | collective-permute-start | bytes 12296 | tf_op jit(solution)/shard_map/ppermute | solution.py:86
  80.5 15.1 %collective-permute-start.5 = (f32[384]{0:T(512)S(1)}, f32[384]{0:T(512)S(1)}, u32[]{:S(2)}, u32[]{:S(2)}) collective-permute-start(f32[384]{0:T(512)S(1)} %get-tuple-element.18), channel_id=1, source_target_pairs={{0,16},{16,32},{32,48},{48,64},{64,80},{80,96},{96,112},{112,128},... | collective-permute-start | bytes 4616 | tf_op jit(solution)/shard_map/ppermute | solution.py:124
  83.4 20.9 %collective-permute-start.1 = (bf16[2,384,384]{2,1,0:T(8,128)(2,1)}, bf16[2,384,384]{2,1,0:T(8,128)(2,1)}, u32[]{:S(2)}, u32[]{:S(2)}) collective-permute-start(bf16[2,384,384]{2,1,0:T(8,128)(2,1)} %fusion.3), channel_id=1, source_target_pairs={{0,16},{16,32},{32,48},{48,64},{64,80},{80,96},{96,112},{112,128},... | collective-permute-start | bytes 1769480 | tf_op jit(solution)/shard_map/ppermute | solution.py:110
  86.8 21.3 %collective-permute-start.2 = (bf16[2,384,384]{2,1,0:T(8,128)(2,1)}, bf16[2,384,384]{2,1,0:T(8,128)(2,1)}, u32[]{:S(2)}, u32[]{:S(2)}) collective-permute-start(bf16[2,384,384]{2,1,0:T(8,128)(2,1)} %fusion.3), channel_id=1, source_target_pairs={{16,0},{32,16},{48,32},{64,48},{80,64},{96,80},{112,96},{128,112},... | collective-permute-start | bytes 1769480 | tf_op jit(solution)/shard_map/ppermute | solution.py:110
  89.2 42.6 %collective-permute-start.3 = (bf16[2,384,384]{2,1,0:T(8,128)(2,1)}, bf16[2,384,384]{2,1,0:T(8,128)(2,1)}, u32[]{:S(2)}, u32[]{:S(2)}) collective-permute-start(bf16[2,384,384]{2,1,0:T(8,128)(2,1)} %fusion.3), channel_id=1, source_target_pairs={{32,0},{48,16},{64,32},{80,48},{96,64},{112,80},{128,96},{144,112}... | collective-permute-start | bytes 1769480 | tf_op jit(solution)/shard_map/ppermute | solution.py:110
  95.9 9.5 %copy-start.8 = (bf16[1,384,384]{2,1,0:T(8,128)(2,1)S(1)}, bf16[1,384,384]{2,1,0:T(8,128)(2,1)}, u32[]{:S(2)}) copy-start(bf16[1,384,384]{2,1,0:T(8,128)(2,1)} %slice.85) | copy-start | bytes 884740
  96.1 37.0 %copy-start.7 = (bf16[1,384,384]{2,1,0:T(8,128)(2,1)S(1)}, bf16[1,384,384]{2,1,0:T(8,128)(2,1)}, u32[]{:S(2)}) copy-start(bf16[1,384,384]{2,1,0:T(8,128)(2,1)} %slice.91) | copy-start | bytes 884740
  133.0 1.7 %copy-start.3 = (bf16[31,128,384]{2,1,0:T(8,128)(2,1)}, bf16[31,128,384]{2,1,0:T(8,128)(2,1)S(1)}, u32[]{:S(2)}) copy-start(bf16[31,128,384]{2,1,0:T(8,128)(2,1)S(1)} %constant_dynamic-update-slice_fusion.1) | copy-start | bytes 9142276
  134.8 2.8 %copy-start.4 = (bf16[31,128,384]{2,1,0:T(8,128)(2,1)S(1)}, bf16[31,128,384]{2,1,0:T(8,128)(2,1)}, u32[]{:S(2)}) copy-start(bf16[31,128,384]{2,1,0:T(8,128)(2,1)} %copy-done.3) | copy-start | bytes 9142276
  137.6 0.7 copy-start.10
  138.3 1.6 %copy-start.2 = (bf16[31,128,384]{2,1,0:T(8,128)(2,1)}, bf16[31,128,384]{2,1,0:T(8,128)(2,1)S(1)}, u32[]{:S(2)}) copy-start(bf16[31,128,384]{2,1,0:T(8,128)(2,1)S(1)} %constant_dynamic-update-slice_fusion.6.v_ref) | copy-start | bytes 9142276
Sparse Core Ops, SparseCore 0:
  9.2 99.1 all-gather.2
where the time goes:
time: 158 us
  waiting for transfers between devices  55.5 us (35%)
  starting transfers between devices  33.3 us (21%)
  blocking collectives  25.6 us (16%)
  between operations  13.9 us (9%)
  local copies, waits for them, and re-layouts  11.4 us (7%)
  Pallas kernels  11.1 us (7%)
  other arithmetic  7.15 us (5%)
    ppermute x4, waiting for transfers between devices, body(): near[d] = lax.ppermute(tail, 'frame', perms[d])  33.3 us
    psum x1, blocking collectives, body(): lax.psum((jnp.sum(q_wide * q_wide, axis=1), jnp.sum(k_wide * k_wide, axis...  25.6 us
    ppermute x4, waiting for transfers between devices, xor_gather(): got = lax.ppermute(held, 'frame', perm)  22.1 us
    ppermute x4, starting transfers between devices, body(): near[d] = lax.ppermute(tail, 'frame', perms[d])  15.7 us
    ppermute x4, starting transfers between devices, body(): near_sum[d] = lax.ppermute(sum_tail, 'frame', perms[d])  13.4 us
    pallas_call x1, Pallas kernels, sparse_attend(): pl.pallas_call(kernel, grid_spec=grid_spec, out_shape=jax.ShapeDtypeStruc...  11.1 us
    slice x5, local copies, waits for them, and re-layouts, body(): near[d][1].reshape(blocks - 1, BLK, width)  4.15 us
    ppermute x4, starting transfers between devices, xor_gather(): got = lax.ppermute(held, 'frame', perm)  4.13 us
  transfers between devices with their start and end apart: 13, of which 6 were waited for; matrix products, arithmetic and copies ran while one was open for 6% of the time, Pallas kernels for 0%

commit v1 on v0

--- a/solution.py
+++ b/solution.py
@@ -118,15 +118,10 @@
         jnp.bfloat16
     )
     k_sum = row_sums[1]
-    sum_tail = k_sum[BLK:]
-    near_sum = {0: sum_tail}
-    for d in perms:
-        near_sum[d] = lax.ppermute(sum_tail, "frame", perms[d])
-    first_sum = xor_gather(k_sum[:BLK], n_frame, frame_pos)
-
-    bank_sum = jnp.concatenate(
-        [near_sum[d].reshape(blocks - 1, BLK) for d in offsets] + [first_sum], axis=0
-    )
+    all_sum = xor_gather(k_sum, n_frame, frame_pos)
+    near_slab = jnp.clip(frame_pos + jnp.array(offsets), 0, n_frame - 1)
+    near_sum = all_sum[near_slab][:, BLK:].reshape(len(offsets) * (blocks - 1), BLK)
+    bank_sum = jnp.concatenate([near_sum, all_sum[:, :BLK]], axis=0)
     k_scale = lax.rsqrt(bank_sum / full_width + EPS)[:, :, None]
     k_raw = jnp.concatenate(
         [near[d][0].reshape(blocks - 1, BLK, width) for d in offsets] + [first[0]], axis=0

time: 158 us -> 156 us (0.987)
  the two profiles are of different devices: /device:TPU:50 before, /device:TPU:64 now
where the time goes in v1:
time: 156 us; the launch traced here: 155 us
  starting transfers between devices  48.6 us (31%)
  waiting for transfers between devices  32.1 us (21%)
  blocking collectives  31.3 us (20%)
  between operations  13.9 us (9%)
  local copies, waits for them, and re-layouts  11.7 us (8%)
  Pallas kernels  11.1 us (7%)
  other arithmetic  6.16 us (4%)
    ppermute x4, starting transfers between devices, xor_gather(): got = lax.ppermute(held, 'frame', perm)  33.6 us
    ppermute x4, waiting for transfers between devices, xor_gather(): got = lax.ppermute(held, 'frame', perm)  32 us
    psum x1, blocking collectives, body(): lax.psum((jnp.sum(q_wide * q_wide, axis=1), jnp.sum(k_wide * k_wide, axis...  31.3 us
    ppermute x4, starting transfers between devices, body(): near[d] = lax.ppermute(tail, 'frame', perms[d])  15 us
    pallas_call x1, Pallas kernels, sparse_attend(): pl.pallas_call(kernel, grid_spec=grid_spec, out_shape=jax.ShapeDtypeStruc...  11.1 us
    slice x5, local copies, waits for them, and re-layouts, body(): near[d][1].reshape(blocks - 1, BLK, width)  4.19 us
    another operation x2, other arithmetic, body(): kv_raw = jnp.stack([k_proj, v_proj])  3.68 us
    unnamed x35, local copies, waits for them, and re-layouts  3.15 us
  transfers between devices with their start and end apart: 9, of which 4 were waited for; matrix products, arithmetic and copies ran while one was open for 6% of the time, Pallas kernels for 0%

profile of v1, /device:TPU:64, one launch (start us, length us, event | category | flops | bytes accessed | tf_op | source)
XLA Modules:
  0.0 154.9 jit_solution(10709924723508366093)
XLA Ops:
  6.6 1.7 %pad_maximum_fusion = bf16[2,128,384]{2,1,0:T(8,128)(2,1)} fusion(bf16[1,512,384]{2,1,0:T(8,128)(2,1)} %bitcast.20, bf16[1,512,384]{2,1,0:T(8,128)(2,1)} %bitcast.17), kind=kLoop, calls=%fused_computation.11 | loop fusion | flops 393216 | bytes 983040 | tf_op jit(solution)/shard_map/stack | solution.py:105
  8.4 2.0 %fusion.3 = bf16[2,384,384]{2,1,0:T(8,128)(2,1)} fusion(bf16[1,512,384]{2,1,0:T(8,128)(2,1)} %bitcast.18, bf16[1,512,384]{2,1,0:T(8,128)(2,1)} %bitcast.21), kind=kLoop, calls=%fused_computation.10 | loop fusion | flops 294912 | bytes 1376256 | tf_op jit(solution)/shard_map/stack | solution.py:105
  10.3 5.1 %collective-permute-start = (bf16[2,384,384]{2,1,0:T(8,128)(2,1)}, bf16[2,384,384]{2,1,0:T(8,128)(2,1)S(1)}, u32[]{:S(2)}, u32[]{:S(2)}) collective-permute-start(bf16[2,384,384]{2,1,0:T(8,128)(2,1)} %fusion.3), channel_id=1, source_target_pairs={{0,32},{16,48},{32,64},{48,80},{64,96},{80,112},{96,128},{112,144}... | collective-permute-start | bytes 1769480 | tf_op jit(solution)/shard_map/ppermute | solution.py:110
  15.4 2.6 %collective-permute-start.1 = (bf16[2,384,384]{2,1,0:T(8,128)(2,1)}, bf16[2,384,384]{2,1,0:T(8,128)(2,1)}, u32[]{:S(2)}, u32[]{:S(2)}) collective-permute-start(bf16[2,384,384]{2,1,0:T(8,128)(2,1)} %fusion.3), channel_id=1, source_target_pairs={{0,16},{16,32},{32,48},{48,64},{64,80},{80,96},{96,112},{112,128},... | collective-permute-start | bytes 1769480 | tf_op jit(solution)/shard_map/ppermute | solution.py:110
  18.0 5.4 %collective-permute-start.2 = (bf16[2,384,384]{2,1,0:T(8,128)(2,1)}, bf16[2,384,384]{2,1,0:T(8,128)(2,1)}, u32[]{:S(2)}, u32[]{:S(2)}) collective-permute-start(bf16[2,384,384]{2,1,0:T(8,128)(2,1)} %fusion.3), channel_id=1, source_target_pairs={{16,0},{32,16},{48,32},{64,48},{80,64},{96,80},{112,96},{128,112},... | collective-permute-start | bytes 1769480 | tf_op jit(solution)/shard_map/ppermute | solution.py:110
  23.4 1.9 %collective-permute-start.3 = (bf16[2,384,384]{2,1,0:T(8,128)(2,1)}, bf16[2,384,384]{2,1,0:T(8,128)(2,1)}, u32[]{:S(2)}, u32[]{:S(2)}) collective-permute-start(bf16[2,384,384]{2,1,0:T(8,128)(2,1)} %fusion.3), channel_id=1, source_target_pairs={{32,0},{48,16},{64,32},{80,48},{96,64},{112,80},{128,96},{144,112}... | collective-permute-start | bytes 1769480 | tf_op jit(solution)/shard_map/ppermute | solution.py:110
  25.3 1.1 multiply_reduce_fusion
  26.5 0.2 fusion
  26.6 31.3 %all-reduce = (f32[512]{0:T(512)S(1)}, f32[1,512]{1,0:T(1,128)S(1)}) all-reduce(f32[512]{0:T(512)S(1)} %fusion, f32[1,512]{1,0:T(1,128)S(1)} %bitcast.33), channel_id=1, replica_groups=mesh['frame'=16,'tensor'=8,'dp'=2] {'tensor'}, use_global_device_ids=true, to_apply=%region_1.0 | all-reduce | flops 1024 | bytes 8192 | tf_op jit(solution)/shard_map/psum | solution.py:114
  58.0 0.9 collective-permute-start.4
  58.9 0.2 fusion.2.q_ref
  59.2 0.1 copy.9
  59.3 22.3 %collective-permute-done.4 = f32[1,512]{1,0:T(1,128)S(1)} collective-permute-done((f32[1,512]{1,0:T(1,128)S(1)}, f32[1,512]{1,0:T(1,128)S(1)}, u32[]{:S(2)}, u32[]{:S(2)}) %collective-permute-start.4) | collective-permute-done | bytes 2080 | tf_op jit(solution)/shard_map/ppermute | solution.py:86
  81.6 0.1 collective-permute-start.5
  81.7 5.1 %collective-permute-done.5 = f32[2,512]{1,0:T(2,128)S(1)} collective-permute-done((f32[2,512]{1,0:T(2,128)S(1)}, f32[2,512]{1,0:T(2,128)S(1)}, u32[]{:S(2)}, u32[]{:S(2)}) %collective-permute-start.5) | collective-permute-done | bytes 4128 | tf_op jit(solution)/shard_map/ppermute | solution.py:86
  86.8 32.5 %collective-permute-start.6 = (f32[4,512]{1,0:T(4,128)S(1)}, f32[4,512]{1,0:T(4,128)S(1)}, u32[]{:S(2)}, u32[]{:S(2)}) collective-permute-start(f32[4,512]{1,0:T(4,128)S(1)} %maximum_select_fusion.2), channel_id=1, source_target_pairs={{0,64},{16,80},{32,96},{48,112},{64,0},{80,16},{96,32},{112,48},{1... | collective-permute-start | bytes 24584 | tf_op jit(solution)/shard_map/ppermute | solution.py:86
  119.4 1.6 %collective-permute-done.6 = f32[4,512]{1,0:T(4,128)S(1)} collective-permute-done((f32[4,512]{1,0:T(4,128)S(1)}, f32[4,512]{1,0:T(4,128)S(1)}, u32[]{:S(2)}, u32[]{:S(2)}) %collective-permute-start.6) | collective-permute-done | bytes 8224 | tf_op jit(solution)/shard_map/ppermute | solution.py:86
  121.1 0.7 slice.76
  121.9 0.7 slice.84
  122.6 3.1 %collective-permute-done.7 = f32[8,512]{1,0:T(8,128)S(1)} collective-permute-done((f32[8,512]{1,0:T(8,128)S(1)}, f32[8,512]{1,0:T(8,128)S(1)}, u32[]{:S(2)}, u32[]{:S(2)}) %collective-permute-start.7) | collective-permute-done | bytes 16416 | tf_op jit(solution)/shard_map/ppermute | solution.py:86
  125.7 0.6 gather_fusion
  126.5 1.2 fusion.12
  127.8 1.1 fusion.11
  129.0 1.1 fusion.10
  130.3 1.4 copy-done.3
  131.9 2.3 %fusion.9 = (bf16[1,2048,384]{2,1,0:T(8,128)(2,1)S(1)}, bf16[1,2048,384]{2,1,0:T(8,128)(2,1)S(1)}) fusion(bf16[2,2048,384]{2,1,0:T(8,128)(2,1)} %all-gather.3.cloned.1.call-done), kind=kLoop, calls=%fused_computation.46 | loop fusion | bytes 6291456 | tf_op jit(solution)/shard_map/slice | solution.py:131
  134.2 0.4 copy-done.4
  134.7 0.3 constant_dynamic-update-slice_fusion
  135.0 0.3 constant_dynamic-update-slice_fusion.6.v_ref
  135.4 0.9 multiply_convert_fusion.k_ref
  136.3 0.7 copy-done.2
  137.0 11.1 %shard_map.73 = bf16[512,384]{1,0:T(8,128)(2,1)} custom-call(s32[4,12]{1,0:T(4,128)S(1)} %select_clamp_fusion.idx_ref, bf16[512,384]{1,0:T(8,128)(2,1)S(1)} %fusion.2.q_ref, bf16[31,128,384]{2,1,0:T(8,128)(2,1)S(1)} %multiply_convert_fusion.k_ref, bf16[31,128,384]{2,1,0:T(8,128)(2,1)} %copy-done.2), custom_call_target="tpu_custom_call" | custom-call | flops 1207959552 | bytes 6881280 | tf_op jit(solution)/shard_map/pallas_call | solution.py:68
  (53 shorter events, 0.9 us)
Async XLA Ops:
  6.5 52.5 %copy-start = (s32[64,12]{0,1:T(8,128)S(1)}, s32[64,12]{0,1:T(8,128)}, u32[]{:S(2)}) copy-start(s32[64,12]{0,1:T(8,128)} %param.12) | copy-start | bytes 9220
  6.5 112.8 %copy-start.11 = (s32[5]{0:T(128)S(1)}, s32[5]{0:T(128)}, u32[]{:S(2)}) copy-start(s32[5]{0:T(128)} %constant.119.clone) | copy-start | bytes 64
  6.5 114.6 %copy-start.1 = (bf16[512,384]{1,0:T(8,128)(2,1)S(1)}, bf16[512,384]{1,0:T(8,128)(2,1)}, u32[]{:S(2)}) copy-start(bf16[512,384]{1,0:T(8,128)(2,1)} %param.8) | copy-start | bytes 1179652
  6.5 115.3 %copy-start.5 = (bf16[512,384]{1,0:T(8,128)(2,1)S(1)}, bf16[512,384]{1,0:T(8,128)(2,1)}, u32[]{:S(2)}) copy-start(bf16[512,384]{1,0:T(8,128)(2,1)} %param.9) | copy-start | bytes 1179652
  6.5 19.9 %copy-start.6 = (bf16[512,384]{1,0:T(8,128)(2,1)S(1)}, bf16[512,384]{1,0:T(8,128)(2,1)}, u32[]{:S(2)}) copy-start(bf16[512,384]{1,0:T(8,128)(2,1)} %param.7) | copy-start | bytes 1179652
  6.5 52.3 %copy-start.9 = (f32[384]{0:T(512)S(1)}, f32[384]{0:T(512)}, u32[]{:S(2)}) copy-start(f32[384]{0:T(512)} %param.10) | copy-start | bytes 4612
  6.6 125.3 %all-gather.3.cloned.1.call-start = ((), (), s32[]{:S(2)}) async-start(), calls=%async_computation | async-start | bytes 3342336 | tf_op jit(solution)/shard_map/all_gather | solution.py:106
  10.3 116.0 %collective-permute-start = (bf16[2,384,384]{2,1,0:T(8,128)(2,1)}, bf16[2,384,384]{2,1,0:T(8,128)(2,1)S(1)}, u32[]{:S(2)}, u32[]{:S(2)}) collective-permute-start(bf16[2,384,384]{2,1,0:T(8,128)(2,1)} %fusion.3), channel_id=1, source_target_pairs={{0,32},{16,48},{32,64},{48,80},{64,96},{80,112},{96,128},{112,144}... | collective-permute-start | bytes 1769480 | tf_op jit(solution)/shard_map/ppermute | solution.py:110
  15.4 111.1 %collective-permute-start.1 = (bf16[2,384,384]{2,1,0:T(8,128)(2,1)}, bf16[2,384,384]{2,1,0:T(8,128)(2,1)}, u32[]{:S(2)}, u32[]{:S(2)}) collective-permute-start(bf16[2,384,384]{2,1,0:T(8,128)(2,1)} %fusion.3), channel_id=1, source_target_pairs={{0,16},{16,32},{32,48},{48,64},{64,80},{80,96},{96,112},{112,128},... | collective-permute-start | bytes 1769480 | tf_op jit(solution)/shard_map/ppermute | solution.py:110
  18.0 109.8 %collective-permute-start.2 = (bf16[2,384,384]{2,1,0:T(8,128)(2,1)}, bf16[2,384,384]{2,1,0:T(8,128)(2,1)}, u32[]{:S(2)}, u32[]{:S(2)}) collective-permute-start(bf16[2,384,384]{2,1,0:T(8,128)(2,1)} %fusion.3), channel_id=1, source_target_pairs={{16,0},{32,16},{48,32},{64,48},{80,64},{96,80},{112,96},{128,112},... | collective-permute-start | bytes 1769480 | tf_op jit(solution)/shard_map/ppermute | solution.py:110
  23.4 105.6 %collective-permute-start.3 = (bf16[2,384,384]{2,1,0:T(8,128)(2,1)}, bf16[2,384,384]{2,1,0:T(8,128)(2,1)}, u32[]{:S(2)}, u32[]{:S(2)}) collective-permute-start(bf16[2,384,384]{2,1,0:T(8,128)(2,1)} %fusion.3), channel_id=1, source_target_pairs={{32,0},{48,16},{64,32},{80,48},{96,64},{112,80},{128,96},{144,112}... | collective-permute-start | bytes 1769480 | tf_op jit(solution)/shard_map/ppermute | solution.py:110
  58.0 23.6 %collective-permute-start.4 = (f32[1,512]{1,0:T(1,128)S(1)}, f32[1,512]{1,0:T(1,128)S(1)}, u32[]{:S(2)}, u32[]{:S(2)}) collective-permute-start(f32[1,512]{1,0:T(1,128)S(1)} %get-tuple-element.6), channel_id=1, source_target_pairs={{0,16},{16,0},{32,48},{48,32},{64,80},{80,64},{96,112},{112,96},{1... | collective-permute-start | bytes 6152 | tf_op jit(solution)/shard_map/ppermute | solution.py:86
  81.6 5.2 %collective-permute-start.5 = (f32[2,512]{1,0:T(2,128)S(1)}, f32[2,512]{1,0:T(2,128)S(1)}, u32[]{:S(2)}, u32[]{:S(2)}) collective-permute-start(f32[2,512]{1,0:T(2,128)S(1)} %maximum_select_fusion.3), channel_id=1, source_target_pairs={{0,32},{16,48},{32,0},{48,16},{64,96},{80,112},{96,64},{112,80},{1... | collective-permute-start | bytes 12296 | tf_op jit(solution)/shard_map/ppermute | solution.py:86
  86.8 34.1 %collective-permute-start.6 = (f32[4,512]{1,0:T(4,128)S(1)}, f32[4,512]{1,0:T(4,128)S(1)}, u32[]{:S(2)}, u32[]{:S(2)}) collective-permute-start(f32[4,512]{1,0:T(4,128)S(1)} %maximum_select_fusion.2), channel_id=1, source_target_pairs={{0,64},{16,80},{32,96},{48,112},{64,0},{80,16},{96,32},{112,48},{1... | collective-permute-start | bytes 24584 | tf_op jit(solution)/shard_map/ppermute | solution.py:86
  121.0 4.7 %collective-permute-start.7 = (f32[8,512]{1,0:T(8,128)S(1)}, f32[8,512]{1,0:T(8,128)S(1)}, u32[]{:S(2)}, u32[]{:S(2)}) collective-permute-start(f32[8,512]{1,0:T(8,128)S(1)} %maximum_select_fusion.1), channel_id=1, source_target_pairs={{0,128},{16,144},{32,160},{48,176},{64,192},{80,208},{96,224},{112... | collective-permute-start | bytes 49160 | tf_op jit(solution)/shard_map/ppermute | solution.py:86
  126.3 1.4 copy-start.8
  126.5 3.7 %copy-start.7 = (bf16[1,384,384]{2,1,0:T(8,128)(2,1)S(1)}, bf16[1,384,384]{2,1,0:T(8,128)(2,1)}, u32[]{:S(2)}) copy-start(bf16[1,384,384]{2,1,0:T(8,128)(2,1)} %slice.84) | copy-start | bytes 884740
  130.2 1.6 %copy-start.3 = (bf16[31,128,384]{2,1,0:T(8,128)(2,1)}, bf16[31,128,384]{2,1,0:T(8,128)(2,1)S(1)}, u32[]{:S(2)}) copy-start(bf16[31,128,384]{2,1,0:T(8,128)(2,1)S(1)} %constant_dynamic-update-slice_fusion.1) | copy-start | bytes 9142276
  131.9 2.8 %copy-start.4 = (bf16[31,128,384]{2,1,0:T(8,128)(2,1)S(1)}, bf16[31,128,384]{2,1,0:T(8,128)(2,1)}, u32[]{:S(2)}) copy-start(bf16[31,128,384]{2,1,0:T(8,128)(2,1)} %copy-done.3) | copy-start | bytes 9142276
  134.7 0.7 copy-start.10
  135.4 1.6 %copy-start.2 = (bf16[31,128,384]{2,1,0:T(8,128)(2,1)}, bf16[31,128,384]{2,1,0:T(8,128)(2,1)S(1)}, u32[]{:S(2)}) copy-start(bf16[31,128,384]{2,1,0:T(8,128)(2,1)S(1)} %constant_dynamic-update-slice_fusion.6.v_ref) | copy-start | bytes 9142276
Sparse Core Ops, SparseCore 0:
  9.2 102.9 all-gather.2

commit v2 on v1

v2 whole, which is shorter than its diff:
```python
import functools
import math

import jax
import jax.numpy as jnp
from jax import lax
from jax.experimental import pallas as pl
from jax.experimental.pallas import tpu as pltpu
from jax.sharding import PartitionSpec as P


HD = 128
BLK = 128
NEAR = 2

EPS = 1e-06


def attn_kernel(sel_ref, q_ref, kn_ref, vn_ref, kf_ref, vf_ref, o_ref, s_ref, *, q_blocks, slots):
    scale = 1.0 / math.sqrt(HD)
    for b in range(q_blocks):
        qh = q_ref[pl.ds(b * BLK, BLK), :]
        top = None
        for j in range(slots):
            use_near = sel_ref[0, b, j] == 1
            kh = jnp.where(use_near, kn_ref[sel_ref[1, b, j]], kf_ref[sel_ref[2, b, j]])
            s = lax.dot_general(
                qh, kh, (((1,), (1,)), ((), ())), preferred_element_type=jnp.float32
            ) * scale
            s_ref[j] = s
            top = s if top is None else jnp.maximum(top, s)
        top = jnp.max(top, axis=1, keepdims=True)
        total = None
        acc = None
        for j in range(slots):
            use_near = sel_ref[0, b, j] == 1
            vh = jnp.where(use_near, vn_ref[sel_ref[1, b, j]], vf_ref[0, sel_ref[2, b, j]])
            w = jnp.exp(s_ref[j] - top)
            total = w if total is None else total + w
            prod = jnp.dot(w.astype(jnp.bfloat16), vh, preferred_element_type=jnp.float32)
            acc = prod if acc is None else acc + prod
        total = jnp.sum(total, axis=1, keepdims=True)
        o_ref[pl.ds(b * BLK, BLK), :] = (acc / total).astype(o_ref.dtype)


def sparse_attend(sel, qn, kn_near, v_near, kn_first, first):
    tok_rows, width = qn.shape
    heads = width // HD
    q_blocks = tok_rows // BLK
    slots = sel.shape[2]
    n_near = kn_near.shape[0]
    n_first = kn_first.shape[0]
    kernel = functools.partial(attn_kernel, q_blocks=q_blocks, slots=slots)
    grid_spec = pltpu.PrefetchScalarGridSpec(
        num_scalar_prefetch=1,
        grid=(heads,),
        in_specs=[
            pl.BlockSpec((tok_rows, HD), lambda h, sel_ref: (0, h)),
            pl.BlockSpec((n_near, BLK, HD), lambda h, sel_ref: (0, 0, h)),
            pl.BlockSpec((n_near, BLK, HD), lambda h, sel_ref: (0, 0, h)),
            pl.BlockSpec((n_first, BLK, HD), lambda h, sel_ref: (0, 0, h)),
            pl.BlockSpec((1, n_first, BLK, HD), lambda h, sel_ref: (1, 0, 0, h)),
        ],
        out_specs=pl.BlockSpec((tok_rows, HD), lambda h, sel_ref: (0, h)),
        scratch_shapes=[pltpu.VMEM((slots, BLK, BLK), jnp.float32)],
    )
    flops = 4 * q_blocks * slots * heads * BLK * BLK * HD
    return pl.pallas_call(
        kernel,
        grid_spec=grid_spec,
        out_shape=jax.ShapeDtypeStruct((tok_rows, width), jnp.bfloat16),
        compiler_params=pltpu.CompilerParams(vmem_limit_bytes=48 * 1024 * 1024),
        cost_estimate=pl.CostEstimate(
            flops=flops,
            transcendentals=q_blocks * slots * heads * BLK * BLK,
            bytes_accessed=2 * (2 * tok_rows * width + 2 * (n_near + n_first) * BLK * width),
        ),
    )(sel, qn, kn_near, v_near, kn_first, first)


def xor_gather(piece, n_frame, frame_pos):
    held = piece[None]
    bit = 1
    while bit < n_frame:
        perm = [(i, i ^ bit) for i in range(n_frame)]
        got = lax.ppermute(held, "frame", perm)
        upper = (frame_pos // bit) % 2 == 1
        held = jnp.where(
            upper, jnp.concatenate([got, held], axis=0), jnp.concatenate([held, got], axis=0)
        )
        bit *= 2
    return held


def body(q_proj, k_proj, v_proj, gain_q, gain_k, tiles, *, n_frame):
    tok_rows, width = q_proj.shape
    blocks = tok_rows // BLK
    frame_pos = lax.axis_index("frame")
    full_width = width * lax.axis_size("tensor")
    offsets = list(range(-NEAR, NEAR + 1))
    perms = {
        d: [(i, i - d) for i in range(n_frame) if 0 <= i - d < n_frame] for d in offsets if d != 0
    }

    kv_raw = jnp.stack([k_proj, v_proj])
    first = lax.all_gather(kv_raw[:, :BLK], "frame", axis=1, tiled=False)
    tail = kv_raw[:, BLK:]
    near = {0: tail}
    for d in perms:
        near[d] = lax.ppermute(tail, "frame", perms[d])

    q_wide = q_proj.astype(jnp.float32)
    k_wide = k_proj.astype(jnp.float32)
    row_sums = lax.psum(
        (jnp.sum(q_wide * q_wide, axis=1), jnp.sum(k_wide * k_wide, axis=1)), "tensor"
    )
    q_norm = (q_wide * lax.rsqrt(row_sums[0] / full_width + EPS)[:, None] * gain_q).astype(
        jnp.bfloat16
    )
    k_sum = row_sums[1]
    all_sum = xor_gather(k_sum, n_frame, frame_pos)
    near_slab = jnp.clip(frame_pos + jnp.array(offsets), 0, n_frame - 1)
    near_sum = all_sum[near_slab][:, BLK:].reshape(len(offsets) * (blocks - 1), BLK)
    near_scale = lax.rsqrt(near_sum / full_width + EPS)[:, :, None]
    first_scale = lax.rsqrt(all_sum[:, :BLK] / full_width + EPS)[:, :, None]
    k_near = jnp.concatenate(
        [near[d][0].reshape(blocks - 1, BLK, width) for d in offsets], axis=0
    )
    kn_near = (k_near.astype(jnp.float32) * near_scale * gain_k).astype(jnp.bfloat16)
    v_near = jnp.concatenate(
        [near[d][1].reshape(blocks - 1, BLK, width) for d in offsets], axis=0
    )
    kn_first = (first[0].astype(jnp.float32) * first_scale * gain_k).astype(jnp.bfloat16)

    q_tiles = lax.dynamic_slice_in_dim(tiles, frame_pos * blocks, blocks, 0)
    key_slab = q_tiles // blocks
    within = q_tiles % blocks
    dist = key_slab - frame_pos
    near_ok = (jnp.abs(dist) <= NEAR) & (within > 0)
    near_idx = jnp.clip((dist + NEAR) * (blocks - 1) + within - 1, 0, len(offsets) * (blocks - 1) - 1)
    first_idx = jnp.clip(key_slab, 0, n_frame - 1)
    sel = jnp.stack([near_ok.astype(jnp.int32), near_idx, first_idx]).astype(jnp.int32)
    return sparse_attend(sel, q_norm, kn_near, v_near, kn_first, first)


def solution(mesh):
    return jax.shard_map(
        functools.partial(body, n_frame=mesh.shape["frame"]),
        mesh=mesh,
        in_specs=(
            P(("dp", "frame"), "tensor"),
            P(("dp", "frame"), "tensor"),
            P(("dp", "frame"), "tensor"),
            P("tensor"),
            P("tensor"),
            P("dp", None),
        ),
        out_specs=P(("dp", "frame"), "tensor"),
        check_vma=False,
    )
```

time: 156 us -> 150 us (0.962)
  the two profiles are of different devices: /device:TPU:64 before, /device:TPU:26 now
where the time goes in v2:
time: 150 us; the launch traced here: 149 us
  blocking collectives  81.8 us (55%)
  waiting for transfers between devices  16.3 us (11%)
  starting transfers between devices  14.4 us (10%)
  between operations  13.9 us (9%)
  Pallas kernels  11.2 us (7%)
  local copies, waits for them, and re-layouts  6.47 us (4%)
  other arithmetic  5.13 us (3%)
    psum x1, blocking collectives, body(): lax.psum((jnp.sum(q_wide * q_wide, axis=1), jnp.sum(k_wide * k_wide, axis...  81.8 us
    ppermute x4, waiting for transfers between devices, xor_gather(): got = lax.ppermute(held, 'frame', perm)  16.3 us
    ppermute x4, starting transfers between devices, body(): near[d] = lax.ppermute(tail, 'frame', perms[d])  14.1 us
    pallas_call x1, Pallas kernels, sparse_attend(): pl.pallas_call(kernel, grid_spec=grid_spec, out_shape=jax.ShapeDtypeStruc...  11.2 us
    another operation x2, other arithmetic, body(): kv_raw = jnp.stack([k_proj, v_proj])  3.69 us
    slice x5, local copies, waits for them, and re-layouts, body(): near[d][1].reshape(blocks - 1, BLK, width)  3.43 us
  transfers between devices with their start and end apart: 9, of which 4 were waited for; matrix products, arithmetic and copies ran while one was open for 5% of the time, Pallas kernels for 0%

profile of v2, /device:TPU:26, one launch (start us, length us, event | category | flops | bytes accessed | tf_op | source)
XLA Modules:
  0.0 149.2 jit_solution(13595815592133476033)
XLA Ops:
  6.6 1.7 %pad_maximum_fusion = bf16[2,128,384]{2,1,0:T(8,128)(2,1)} fusion(bf16[1,512,384]{2,1,0:T(8,128)(2,1)} %bitcast.27, bf16[1,512,384]{2,1,0:T(8,128)(2,1)} %bitcast.24), kind=kLoop, calls=%fused_computation.14 | loop fusion | flops 393216 | bytes 983040 | tf_op jit(solution)/shard_map/stack | solution.py:105
  8.3 0.0 all-gather.3.cloned.1.call-update
  8.3 2.0 %fusion.5 = bf16[2,384,384]{2,1,0:T(8,128)(2,1)} fusion(bf16[1,512,384]{2,1,0:T(8,128)(2,1)} %bitcast.25, bf16[1,512,384]{2,1,0:T(8,128)(2,1)} %bitcast.28), kind=kLoop, calls=%fused_computation.13 | loop fusion | flops 294912 | bytes 1376256 | tf_op jit(solution)/shard_map/stack | solution.py:105
  10.3 3.1 %collective-permute-start.3 = (bf16[2,384,384]{2,1,0:T(8,128)(2,1)}, bf16[2,384,384]{2,1,0:T(8,128)(2,1)}, u32[]{:S(2)}, u32[]{:S(2)}) collective-permute-start(bf16[2,384,384]{2,1,0:T(8,128)(2,1)} %fusion.5), channel_id=1, source_target_pairs={{32,0},{48,16},{64,32},{80,48},{96,64},{112,80},{128,96},{144,112}... | collective-permute-start | bytes 1769480 | tf_op jit(solution)/shard_map/ppermute | solution.py:110
  13.4 1.9 %collective-permute-start.2 = (bf16[2,384,384]{2,1,0:T(8,128)(2,1)}, bf16[2,384,384]{2,1,0:T(8,128)(2,1)}, u32[]{:S(2)}, u32[]{:S(2)}) collective-permute-start(bf16[2,384,384]{2,1,0:T(8,128)(2,1)} %fusion.5), channel_id=1, source_target_pairs={{16,0},{32,16},{48,32},{64,48},{80,64},{96,80},{112,96},{128,112},... | collective-permute-start | bytes 1769480 | tf_op jit(solution)/shard_map/ppermute | solution.py:110
  15.4 6.0 %collective-permute-start.1 = (bf16[2,384,384]{2,1,0:T(8,128)(2,1)}, bf16[2,384,384]{2,1,0:T(8,128)(2,1)}, u32[]{:S(2)}, u32[]{:S(2)}) collective-permute-start(bf16[2,384,384]{2,1,0:T(8,128)(2,1)} %fusion.5), channel_id=1, source_target_pairs={{0,16},{16,32},{32,48},{48,64},{64,80},{80,96},{96,112},{112,128},... | collective-permute-start | bytes 1769480 | tf_op jit(solution)/shard_map/ppermute | solution.py:110
  21.4 3.0 %collective-permute-start = (bf16[2,384,384]{2,1,0:T(8,128)(2,1)}, bf16[2,384,384]{2,1,0:T(8,128)(2,1)S(1)}, u32[]{:S(2)}, u32[]{:S(2)}) collective-permute-start(bf16[2,384,384]{2,1,0:T(8,128)(2,1)} %fusion.5), channel_id=1, source_target_pairs={{0,32},{16,48},{32,64},{48,80},{64,96},{80,112},{96,128},{112,144}... | collective-permute-start | bytes 1769480 | tf_op jit(solution)/shard_map/ppermute | solution.py:110
  24.4 0.2 multiply_reduce_fusion
  24.6 0.2 fusion.2
  24.7 81.8 %all-reduce = (f32[512]{0:T(512)S(1)}, f32[1,512]{1,0:T(1,128)S(1)}) all-reduce(f32[512]{0:T(512)S(1)} %fusion.2, f32[1,512]{1,0:T(1,128)S(1)} %bitcast.40), channel_id=1, replica_groups=mesh['frame'=16,'tensor'=8,'dp'=2] {'tensor'}, use_global_device_ids=true, to_apply=%region_1.0 | all-reduce | flops 1024 | bytes 8192 | tf_op jit(solution)/shard_map/psum | solution.py:114
  106.5 0.1 collective-permute-start.4
  106.6 0.1 constant_dynamic-slice_fusion
  106.7 0.1 copy.12
  106.8 0.2 fusion.4.q_ref
  107.0 3.1 %collective-permute-done.4 = f32[1,512]{1,0:T(1,128)S(1)} collective-permute-done((f32[1,512]{1,0:T(1,128)S(1)}, f32[1,512]{1,0:T(1,128)S(1)}, u32[]{:S(2)}, u32[]{:S(2)}) %collective-permute-start.4) | collective-permute-done | bytes 2080 | tf_op jit(solution)/shard_map/ppermute | solution.py:86
  110.2 0.1 collective-permute-start.5
  110.3 5.0 %collective-permute-done.5 = f32[2,512]{1,0:T(2,128)S(1)} collective-permute-done((f32[2,512]{1,0:T(2,128)S(1)}, f32[2,512]{1,0:T(2,128)S(1)}, u32[]{:S(2)}, u32[]{:S(2)}) %collective-permute-start.5) | collective-permute-done | bytes 4128 | tf_op jit(solution)/shard_map/ppermute | solution.py:86
  115.4 0.1 collective-permute-start.6
  115.5 3.6 %collective-permute-done.6 = f32[4,512]{1,0:T(4,128)S(1)} collective-permute-done((f32[4,512]{1,0:T(4,128)S(1)}, f32[4,512]{1,0:T(4,128)S(1)}, u32[]{:S(2)}, u32[]{:S(2)}) %collective-permute-start.6) | collective-permute-done | bytes 8224 | tf_op jit(solution)/shard_map/ppermute | solution.py:86
  119.1 0.1 collective-permute-start.7
  119.4 4.5 %collective-permute-done.7 = f32[8,512]{1,0:T(8,128)S(1)} collective-permute-done((f32[8,512]{1,0:T(8,128)S(1)}, f32[8,512]{1,0:T(8,128)S(1)}, u32[]{:S(2)}, u32[]{:S(2)}) %collective-permute-start.7) | collective-permute-done | bytes 16416 | tf_op jit(solution)/shard_map/ppermute | solution.py:86
  123.9 0.6 gather_fusion
  124.5 0.1 fusion.15
  124.6 1.1 fusion.14
  125.9 1.1 fusion.13
  127.1 1.1 fusion.12
  128.5 0.4 copy-done.4
  128.9 0.4 multiply_convert_fusion.kn_ref
  129.3 0.0 all-gather.3.cloned.1.call-done
  129.3 1.4 slice-done
  130.7 0.4 fusion.1.kf_ref
  131.2 11.2 %shard_map.73 = bf16[512,384]{1,0:T(8,128)(2,1)} custom-call(s32[3,4,12]{2,1,0:T(4,128)S(1)} %pad_add_fusion.sel_ref, bf16[512,384]{1,0:T(8,128)(2,1)S(1)} %fusion.4.q_ref, bf16[15,128,384]{2,1,0:T(8,128)(2,1)S(1)} %multiply_convert_fusion.kn_ref, bf16[15,128,384]{2,1,0:T(8,128)(2,1)S(1)} %constant_dynamic-update-slice_fusion.5.vn_ref, ...), custom_call_target="tpu_custom_call" | custom-call | flops 1207959552 | bytes 6881280 | tf_op jit(solution)/shard_map/pallas_call | solution.py:68
  (44 shorter events, 0.7 us)
Async XLA Ops:
  6.5 100.1 %copy-start = (s32[64,12]{0,1:T(8,128)S(1)}, s32[64,12]{0,1:T(8,128)}, u32[]{:S(2)}) copy-start(s32[64,12]{0,1:T(8,128)} %param.12) | copy-start | bytes 9220
  6.5 17.9 %copy-start.1 = (bf16[512,384]{1,0:T(8,128)(2,1)S(1)}, bf16[512,384]{1,0:T(8,128)(2,1)}, u32[]{:S(2)}) copy-start(bf16[512,384]{1,0:T(8,128)(2,1)} %param.8) | copy-start | bytes 1179652
  6.5 122.8 %all-gather.3.cloned.1.call-start = ((), (), s32[]{:S(2)}) async-start(), calls=%async_computation | async-start | bytes 3342336 | tf_op jit(solution)/shard_map/all_gather | solution.py:106
  6.5 18.0 %copy-start.3 = (bf16[512,384]{1,0:T(8,128)(2,1)S(1)}, bf16[512,384]{1,0:T(8,128)(2,1)}, u32[]{:S(2)}) copy-start(bf16[512,384]{1,0:T(8,128)(2,1)} %param.7) | copy-start | bytes 1179652
  6.5 100.3 %copy-start.5 = (f32[384]{0:T(512)S(1)}, f32[384]{0:T(512)}, u32[]{:S(2)}) copy-start(f32[384]{0:T(512)} %param.10) | copy-start | bytes 4612
  8.3 102.0 %copy-start.6 = (s32[5]{0:T(128)S(1)}, s32[5]{0:T(128)}, u32[]{:S(2)}) copy-start(s32[5]{0:T(128)} %constant.121.clone) | copy-start | bytes 64
  8.3 111.0 %copy-start.2 = (bf16[512,384]{1,0:T(8,128)(2,1)S(1)}, bf16[512,384]{1,0:T(8,128)(2,1)}, u32[]{:S(2)}) copy-start(bf16[512,384]{1,0:T(8,128)(2,1)} %param.9) | copy-start | bytes 1179652
  10.3 116.8 %collective-permute-start.3 = (bf16[2,384,384]{2,1,0:T(8,128)(2,1)}, bf16[2,384,384]{2,1,0:T(8,128)(2,1)}, u32[]{:S(2)}, u32[]{:S(2)}) collective-permute-start(bf16[2,384,384]{2,1,0:T(8,128)(2,1)} %fusion.5), channel_id=1, source_target_pairs={{32,0},{48,16},{64,32},{80,48},{96,64},{112,80},{128,96},{144,112}... | collective-permute-start | bytes 1769480 | tf_op jit(solution)/shard_map/ppermute | solution.py:110
  13.4 112.4 %collective-permute-start.2 = (bf16[2,384,384]{2,1,0:T(8,128)(2,1)}, bf16[2,384,384]{2,1,0:T(8,128)(2,1)}, u32[]{:S(2)}, u32[]{:S(2)}) collective-permute-start(bf16[2,384,384]{2,1,0:T(8,128)(2,1)} %fusion.5), channel_id=1, source_target_pairs={{16,0},{32,16},{48,32},{64,48},{80,64},{96,80},{112,96},{128,112},... | collective-permute-start | bytes 1769480 | tf_op jit(solution)/shard_map/ppermute | solution.py:110
  15.4 109.3 %collective-permute-start.1 = (bf16[2,384,384]{2,1,0:T(8,128)(2,1)}, bf16[2,384,384]{2,1,0:T(8,128)(2,1)}, u32[]{:S(2)}, u32[]{:S(2)}) collective-permute-start(bf16[2,384,384]{2,1,0:T(8,128)(2,1)} %fusion.5), channel_id=1, source_target_pairs={{0,16},{16,32},{32,48},{48,64},{64,80},{80,96},{96,112},{112,128},... | collective-permute-start | bytes 1769480 | tf_op jit(solution)/shard_map/ppermute | solution.py:110
  21.4 103.1 %collective-permute-start = (bf16[2,384,384]{2,1,0:T(8,128)(2,1)}, bf16[2,384,384]{2,1,0:T(8,128)(2,1)S(1)}, u32[]{:S(2)}, u32[]{:S(2)}) collective-permute-start(bf16[2,384,384]{2,1,0:T(8,128)(2,1)} %fusion.5), channel_id=1, source_target_pairs={{0,32},{16,48},{32,64},{48,80},{64,96},{80,112},{96,128},{112,144}... | collective-permute-start | bytes 1769480 | tf_op jit(solution)/shard_map/ppermute | solution.py:110
  106.5 3.7 %collective-permute-start.4 = (f32[1,512]{1,0:T(1,128)S(1)}, f32[1,512]{1,0:T(1,128)S(1)}, u32[]{:S(2)}, u32[]{:S(2)}) collective-permute-start(f32[1,512]{1,0:T(1,128)S(1)} %get-tuple-element.6), channel_id=1, source_target_pairs={{0,16},{16,0},{32,48},{48,32},{64,80},{80,64},{96,112},{112,96},{1... | collective-permute-start | bytes 6152 | tf_op jit(solution)/shard_map/ppermute | solution.py:86
  110.2 5.2 %collective-permute-start.5 = (f32[2,512]{1,0:T(2,128)S(1)}, f32[2,512]{1,0:T(2,128)S(1)}, u32[]{:S(2)}, u32[]{:S(2)}) collective-permute-start(f32[2,512]{1,0:T(2,128)S(1)} %maximum_select_fusion.3), channel_id=1, source_target_pairs={{0,32},{16,48},{32,0},{48,16},{64,96},{80,112},{96,64},{112,80},{1... | collective-permute-start | bytes 12296 | tf_op jit(solution)/shard_map/ppermute | solution.py:86
  115.4 3.7 %collective-permute-start.6 = (f32[4,512]{1,0:T(4,128)S(1)}, f32[4,512]{1,0:T(4,128)S(1)}, u32[]{:S(2)}, u32[]{:S(2)}) collective-permute-start(f32[4,512]{1,0:T(4,128)S(1)} %maximum_select_fusion.2), channel_id=1, source_target_pairs={{0,64},{16,80},{32,96},{48,112},{64,0},{80,16},{96,32},{112,48},{1... | collective-permute-start | bytes 24584 | tf_op jit(solution)/shard_map/ppermute | solution.py:86
  119.1 4.7 %collective-permute-start.7 = (f32[8,512]{1,0:T(8,128)S(1)}, f32[8,512]{1,0:T(8,128)S(1)}, u32[]{:S(2)}, u32[]{:S(2)}) collective-permute-start(f32[8,512]{1,0:T(8,128)S(1)} %maximum_select_fusion.1), channel_id=1, source_target_pairs={{0,128},{16,144},{32,160},{48,176},{64,192},{80,208},{96,224},{112... | collective-permute-start | bytes 49160 | tf_op jit(solution)/shard_map/ppermute | solution.py:86
  128.2 0.7 copy-start.4
  129.3 1.4 slice-start
Sparse Core Ops, SparseCore 0:
  9.1 104.9 all-gather.2

commit v3 on v2

--- a/solution.py
+++ b/solution.py
@@ -16,30 +16,24 @@
 EPS = 1e-06
 
 
-def attn_kernel(sel_ref, q_ref, kn_ref, vn_ref, kf_ref, vf_ref, o_ref, s_ref, *, q_blocks, slots):
+def attn_kernel(sel_ref, q_ref, kn_ref, vn_ref, kf_ref, vf_ref, o_ref, kc_ref, vc_ref, *, q_blocks, slots):
     scale = 1.0 / math.sqrt(HD)
     for b in range(q_blocks):
-        qh = q_ref[pl.ds(b * BLK, BLK), :]
-        top = None
         for j in range(slots):
             use_near = sel_ref[0, b, j] == 1
-            kh = jnp.where(use_near, kn_ref[sel_ref[1, b, j]], kf_ref[sel_ref[2, b, j]])
-            s = lax.dot_general(
-                qh, kh, (((1,), (1,)), ((), ())), preferred_element_type=jnp.float32
-            ) * scale
-            s_ref[j] = s
-            top = s if top is None else jnp.maximum(top, s)
-        top = jnp.max(top, axis=1, keepdims=True)
-        total = None
-        acc = None
-        for j in range(slots):
-            use_near = sel_ref[0, b, j] == 1
-            vh = jnp.where(use_near, vn_ref[sel_ref[1, b, j]], vf_ref[0, sel_ref[2, b, j]])
-            w = jnp.exp(s_ref[j] - top)
-            total = w if total is None else total + w
-            prod = jnp.dot(w.astype(jnp.bfloat16), vh, preferred_element_type=jnp.float32)
-            acc = prod if acc is None else acc + prod
-        total = jnp.sum(total, axis=1, keepdims=True)
+            rows = pl.ds(j * BLK, BLK)
+            kc_ref[rows, :] = jnp.where(use_near, kn_ref[sel_ref[1, b, j]], kf_ref[sel_ref[2, b, j]])
+            vc_ref[rows, :] = jnp.where(
+                use_near, vn_ref[sel_ref[1, b, j]], vf_ref[0, sel_ref[2, b, j]]
+            )
+        qh = q_ref[pl.ds(b * BLK, BLK), :]
+        s = lax.dot_general(
+            qh, kc_ref[...], (((1,), (1,)), ((), ())), preferred_element_type=jnp.float32
+        ) * scale
+        top = jnp.max(s, axis=1, keepdims=True)
+        w = jnp.exp(s - top)
+        total = jnp.sum(w, axis=1, keepdims=True)
+        acc = jnp.dot(w.astype(jnp.bfloat16), vc_ref[...], preferred_element_type=jnp.float32)
         o_ref[pl.ds(b * BLK, BLK), :] = (acc / total).astype(o_ref.dtype)
 
 
@@ -62,7 +56,10 @@
             pl.BlockSpec((1, n_first, BLK, HD), lambda h, sel_ref: (1, 0, 0, h)),
         ],
         out_specs=pl.BlockSpec((tok_rows, HD), lambda h, sel_ref: (0, h)),
-        scratch_shapes=[pltpu.VMEM((slots, BLK, BLK), jnp.float32)],
+        scratch_shapes=[
+            pltpu.VMEM((slots * BLK, HD), jnp.bfloat16),
+            pltpu.VMEM((slots * BLK, HD), jnp.bfloat16),
+        ],
     )
     flops = 4 * q_blocks * slots * heads * BLK * BLK * HD
     return pl.pallas_call(

time: 150 us -> 149 us (level)
  no operation moved by 1% of the time
where the time goes in v3:
time: 149 us
  blocking collectives  81.8 us (55%)
  waiting for transfers between devices  16.3 us (11%)
  starting transfers between devices  14.4 us (10%)
  between operations  13.9 us (9%)
  Pallas kernels  10.8 us (7%)
  local copies, waits for them, and re-layouts  6.47 us (4%)
  other arithmetic  5.13 us (3%)
    psum x1, blocking collectives, body(): lax.psum((jnp.sum(q_wide * q_wide, axis=1), jnp.sum(k_wide * k_wide, axis...  81.8 us
    ppermute x4, waiting for transfers between devices, xor_gather(): got = lax.ppermute(held, 'frame', perm)  16.3 us
    ppermute x4, starting transfers between devices, body(): near[d] = lax.ppermute(tail, 'frame', perms[d])  14.1 us
    pallas_call x1, Pallas kernels, sparse_attend(): pl.pallas_call(kernel, grid_spec=grid_spec, out_shape=jax.ShapeDtypeStruc...  10.8 us
    another operation x2, other arithmetic, body(): kv_raw = jnp.stack([k_proj, v_proj])  3.69 us
    slice x5, local copies, waits for them, and re-layouts, body(): near[d][1].reshape(blocks - 1, BLK, width)  3.43 us
  transfers between devices with their start and end apart: 9, of which 4 were waited for; matrix products, arithmetic and copies ran while one was open for 5% of the time, Pallas kernels for 0%

profile of v3, /device:TPU:26, one launch (start us, length us, event | category | flops | bytes accessed | tf_op | source)
XLA Modules:
  0.0 148.9 jit_solution(15614889385977785082)
XLA Ops:
  6.6 1.7 %pad_maximum_fusion = bf16[2,128,384]{2,1,0:T(8,128)(2,1)} fusion(bf16[1,512,384]{2,1,0:T(8,128)(2,1)} %bitcast.27, bf16[1,512,384]{2,1,0:T(8,128)(2,1)} %bitcast.24), kind=kLoop, calls=%fused_computation.14 | loop fusion | flops 393216 | bytes 983040 | tf_op jit(solution)/shard_map/stack | solution.py:102
  8.3 0.0 all-gather.3.cloned.1.call-update
  8.3 2.0 %fusion.5 = bf16[2,384,384]{2,1,0:T(8,128)(2,1)} fusion(bf16[1,512,384]{2,1,0:T(8,128)(2,1)} %bitcast.25, bf16[1,512,384]{2,1,0:T(8,128)(2,1)} %bitcast.28), kind=kLoop, calls=%fused_computation.13 | loop fusion | flops 294912 | bytes 1376256 | tf_op jit(solution)/shard_map/stack | solution.py:102
  10.3 3.1 %collective-permute-start.3 = (bf16[2,384,384]{2,1,0:T(8,128)(2,1)}, bf16[2,384,384]{2,1,0:T(8,128)(2,1)}, u32[]{:S(2)}, u32[]{:S(2)}) collective-permute-start(bf16[2,384,384]{2,1,0:T(8,128)(2,1)} %fusion.5), channel_id=1, source_target_pairs={{32,0},{48,16},{64,32},{80,48},{96,64},{112,80},{128,96},{144,112}... | collective-permute-start | bytes 1769480 | tf_op jit(solution)/shard_map/ppermute | solution.py:107
  13.4 1.9 %collective-permute-start.2 = (bf16[2,384,384]{2,1,0:T(8,128)(2,1)}, bf16[2,384,384]{2,1,0:T(8,128)(2,1)}, u32[]{:S(2)}, u32[]{:S(2)}) collective-permute-start(bf16[2,384,384]{2,1,0:T(8,128)(2,1)} %fusion.5), channel_id=1, source_target_pairs={{16,0},{32,16},{48,32},{64,48},{80,64},{96,80},{112,96},{128,112},... | collective-permute-start | bytes 1769480 | tf_op jit(solution)/shard_map/ppermute | solution.py:107
  15.4 6.0 %collective-permute-start.1 = (bf16[2,384,384]{2,1,0:T(8,128)(2,1)}, bf16[2,384,384]{2,1,0:T(8,128)(2,1)}, u32[]{:S(2)}, u32[]{:S(2)}) collective-permute-start(bf16[2,384,384]{2,1,0:T(8,128)(2,1)} %fusion.5), channel_id=1, source_target_pairs={{0,16},{16,32},{32,48},{48,64},{64,80},{80,96},{96,112},{112,128},... | collective-permute-start | bytes 1769480 | tf_op jit(solution)/shard_map/ppermute | solution.py:107
  21.4 3.0 %collective-permute-start = (bf16[2,384,384]{2,1,0:T(8,128)(2,1)}, bf16[2,384,384]{2,1,0:T(8,128)(2,1)S(1)}, u32[]{:S(2)}, u32[]{:S(2)}) collective-permute-start(bf16[2,384,384]{2,1,0:T(8,128)(2,1)} %fusion.5), channel_id=1, source_target_pairs={{0,32},{16,48},{32,64},{48,80},{64,96},{80,112},{96,128},{112,144}... | collective-permute-start | bytes 1769480 | tf_op jit(solution)/shard_map/ppermute | solution.py:107
  24.4 0.2 multiply_reduce_fusion
  24.6 0.2 fusion.2
  24.7 81.8 %all-reduce = (f32[512]{0:T(512)S(1)}, f32[1,512]{1,0:T(1,128)S(1)}) all-reduce(f32[512]{0:T(512)S(1)} %fusion.2, f32[1,512]{1,0:T(1,128)S(1)} %bitcast.40), channel_id=1, replica_groups=mesh['frame'=16,'tensor'=8,'dp'=2] {'tensor'}, use_global_device_ids=true, to_apply=%region_1.0 | all-reduce | flops 1024 | bytes 8192 | tf_op jit(solution)/shard_map/psum | solution.py:111
  106.5 0.1 collective-permute-start.4
  106.6 0.1 constant_dynamic-slice_fusion
  106.7 0.1 copy.12
  106.8 0.2 fusion.4.q_ref
  107.0 3.1 %collective-permute-done.4 = f32[1,512]{1,0:T(1,128)S(1)} collective-permute-done((f32[1,512]{1,0:T(1,128)S(1)}, f32[1,512]{1,0:T(1,128)S(1)}, u32[]{:S(2)}, u32[]{:S(2)}) %collective-permute-start.4) | collective-permute-done | bytes 2080 | tf_op jit(solution)/shard_map/ppermute | solution.py:83
  110.2 0.1 collective-permute-start.5
  110.3 5.0 %collective-permute-done.5 = f32[2,512]{1,0:T(2,128)S(1)} collective-permute-done((f32[2,512]{1,0:T(2,128)S(1)}, f32[2,512]{1,0:T(2,128)S(1)}, u32[]{:S(2)}, u32[]{:S(2)}) %collective-permute-start.5) | collective-permute-done | bytes 4128 | tf_op jit(solution)/shard_map/ppermute | solution.py:83
  115.4 0.1 collective-permute-start.6
  115.5 3.6 %collective-permute-done.6 = f32[4,512]{1,0:T(4,128)S(1)} collective-permute-done((f32[4,512]{1,0:T(4,128)S(1)}, f32[4,512]{1,0:T(4,128)S(1)}, u32[]{:S(2)}, u32[]{:S(2)}) %collective-permute-start.6) | collective-permute-done | bytes 8224 | tf_op jit(solution)/shard_map/ppermute | solution.py:83
  119.1 0.1 collective-permute-start.7
  119.4 4.5 %collective-permute-done.7 = f32[8,512]{1,0:T(8,128)S(1)} collective-permute-done((f32[8,512]{1,0:T(8,128)S(1)}, f32[8,512]{1,0:T(8,128)S(1)}, u32[]{:S(2)}, u32[]{:S(2)}) %collective-permute-start.7) | collective-permute-done | bytes 16416 | tf_op jit(solution)/shard_map/ppermute | solution.py:83
  123.9 0.6 gather_fusion
  124.5 0.1 fusion.15
  124.6 1.1 fusion.14
  125.9 1.1 fusion.13
  127.1 1.1 fusion.12
  128.5 0.4 copy-done.4
  128.9 0.4 multiply_convert_fusion.kn_ref
  129.3 0.0 all-gather.3.cloned.1.call-done
  129.3 1.4 slice-done
  130.7 0.4 fusion.1.kf_ref
  131.2 10.8 %shard_map.73 = bf16[512,384]{1,0:T(8,128)(2,1)} custom-call(s32[3,4,12]{2,1,0:T(4,128)S(1)} %pad_add_fusion.sel_ref, bf16[512,384]{1,0:T(8,128)(2,1)S(1)} %fusion.4.q_ref, bf16[15,128,384]{2,1,0:T(8,128)(2,1)S(1)} %multiply_convert_fusion.kn_ref, bf16[15,128,384]{2,1,0:T(8,128)(2,1)S(1)} %constant_dynamic-update-slice_fusion.5.vn_ref, ...), custom_call_target="tpu_custom_call" | custom-call | flops 1207959552 | bytes 6881280 | tf_op jit(solution)/shard_map/pallas_call | solution.py:65
  (44 shorter events, 0.7 us)
Async XLA Ops:
  6.5 100.1 %copy-start = (s32[64,12]{0,1:T(8,128)S(1)}, s32[64,12]{0,1:T(8,128)}, u32[]{:S(2)}) copy-start(s32[64,12]{0,1:T(8,128)} %param.12) | copy-start | bytes 9220
  6.5 17.9 %copy-start.1 = (bf16[512,384]{1,0:T(8,128)(2,1)S(1)}, bf16[512,384]{1,0:T(8,128)(2,1)}, u32[]{:S(2)}) copy-start(bf16[512,384]{1,0:T(8,128)(2,1)} %param.8) | copy-start | bytes 1179652
  6.5 122.8 %all-gather.3.cloned.1.call-start = ((), (), s32[]{:S(2)}) async-start(), calls=%async_computation | async-start | bytes 3342336 | tf_op jit(solution)/shard_map/all_gather | solution.py:103
  6.5 18.0 %copy-start.3 = (bf16[512,384]{1,0:T(8,128)(2,1)S(1)}, bf16[512,384]{1,0:T(8,128)(2,1)}, u32[]{:S(2)}) copy-start(bf16[512,384]{1,0:T(8,128)(2,1)} %param.7) | copy-start | bytes 1179652
  6.5 100.3 %copy-start.5 = (f32[384]{0:T(512)S(1)}, f32[384]{0:T(512)}, u32[]{:S(2)}) copy-start(f32[384]{0:T(512)} %param.10) | copy-start | bytes 4612
  8.3 102.0 %copy-start.6 = (s32[5]{0:T(128)S(1)}, s32[5]{0:T(128)}, u32[]{:S(2)}) copy-start(s32[5]{0:T(128)} %constant.121.clone) | copy-start | bytes 64
  8.3 111.0 %copy-start.2 = (bf16[512,384]{1,0:T(8,128)(2,1)S(1)}, bf16[512,384]{1,0:T(8,128)(2,1)}, u32[]{:S(2)}) copy-start(bf16[512,384]{1,0:T(8,128)(2,1)} %param.9) | copy-start | bytes 1179652
  10.3 116.8 %collective-permute-start.3 = (bf16[2,384,384]{2,1,0:T(8,128)(2,1)}, bf16[2,384,384]{2,1,0:T(8,128)(2,1)}, u32[]{:S(2)}, u32[]{:S(2)}) collective-permute-start(bf16[2,384,384]{2,1,0:T(8,128)(2,1)} %fusion.5), channel_id=1, source_target_pairs={{32,0},{48,16},{64,32},{80,48},{96,64},{112,80},{128,96},{144,112}... | collective-permute-start | bytes 1769480 | tf_op jit(solution)/shard_map/ppermute | solution.py:107
  13.4 112.4 %collective-permute-start.2 = (bf16[2,384,384]{2,1,0:T(8,128)(2,1)}, bf16[2,384,384]{2,1,0:T(8,128)(2,1)}, u32[]{:S(2)}, u32[]{:S(2)}) collective-permute-start(bf16[2,384,384]{2,1,0:T(8,128)(2,1)} %fusion.5), channel_id=1, source_target_pairs={{16,0},{32,16},{48,32},{64,48},{80,64},{96,80},{112,96},{128,112},... | collective-permute-start | bytes 1769480 | tf_op jit(solution)/shard_map/ppermute | solution.py:107
  15.4 109.3 %collective-permute-start.1 = (bf16[2,384,384]{2,1,0:T(8,128)(2,1)}, bf16[2,384,384]{2,1,0:T(8,128)(2,1)}, u32[]{:S(2)}, u32[]{:S(2)}) collective-permute-start(bf16[2,384,384]{2,1,0:T(8,128)(2,1)} %fusion.5), channel_id=1, source_target_pairs={{0,16},{16,32},{32,48},{48,64},{64,80},{80,96},{96,112},{112,128},... | collective-permute-start | bytes 1769480 | tf_op jit(solution)/shard_map/ppermute | solution.py:107
  21.4 103.1 %collective-permute-start = (bf16[2,384,384]{2,1,0:T(8,128)(2,1)}, bf16[2,384,384]{2,1,0:T(8,128)(2,1)S(1)}, u32[]{:S(2)}, u32[]{:S(2)}) collective-permute-start(bf16[2,384,384]{2,1,0:T(8,128)(2,1)} %fusion.5), channel_id=1, source_target_pairs={{0,32},{16,48},{32,64},{48,80},{64,96},{80,112},{96,128},{112,144}... | collective-permute-start | bytes 1769480 | tf_op jit(solution)/shard_map/ppermute | solution.py:107
  106.5 3.7 %collective-permute-start.4 = (f32[1,512]{1,0:T(1,128)S(1)}, f32[1,512]{1,0:T(1,128)S(1)}, u32[]{:S(2)}, u32[]{:S(2)}) collective-permute-start(f32[1,512]{1,0:T(1,128)S(1)} %get-tuple-element.6), channel_id=1, source_target_pairs={{0,16},{16,0},{32,48},{48,32},{64,80},{80,64},{96,112},{112,96},{1... | collective-permute-start | bytes 6152 | tf_op jit(solution)/shard_map/ppermute | solution.py:83
  110.2 5.2 %collective-permute-start.5 = (f32[2,512]{1,0:T(2,128)S(1)}, f32[2,512]{1,0:T(2,128)S(1)}, u32[]{:S(2)}, u32[]{:S(2)}) collective-permute-start(f32[2,512]{1,0:T(2,128)S(1)} %maximum_select_fusion.3), channel_id=1, source_target_pairs={{0,32},{16,48},{32,0},{48,16},{64,96},{80,112},{96,64},{112,80},{1... | collective-permute-start | bytes 12296 | tf_op jit(solution)/shard_map/ppermute | solution.py:83
  115.4 3.7 %collective-permute-start.6 = (f32[4,512]{1,0:T(4,128)S(1)}, f32[4,512]{1,0:T(4,128)S(1)}, u32[]{:S(2)}, u32[]{:S(2)}) collective-permute-start(f32[4,512]{1,0:T(4,128)S(1)} %maximum_select_fusion.2), channel_id=1, source_target_pairs={{0,64},{16,80},{32,96},{48,112},{64,0},{80,16},{96,32},{112,48},{1... | collective-permute-start | bytes 24584 | tf_op jit(solution)/shard_map/ppermute | solution.py:83
  119.1 4.7 %collective-permute-start.7 = (f32[8,512]{1,0:T(8,128)S(1)}, f32[8,512]{1,0:T(8,128)S(1)}, u32[]{:S(2)}, u32[]{:S(2)}) collective-permute-start(f32[8,512]{1,0:T(8,128)S(1)} %maximum_select_fusion.1), channel_id=1, source_target_pairs={{0,128},{16,144},{32,160},{48,176},{64,192},{80,208},{96,224},{112... | collective-permute-start | bytes 49160 | tf_op jit(solution)/shard_map/ppermute | solution.py:83
  128.2 0.7 copy-start.4
  129.3 1.4 slice-start
Sparse Core Ops, SparseCore 0:
  9.1 104.9 all-gather.2

commit v4 on v3

--- a/solution.py
+++ b/solution.py
@@ -28,12 +28,16 @@
             )
         qh = q_ref[pl.ds(b * BLK, BLK), :]
         s = lax.dot_general(
-            qh, kc_ref[...], (((1,), (1,)), ((), ())), preferred_element_type=jnp.float32
+            kc_ref[...], qh, (((1,), (1,)), ((), ())), preferred_element_type=jnp.float32
         ) * scale
-        top = jnp.max(s, axis=1, keepdims=True)
+        top = jnp.max(s, axis=0, keepdims=True)
         w = jnp.exp(s - top)
-        total = jnp.sum(w, axis=1, keepdims=True)
-        acc = jnp.dot(w.astype(jnp.bfloat16), vc_ref[...], preferred_element_type=jnp.float32)
+        total = jnp.sum(w, axis=0, keepdims=True)
+        acc = lax.dot_general(
+            w.astype(jnp.bfloat16), vc_ref[...], (((0,), (0,)), ((), ())),
+            preferred_element_type=jnp.float32,
+        )
+        total = jnp.transpose(jnp.broadcast_to(total, (BLK, BLK)))
         o_ref[pl.ds(b * BLK, BLK), :] = (acc / total).astype(o_ref.dtype)
 
 

time: 149 us -> 149 us (level)
  no operation moved by 1% of the time
where the time goes in v4:
time: 149 us
  blocking collectives  81.8 us (55%)
  waiting for transfers between devices  16.3 us (11%)
  starting transfers between devices  14.4 us (10%)
  between operations  13.9 us (9%)
  Pallas kernels  11 us (7%)
  local copies, waits for them, and re-layouts  6.47 us (4%)
  other arithmetic  5.13 us (3%)
    psum x1, blocking collectives, body(): lax.psum((jnp.sum(q_wide * q_wide, axis=1), jnp.sum(k_wide * k_wide, axis...  81.8 us
    ppermute x4, waiting for transfers between devices, xor_gather(): got = lax.ppermute(held, 'frame', perm)  16.3 us
    ppermute x4, starting transfers between devices, body(): near[d] = lax.ppermute(tail, 'frame', perms[d])  14.1 us
    pallas_call x1, Pallas kernels, sparse_attend(): pl.pallas_call(kernel, grid_spec=grid_spec, out_shape=jax.ShapeDtypeStruc...  11 us
    another operation x2, other arithmetic, body(): kv_raw = jnp.stack([k_proj, v_proj])  3.69 us
    slice x5, local copies, waits for them, and re-layouts, body(): near[d][1].reshape(blocks - 1, BLK, width)  3.43 us
  transfers between devices with their start and end apart: 9, of which 4 were waited for; matrix products, arithmetic and copies ran while one was open for 5% of the time, Pallas kernels for 0%

profile of v4, /device:TPU:26, one launch (start us, length us, event | category | flops | bytes accessed | tf_op | source)
XLA Modules:
  0.0 149.0 jit_solution(10634487961105601728)
XLA Ops:
  6.6 1.7 %pad_maximum_fusion = bf16[2,128,384]{2,1,0:T(8,128)(2,1)} fusion(bf16[1,512,384]{2,1,0:T(8,128)(2,1)} %bitcast.27, bf16[1,512,384]{2,1,0:T(8,128)(2,1)} %bitcast.24), kind=kLoop, calls=%fused_computation.14 | loop fusion | flops 393216 | bytes 983040 | tf_op jit(solution)/shard_map/stack | solution.py:106
  8.3 0.0 all-gather.3.cloned.1.call-update
  8.3 2.0 %fusion.5 = bf16[2,384,384]{2,1,0:T(8,128)(2,1)} fusion(bf16[1,512,384]{2,1,0:T(8,128)(2,1)} %bitcast.25, bf16[1,512,384]{2,1,0:T(8,128)(2,1)} %bitcast.28), kind=kLoop, calls=%fused_computation.13 | loop fusion | flops 294912 | bytes 1376256 | tf_op jit(solution)/shard_map/stack | solution.py:106
  10.3 3.1 %collective-permute-start.3 = (bf16[2,384,384]{2,1,0:T(8,128)(2,1)}, bf16[2,384,384]{2,1,0:T(8,128)(2,1)}, u32[]{:S(2)}, u32[]{:S(2)}) collective-permute-start(bf16[2,384,384]{2,1,0:T(8,128)(2,1)} %fusion.5), channel_id=1, source_target_pairs={{32,0},{48,16},{64,32},{80,48},{96,64},{112,80},{128,96},{144,112}... | collective-permute-start | bytes 1769480 | tf_op jit(solution)/shard_map/ppermute | solution.py:111
  13.4 1.9 %collective-permute-start.2 = (bf16[2,384,384]{2,1,0:T(8,128)(2,1)}, bf16[2,384,384]{2,1,0:T(8,128)(2,1)}, u32[]{:S(2)}, u32[]{:S(2)}) collective-permute-start(bf16[2,384,384]{2,1,0:T(8,128)(2,1)} %fusion.5), channel_id=1, source_target_pairs={{16,0},{32,16},{48,32},{64,48},{80,64},{96,80},{112,96},{128,112},... | collective-permute-start | bytes 1769480 | tf_op jit(solution)/shard_map/ppermute | solution.py:111
  15.4 6.0 %collective-permute-start.1 = (bf16[2,384,384]{2,1,0:T(8,128)(2,1)}, bf16[2,384,384]{2,1,0:T(8,128)(2,1)}, u32[]{:S(2)}, u32[]{:S(2)}) collective-permute-start(bf16[2,384,384]{2,1,0:T(8,128)(2,1)} %fusion.5), channel_id=1, source_target_pairs={{0,16},{16,32},{32,48},{48,64},{64,80},{80,96},{96,112},{112,128},... | collective-permute-start | bytes 1769480 | tf_op jit(solution)/shard_map/ppermute | solution.py:111
  21.4 3.0 %collective-permute-start = (bf16[2,384,384]{2,1,0:T(8,128)(2,1)}, bf16[2,384,384]{2,1,0:T(8,128)(2,1)S(1)}, u32[]{:S(2)}, u32[]{:S(2)}) collective-permute-start(bf16[2,384,384]{2,1,0:T(8,128)(2,1)} %fusion.5), channel_id=1, source_target_pairs={{0,32},{16,48},{32,64},{48,80},{64,96},{80,112},{96,128},{112,144}... | collective-permute-start | bytes 1769480 | tf_op jit(solution)/shard_map/ppermute | solution.py:111
  24.4 0.2 multiply_reduce_fusion
  24.6 0.2 fusion.2
  24.7 81.8 %all-reduce = (f32[512]{0:T(512)S(1)}, f32[1,512]{1,0:T(1,128)S(1)}) all-reduce(f32[512]{0:T(512)S(1)} %fusion.2, f32[1,512]{1,0:T(1,128)S(1)} %bitcast.40), channel_id=1, replica_groups=mesh['frame'=16,'tensor'=8,'dp'=2] {'tensor'}, use_global_device_ids=true, to_apply=%region_1.0 | all-reduce | flops 1024 | bytes 8192 | tf_op jit(solution)/shard_map/psum | solution.py:115
  106.5 0.1 collective-permute-start.4
  106.6 0.1 constant_dynamic-slice_fusion
  106.7 0.1 copy.12
  106.8 0.2 fusion.4.q_ref
  107.0 3.1 %collective-permute-done.4 = f32[1,512]{1,0:T(1,128)S(1)} collective-permute-done((f32[1,512]{1,0:T(1,128)S(1)}, f32[1,512]{1,0:T(1,128)S(1)}, u32[]{:S(2)}, u32[]{:S(2)}) %collective-permute-start.4) | collective-permute-done | bytes 2080 | tf_op jit(solution)/shard_map/ppermute | solution.py:87
  110.2 0.1 collective-permute-start.5
  110.3 5.0 %collective-permute-done.5 = f32[2,512]{1,0:T(2,128)S(1)} collective-permute-done((f32[2,512]{1,0:T(2,128)S(1)}, f32[2,512]{1,0:T(2,128)S(1)}, u32[]{:S(2)}, u32[]{:S(2)}) %collective-permute-start.5) | collective-permute-done | bytes 4128 | tf_op jit(solution)/shard_map/ppermute | solution.py:87
  115.4 0.1 collective-permute-start.6
  115.5 3.6 %collective-permute-done.6 = f32[4,512]{1,0:T(4,128)S(1)} collective-permute-done((f32[4,512]{1,0:T(4,128)S(1)}, f32[4,512]{1,0:T(4,128)S(1)}, u32[]{:S(2)}, u32[]{:S(2)}) %collective-permute-start.6) | collective-permute-done | bytes 8224 | tf_op jit(solution)/shard_map/ppermute | solution.py:87
  119.1 0.1 collective-permute-start.7
  119.4 4.5 %collective-permute-done.7 = f32[8,512]{1,0:T(8,128)S(1)} collective-permute-done((f32[8,512]{1,0:T(8,128)S(1)}, f32[8,512]{1,0:T(8,128)S(1)}, u32[]{:S(2)}, u32[]{:S(2)}) %collective-permute-start.7) | collective-permute-done | bytes 16416 | tf_op jit(solution)/shard_map/ppermute | solution.py:87
  123.9 0.6 gather_fusion
  124.5 0.1 fusion.15
  124.6 1.1 fusion.14
  125.9 1.1 fusion.13
  127.1 1.1 fusion.12
  128.5 0.4 copy-done.4
  128.9 0.4 multiply_convert_fusion.kn_ref
  129.3 0.0 all-gather.3.cloned.1.call-done
  129.3 1.4 slice-done
  130.7 0.4 fusion.1.kf_ref
  131.2 11.0 %shard_map.73 = bf16[512,384]{1,0:T(8,128)(2,1)} custom-call(s32[3,4,12]{2,1,0:T(4,128)S(1)} %pad_add_fusion.sel_ref, bf16[512,384]{1,0:T(8,128)(2,1)S(1)} %fusion.4.q_ref, bf16[15,128,384]{2,1,0:T(8,128)(2,1)S(1)} %multiply_convert_fusion.kn_ref, bf16[15,128,384]{2,1,0:T(8,128)(2,1)S(1)} %constant_dynamic-update-slice_fusion.5.vn_ref, ...), custom_call_target="tpu_custom_call" | custom-call | flops 1207959552 | bytes 6881280 | tf_op jit(solution)/shard_map/pallas_call | solution.py:69
  (44 shorter events, 0.7 us)
Async XLA Ops:
  6.5 100.1 %copy-start = (s32[64,12]{0,1:T(8,128)S(1)}, s32[64,12]{0,1:T(8,128)}, u32[]{:S(2)}) copy-start(s32[64,12]{0,1:T(8,128)} %param.12) | copy-start | bytes 9220
  6.5 17.9 %copy-start.1 = (bf16[512,384]{1,0:T(8,128)(2,1)S(1)}, bf16[512,384]{1,0:T(8,128)(2,1)}, u32[]{:S(2)}) copy-start(bf16[512,384]{1,0:T(8,128)(2,1)} %param.8) | copy-start | bytes 1179652
  6.5 122.8 %all-gather.3.cloned.1.call-start = ((), (), s32[]{:S(2)}) async-start(), calls=%async_computation | async-start | bytes 3342336 | tf_op jit(solution)/shard_map/all_gather | solution.py:107
  6.5 18.0 %copy-start.3 = (bf16[512,384]{1,0:T(8,128)(2,1)S(1)}, bf16[512,384]{1,0:T(8,128)(2,1)}, u32[]{:S(2)}) copy-start(bf16[512,384]{1,0:T(8,128)(2,1)} %param.7) | copy-start | bytes 1179652
  6.5 100.3 %copy-start.5 = (f32[384]{0:T(512)S(1)}, f32[384]{0:T(512)}, u32[]{:S(2)}) copy-start(f32[384]{0:T(512)} %param.10) | copy-start | bytes 4612
  8.3 102.0 %copy-start.6 = (s32[5]{0:T(128)S(1)}, s32[5]{0:T(128)}, u32[]{:S(2)}) copy-start(s32[5]{0:T(128)} %constant.121.clone) | copy-start | bytes 64
  8.3 111.0 %copy-start.2 = (bf16[512,384]{1,0:T(8,128)(2,1)S(1)}, bf16[512,384]{1,0:T(8,128)(2,1)}, u32[]{:S(2)}) copy-start(bf16[512,384]{1,0:T(8,128)(2,1)} %param.9) | copy-start | bytes 1179652
  10.3 116.8 %collective-permute-start.3 = (bf16[2,384,384]{2,1,0:T(8,128)(2,1)}, bf16[2,384,384]{2,1,0:T(8,128)(2,1)}, u32[]{:S(2)}, u32[]{:S(2)}) collective-permute-start(bf16[2,384,384]{2,1,0:T(8,128)(2,1)} %fusion.5), channel_id=1, source_target_pairs={{32,0},{48,16},{64,32},{80,48},{96,64},{112,80},{128,96},{144,112}... | collective-permute-start | bytes 1769480 | tf_op jit(solution)/shard_map/ppermute | solution.py:111
  13.4 112.4 %collective-permute-start.2 = (bf16[2,384,384]{2,1,0:T(8,128)(2,1)}, bf16[2,384,384]{2,1,0:T(8,128)(2,1)}, u32[]{:S(2)}, u32[]{:S(2)}) collective-permute-start(bf16[2,384,384]{2,1,0:T(8,128)(2,1)} %fusion.5), channel_id=1, source_target_pairs={{16,0},{32,16},{48,32},{64,48},{80,64},{96,80},{112,96},{128,112},... | collective-permute-start | bytes 1769480 | tf_op jit(solution)/shard_map/ppermute | solution.py:111
  15.4 109.3 %collective-permute-start.1 = (bf16[2,384,384]{2,1,0:T(8,128)(2,1)}, bf16[2,384,384]{2,1,0:T(8,128)(2,1)}, u32[]{:S(2)}, u32[]{:S(2)}) collective-permute-start(bf16[2,384,384]{2,1,0:T(8,128)(2,1)} %fusion.5), channel_id=1, source_target_pairs={{0,16},{16,32},{32,48},{48,64},{64,80},{80,96},{96,112},{112,128},... | collective-permute-start | bytes 1769480 | tf_op jit(solution)/shard_map/ppermute | solution.py:111
  21.4 103.1 %collective-permute-start = (bf16[2,384,384]{2,1,0:T(8,128)(2,1)}, bf16[2,384,384]{2,1,0:T(8,128)(2,1)S(1)}, u32[]{:S(2)}, u32[]{:S(2)}) collective-permute-start(bf16[2,384,384]{2,1,0:T(8,128)(2,1)} %fusion.5), channel_id=1, source_target_pairs={{0,32},{16,48},{32,64},{48,80},{64,96},{80,112},{96,128},{112,144}... | collective-permute-start | bytes 1769480 | tf_op jit(solution)/shard_map/ppermute | solution.py:111
  106.5 3.7 %collective-permute-start.4 = (f32[1,512]{1,0:T(1,128)S(1)}, f32[1,512]{1,0:T(1,128)S(1)}, u32[]{:S(2)}, u32[]{:S(2)}) collective-permute-start(f32[1,512]{1,0:T(1,128)S(1)} %get-tuple-element.6), channel_id=1, source_target_pairs={{0,16},{16,0},{32,48},{48,32},{64,80},{80,64},{96,112},{112,96},{1... | collective-permute-start | bytes 6152 | tf_op jit(solution)/shard_map/ppermute | solution.py:87
  110.2 5.2 %collective-permute-start.5 = (f32[2,512]{1,0:T(2,128)S(1)}, f32[2,512]{1,0:T(2,128)S(1)}, u32[]{:S(2)}, u32[]{:S(2)}) collective-permute-start(f32[2,512]{1,0:T(2,128)S(1)} %maximum_select_fusion.3), channel_id=1, source_target_pairs={{0,32},{16,48},{32,0},{48,16},{64,96},{80,112},{96,64},{112,80},{1... | collective-permute-start | bytes 12296 | tf_op jit(solution)/shard_map/ppermute | solution.py:87
  115.4 3.7 %collective-permute-start.6 = (f32[4,512]{1,0:T(4,128)S(1)}, f32[4,512]{1,0:T(4,128)S(1)}, u32[]{:S(2)}, u32[]{:S(2)}) collective-permute-start(f32[4,512]{1,0:T(4,128)S(1)} %maximum_select_fusion.2), channel_id=1, source_target_pairs={{0,64},{16,80},{32,96},{48,112},{64,0},{80,16},{96,32},{112,48},{1... | collective-permute-start | bytes 24584 | tf_op jit(solution)/shard_map/ppermute | solution.py:87
  119.1 4.7 %collective-permute-start.7 = (f32[8,512]{1,0:T(8,128)S(1)}, f32[8,512]{1,0:T(8,128)S(1)}, u32[]{:S(2)}, u32[]{:S(2)}) collective-permute-start(f32[8,512]{1,0:T(8,128)S(1)} %maximum_select_fusion.1), channel_id=1, source_target_pairs={{0,128},{16,144},{32,160},{48,176},{64,192},{80,208},{96,224},{112... | collective-permute-start | bytes 49160 | tf_op jit(solution)/shard_map/ppermute | solution.py:87
  128.2 0.7 copy-start.4
  129.3 1.4 slice-start
Sparse Core Ops, SparseCore 0:
  9.1 104.9 all-gather.2

commit v5 on v4

--- a/solution.py
+++ b/solution.py
@@ -93,7 +93,16 @@
     return held
 
 
-def body(q_proj, k_proj, v_proj, gain_q, gain_k, tiles, *, n_frame):
+def xor_sum(x, axis, n):
+    bit = 1
+    while bit < n:
+        perm = [(i, i ^ bit) for i in range(n)]
+        x = x + lax.ppermute(x, axis, perm)
+        bit *= 2
+    return x
+
+
+def body(q_proj, k_proj, v_proj, gain_q, gain_k, tiles, *, n_frame, n_tensor):
     tok_rows, width = q_proj.shape
     blocks = tok_rows // BLK
     frame_pos = lax.axis_index("frame")
@@ -112,8 +121,10 @@
 
     q_wide = q_proj.astype(jnp.float32)
     k_wide = k_proj.astype(jnp.float32)
-    row_sums = lax.psum(
-        (jnp.sum(q_wide * q_wide, axis=1), jnp.sum(k_wide * k_wide, axis=1)), "tensor"
+    row_sums = xor_sum(
+        jnp.stack([jnp.sum(q_wide * q_wide, axis=1), jnp.sum(k_wide * k_wide, axis=1)]),
+        "tensor",
+        n_tensor,
     )
     q_norm = (q_wide * lax.rsqrt(row_sums[0] / full_width + EPS)[:, None] * gain_q).astype(
         jnp.bfloat16
@@ -146,7 +157,7 @@
 
 def solution(mesh):
     return jax.shard_map(
-        functools.partial(body, n_frame=mesh.shape["frame"]),
+        functools.partial(body, n_frame=mesh.shape["frame"], n_tensor=mesh.shape["tensor"]),
         mesh=mesh,
         in_specs=(
             P(("dp", "frame"), "tensor"),

time: 149 us -> 140 us (0.940)
  the two profiles are of different devices: /device:TPU:26 before, /device:TPU:2 now
where the time goes in v5:
time: 140 us
  starting transfers between devices  59.5 us (42%)
  waiting for transfers between devices  43.8 us (31%)
  between operations  13.8 us (10%)
  Pallas kernels  11 us (8%)
  local copies, waits for them, and re-layouts  6.47 us (5%)
  other arithmetic  5.17 us (4%)
    ppermute x4, starting transfers between devices, xor_gather(): got = lax.ppermute(held, 'frame', perm)  34.5 us
    ppermute x4, waiting for transfers between devices, xor_gather(): got = lax.ppermute(held, 'frame', perm)  30.6 us
    ppermute x4, starting transfers between devices, body(): near[d] = lax.ppermute(tail, 'frame', perms[d])  13.5 us
    ppermute x3, starting transfers between devices, xor_sum(): x = x + lax.ppermute(x, axis, perm)  11.5 us
    pallas_call x1, Pallas kernels, sparse_attend(): pl.pallas_call(kernel, grid_spec=grid_spec, out_shape=jax.ShapeDtypeStruc...  11 us
    all_gather x1, waiting for transfers between devices, body(): first = lax.all_gather(kv_raw[:, :BLK], 'frame', axis=1, tiled=False)  7.15 us
    ppermute x3, waiting for transfers between devices, xor_sum(): x = x + lax.ppermute(x, axis, perm)  6.01 us
    another operation x2, other arithmetic, body(): kv_raw = jnp.stack([k_proj, v_proj])  3.7 us
  transfers between devices with their start and end apart: 12, of which 8 were waited for; matrix products, arithmetic and copies ran while one was open for 5% of the time, Pallas kernels for 0%

profile of v5, /device:TPU:2, one launch (start us, length us, event | category | flops | bytes accessed | tf_op | source)
XLA Modules:
  0.0 139.7 jit_solution(1300974261845982982)
XLA Ops:
  6.5 1.7 %pad_maximum_fusion = bf16[2,128,384]{2,1,0:T(8,128)(2,1)} fusion(bf16[1,512,384]{2,1,0:T(8,128)(2,1)} %bitcast.29, bf16[1,512,384]{2,1,0:T(8,128)(2,1)} %bitcast.26), kind=kLoop, calls=%fused_computation.14 | loop fusion | flops 393216 | bytes 983040 | tf_op jit(solution)/shard_map/stack | solution.py:115
  8.3 2.0 %fusion.5 = bf16[2,384,384]{2,1,0:T(8,128)(2,1)} fusion(bf16[1,512,384]{2,1,0:T(8,128)(2,1)} %bitcast.27, bf16[1,512,384]{2,1,0:T(8,128)(2,1)} %bitcast.30), kind=kLoop, calls=%fused_computation.13 | loop fusion | flops 294912 | bytes 1376256 | tf_op jit(solution)/shard_map/stack | solution.py:115
  10.3 1.4 %collective-permute-start.6 = (bf16[2,384,384]{2,1,0:T(8,128)(2,1)}, bf16[2,384,384]{2,1,0:T(8,128)(2,1)}, u32[]{:S(2)}, u32[]{:S(2)}) collective-permute-start(bf16[2,384,384]{2,1,0:T(8,128)(2,1)} %fusion.5), channel_id=1, source_target_pairs={{32,0},{48,16},{64,32},{80,48},{96,64},{112,80},{128,96},{144,112}... | collective-permute-start | bytes 1769480 | tf_op jit(solution)/shard_map/ppermute | solution.py:120
  11.7 1.3 collective-permute-start.5
  13.0 5.4 %collective-permute-start.4 = (bf16[2,384,384]{2,1,0:T(8,128)(2,1)}, bf16[2,384,384]{2,1,0:T(8,128)(2,1)}, u32[]{:S(2)}, u32[]{:S(2)}) collective-permute-start(bf16[2,384,384]{2,1,0:T(8,128)(2,1)} %fusion.5), channel_id=1, source_target_pairs={{0,16},{16,32},{32,48},{48,64},{64,80},{80,96},{96,112},{112,128},... | collective-permute-start | bytes 1769480 | tf_op jit(solution)/shard_map/ppermute | solution.py:120
  18.4 5.4 %collective-permute-start.3 = (bf16[2,384,384]{2,1,0:T(8,128)(2,1)}, bf16[2,384,384]{2,1,0:T(8,128)(2,1)S(1)}, u32[]{:S(2)}, u32[]{:S(2)}) collective-permute-start(bf16[2,384,384]{2,1,0:T(8,128)(2,1)} %fusion.5), channel_id=1, source_target_pairs={{0,32},{16,48},{32,64},{48,80},{64,96},{80,112},{96,128},{112,144}... | collective-permute-start | bytes 1769480 | tf_op jit(solution)/shard_map/ppermute | solution.py:120
  23.8 0.2 multiply_reduce_fusion
  24.0 0.2 fusion.2
  24.2 2.2 %collective-permute-start = (f32[2,512]{1,0:T(2,128)S(1)}, f32[2,512]{1,0:T(2,128)S(1)}, u32[]{:S(2)}, u32[]{:S(2)}) collective-permute-start(f32[2,512]{1,0:T(2,128)S(1)} %pad_maximum_fusion.1), channel_id=1, source_target_pairs={{0,2},{2,0},{4,6},{6,4},{8,10},{10,8},{12,14},{14,12},{1,3},{3,1},... | collective-permute-start | bytes 12296 | tf_op jit(solution)/shard_map/ppermute | solution.py:100
  26.4 0.1 copy.12
  26.5 1.4 %collective-permute-done = f32[2,512]{1,0:T(2,128)S(1)} collective-permute-done((f32[2,512]{1,0:T(2,128)S(1)}, f32[2,512]{1,0:T(2,128)S(1)}, u32[]{:S(2)}, u32[]{:S(2)}) %collective-permute-start) | collective-permute-done | bytes 4128 | tf_op jit(solution)/shard_map/ppermute | solution.py:100
  27.9 2.2 %collective-permute-start.1 = (f32[2,512]{1,0:T(2,128)S(1)}, f32[2,512]{1,0:T(2,128)S(1)}, u32[]{:S(2)}, u32[]{:S(2)}) collective-permute-start(f32[2,512]{1,0:T(2,128)S(1)} %fusion.14), channel_id=1, source_target_pairs={{0,4},{2,6},{4,0},{6,2},{8,12},{10,14},{12,8},{14,10},{1,5},{3,7},... | collective-permute-start | bytes 12296 | tf_op jit(solution)/shard_map/ppermute | solution.py:100
  30.1 3.0 %collective-permute-done.1 = f32[2,512]{1,0:T(2,128)S(1)} collective-permute-done((f32[2,512]{1,0:T(2,128)S(1)}, f32[2,512]{1,0:T(2,128)S(1)}, u32[]{:S(2)}, u32[]{:S(2)}) %collective-permute-start.1) | collective-permute-done | bytes 4128 | tf_op jit(solution)/shard_map/ppermute | solution.py:100
  33.1 7.2 %collective-permute-start.2 = (f32[2,512]{1,0:T(2,128)S(1)}, f32[2,512]{1,0:T(2,128)S(1)}, u32[]{:S(2)}, u32[]{:S(2)}) collective-permute-start(f32[2,512]{1,0:T(2,128)S(1)} %fusion.20), channel_id=1, source_target_pairs={{0,8},{2,10},{4,12},{6,14},{8,0},{10,2},{12,4},{14,6},{1,9},{3,11}... | collective-permute-start | bytes 12296 | tf_op jit(solution)/shard_map/ppermute | solution.py:100
  40.4 1.6 %collective-permute-done.2 = f32[2,512]{1,0:T(2,128)S(1)} collective-permute-done((f32[2,512]{1,0:T(2,128)S(1)}, f32[2,512]{1,0:T(2,128)S(1)}, u32[]{:S(2)}, u32[]{:S(2)}) %collective-permute-start.2) | collective-permute-done | bytes 4128 | tf_op jit(solution)/shard_map/ppermute | solution.py:100
  42.0 3.6 %collective-permute-start.7 = (f32[1,512]{1,0:T(1,128)S(1)}, f32[1,512]{1,0:T(1,128)S(1)}, u32[]{:S(2)}, u32[]{:S(2)}) collective-permute-start(f32[1,512]{1,0:T(1,128)S(1)} %get-tuple-element.13), channel_id=1, source_target_pairs={{0,16},{16,0},{32,48},{48,32},{64,80},{80,64},{96,112},{112,96},{1... | collective-permute-start | bytes 6152 | tf_op jit(solution)/shard_map/ppermute | solution.py:87
  45.6 21.0 %collective-permute-done.7 = f32[1,512]{1,0:T(1,128)S(1)} collective-permute-done((f32[1,512]{1,0:T(1,128)S(1)}, f32[1,512]{1,0:T(1,128)S(1)}, u32[]{:S(2)}, u32[]{:S(2)}) %collective-permute-start.7) | collective-permute-done | bytes 2080 | tf_op jit(solution)/shard_map/ppermute | solution.py:87
  66.6 30.7 %collective-permute-start.8 = (f32[2,512]{1,0:T(2,128)S(1)}, f32[2,512]{1,0:T(2,128)S(1)}, u32[]{:S(2)}, u32[]{:S(2)}) collective-permute-start(f32[2,512]{1,0:T(2,128)S(1)} %maximum_select_fusion.3), channel_id=1, source_target_pairs={{0,32},{16,48},{32,0},{48,16},{64,96},{80,112},{96,64},{112,80},{1... | collective-permute-start | bytes 12296 | tf_op jit(solution)/shard_map/ppermute | solution.py:87
  97.3 1.6 %collective-permute-done.8 = f32[2,512]{1,0:T(2,128)S(1)} collective-permute-done((f32[2,512]{1,0:T(2,128)S(1)}, f32[2,512]{1,0:T(2,128)S(1)}, u32[]{:S(2)}, u32[]{:S(2)}) %collective-permute-start.8) | collective-permute-done | bytes 4128 | tf_op jit(solution)/shard_map/ppermute | solution.py:87
  99.1 3.5 %collective-permute-done.9 = f32[4,512]{1,0:T(4,128)S(1)} collective-permute-done((f32[4,512]{1,0:T(4,128)S(1)}, f32[4,512]{1,0:T(4,128)S(1)}, u32[]{:S(2)}, u32[]{:S(2)}) %collective-permute-start.9) | collective-permute-done | bytes 8224 | tf_op jit(solution)/shard_map/ppermute | solution.py:87
  102.7 0.2 fusion.4.q_ref
  102.9 4.5 %collective-permute-done.10 = f32[8,512]{1,0:T(8,128)S(1)} collective-permute-done((f32[8,512]{1,0:T(8,128)S(1)}, f32[8,512]{1,0:T(8,128)S(1)}, u32[]{:S(2)}, u32[]{:S(2)}) %collective-permute-start.10) | collective-permute-done | bytes 16416 | tf_op jit(solution)/shard_map/ppermute | solution.py:87
  107.5 0.6 gather_fusion
  108.2 1.1 fusion.17
  109.5 1.1 fusion.16
  110.7 1.1 fusion.15
  112.1 0.4 copy-done.4
  112.5 0.4 multiply_convert_fusion.kn_ref
  112.9 7.2 %all-gather.3.cloned.1.call-done = bf16[2,2048,384]{2,1,0:T(8,128)(2,1)} async-done(((bf16[2,128,384]{2,1,0:T(8,128)(2,1)}), bf16[2,2048,384]{2,1,0:T(8,128)(2,1)}) %all-gather.3.cloned.1.call-update) | async-done | bytes 3145744 | tf_op jit(solution)/shard_map/all_gather | solution.py:116
  120.0 1.4 %slice-done = bf16[1,2048,384]{2,1,0:T(8,128)(2,1)S(1)} async-done(((bf16[2,2048,384]{2,1,0:T(8,128)(2,1)}), bf16[1,2048,384]{2,1,0:T(8,128)(2,1)S(1)}, s32[]{:S(2)}) %slice-start) | async-done | bytes 1572888 | tf_op jit(solution)/shard_map/slice | solution.py:145
  121.5 0.4 fusion.1.kf_ref
  121.9 11.0 %shard_map.73 = bf16[512,384]{1,0:T(8,128)(2,1)} custom-call(s32[3,4,12]{2,1,0:T(4,128)S(1)} %pad_add_fusion.sel_ref, bf16[512,384]{1,0:T(8,128)(2,1)S(1)} %fusion.4.q_ref, bf16[15,128,384]{2,1,0:T(8,128)(2,1)S(1)} %multiply_convert_fusion.kn_ref, bf16[15,128,384]{2,1,0:T(8,128)(2,1)S(1)} %constant_dynamic-update-slice_fusion.5.vn_ref, ...), custom_call_target="tpu_custom_call" | custom-call | flops 1207959552 | bytes 6881280 | tf_op jit(solution)/shard_map/pallas_call | solution.py:69
  (53 shorter events, 1.0 us)
Async XLA Ops:
  6.5 19.8 %copy-start = (s32[64,12]{0,1:T(8,128)S(1)}, s32[64,12]{0,1:T(8,128)}, u32[]{:S(2)}) copy-start(s32[64,12]{0,1:T(8,128)} %param.12) | copy-start | bytes 9220
  6.5 17.3 %copy-start.1 = (bf16[512,384]{1,0:T(8,128)(2,1)S(1)}, bf16[512,384]{1,0:T(8,128)(2,1)}, u32[]{:S(2)}) copy-start(bf16[512,384]{1,0:T(8,128)(2,1)} %param.8) | copy-start | bytes 1179652
  6.5 113.5 %all-gather.3.cloned.1.call-start = ((), (), s32[]{:S(2)}) async-start(), calls=%async_computation | async-start | bytes 3342336 | tf_op jit(solution)/shard_map/all_gather | solution.py:116
  6.5 17.4 %copy-start.3 = (bf16[512,384]{1,0:T(8,128)(2,1)S(1)}, bf16[512,384]{1,0:T(8,128)(2,1)}, u32[]{:S(2)}) copy-start(bf16[512,384]{1,0:T(8,128)(2,1)} %param.7) | copy-start | bytes 1179652
  8.3 37.3 %copy-start.6 = (s32[5]{0:T(128)S(1)}, s32[5]{0:T(128)}, u32[]{:S(2)}) copy-start(s32[5]{0:T(128)} %constant.121.clone) | copy-start | bytes 64
  8.3 90.8 %copy-start.2 = (bf16[512,384]{1,0:T(8,128)(2,1)S(1)}, bf16[512,384]{1,0:T(8,128)(2,1)}, u32[]{:S(2)}) copy-start(bf16[512,384]{1,0:T(8,128)(2,1)} %param.9) | copy-start | bytes 1179652
  10.3 92.5 %copy-start.5 = (f32[384]{0:T(512)S(1)}, f32[384]{0:T(512)}, u32[]{:S(2)}) copy-start(f32[384]{0:T(512)} %param.10) | copy-start | bytes 4612
  10.3 100.4 %collective-permute-start.6 = (bf16[2,384,384]{2,1,0:T(8,128)(2,1)}, bf16[2,384,384]{2,1,0:T(8,128)(2,1)}, u32[]{:S(2)}, u32[]{:S(2)}) collective-permute-start(bf16[2,384,384]{2,1,0:T(8,128)(2,1)} %fusion.5), channel_id=1, source_target_pairs={{32,0},{48,16},{64,32},{80,48},{96,64},{112,80},{128,96},{144,112}... | collective-permute-start | bytes 1769480 | tf_op jit(solution)/shard_map/ppermute | solution.py:120
  11.7 97.8 %collective-permute-start.5 = (bf16[2,384,384]{2,1,0:T(8,128)(2,1)}, bf16[2,384,384]{2,1,0:T(8,128)(2,1)}, u32[]{:S(2)}, u32[]{:S(2)}) collective-permute-start(bf16[2,384,384]{2,1,0:T(8,128)(2,1)} %fusion.5), channel_id=1, source_target_pairs={{16,0},{32,16},{48,32},{64,48},{80,64},{96,80},{112,96},{128,112},... | collective-permute-start | bytes 1769480 | tf_op jit(solution)/shard_map/ppermute | solution.py:120
  13.0 95.2 %collective-permute-start.4 = (bf16[2,384,384]{2,1,0:T(8,128)(2,1)}, bf16[2,384,384]{2,1,0:T(8,128)(2,1)}, u32[]{:S(2)}, u32[]{:S(2)}) collective-permute-start(bf16[2,384,384]{2,1,0:T(8,128)(2,1)} %fusion.5), channel_id=1, source_target_pairs={{0,16},{16,32},{32,48},{48,64},{64,80},{80,96},{96,112},{112,128},... | collective-permute-start | bytes 1769480 | tf_op jit(solution)/shard_map/ppermute | solution.py:120
  18.4 89.7 %collective-permute-start.3 = (bf16[2,384,384]{2,1,0:T(8,128)(2,1)}, bf16[2,384,384]{2,1,0:T(8,128)(2,1)S(1)}, u32[]{:S(2)}, u32[]{:S(2)}) collective-permute-start(bf16[2,384,384]{2,1,0:T(8,128)(2,1)} %fusion.5), channel_id=1, source_target_pairs={{0,32},{16,48},{32,64},{48,80},{64,96},{80,112},{96,128},{112,144}... | collective-permute-start | bytes 1769480 | tf_op jit(solution)/shard_map/ppermute | solution.py:120
  24.2 3.7 %collective-permute-start = (f32[2,512]{1,0:T(2,128)S(1)}, f32[2,512]{1,0:T(2,128)S(1)}, u32[]{:S(2)}, u32[]{:S(2)}) collective-permute-start(f32[2,512]{1,0:T(2,128)S(1)} %pad_maximum_fusion.1), channel_id=1, source_target_pairs={{0,2},{2,0},{4,6},{6,4},{8,10},{10,8},{12,14},{14,12},{1,3},{3,1},... | collective-permute-start | bytes 12296 | tf_op jit(solution)/shard_map/ppermute | solution.py:100
  27.9 5.2 %collective-permute-start.1 = (f32[2,512]{1,0:T(2,128)S(1)}, f32[2,512]{1,0:T(2,128)S(1)}, u32[]{:S(2)}, u32[]{:S(2)}) collective-permute-start(f32[2,512]{1,0:T(2,128)S(1)} %fusion.14), channel_id=1, source_target_pairs={{0,4},{2,6},{4,0},{6,2},{8,12},{10,14},{12,8},{14,10},{1,5},{3,7},... | collective-permute-start | bytes 12296 | tf_op jit(solution)/shard_map/ppermute | solution.py:100
  33.1 8.8 %collective-permute-start.2 = (f32[2,512]{1,0:T(2,128)S(1)}, f32[2,512]{1,0:T(2,128)S(1)}, u32[]{:S(2)}, u32[]{:S(2)}) collective-permute-start(f32[2,512]{1,0:T(2,128)S(1)} %fusion.20), channel_id=1, source_target_pairs={{0,8},{2,10},{4,12},{6,14},{8,0},{10,2},{12,4},{14,6},{1,9},{3,11}... | collective-permute-start | bytes 12296 | tf_op jit(solution)/shard_map/ppermute | solution.py:100
  42.0 24.6 %collective-permute-start.7 = (f32[1,512]{1,0:T(1,128)S(1)}, f32[1,512]{1,0:T(1,128)S(1)}, u32[]{:S(2)}, u32[]{:S(2)}) collective-permute-start(f32[1,512]{1,0:T(1,128)S(1)} %get-tuple-element.13), channel_id=1, source_target_pairs={{0,16},{16,0},{32,48},{48,32},{64,80},{80,64},{96,112},{112,96},{1... | collective-permute-start | bytes 6152 | tf_op jit(solution)/shard_map/ppermute | solution.py:87
  66.6 32.3 %collective-permute-start.8 = (f32[2,512]{1,0:T(2,128)S(1)}, f32[2,512]{1,0:T(2,128)S(1)}, u32[]{:S(2)}, u32[]{:S(2)}) collective-permute-start(f32[2,512]{1,0:T(2,128)S(1)} %maximum_select_fusion.3), channel_id=1, source_target_pairs={{0,32},{16,48},{32,0},{48,16},{64,96},{80,112},{96,64},{112,80},{1... | collective-permute-start | bytes 12296 | tf_op jit(solution)/shard_map/ppermute | solution.py:87
  98.9 3.8 %collective-permute-start.9 = (f32[4,512]{1,0:T(4,128)S(1)}, f32[4,512]{1,0:T(4,128)S(1)}, u32[]{:S(2)}, u32[]{:S(2)}) collective-permute-start(f32[4,512]{1,0:T(4,128)S(1)} %maximum_select_fusion.2), channel_id=1, source_target_pairs={{0,64},{16,80},{32,96},{48,112},{64,0},{80,16},{96,32},{112,48},{1... | collective-permute-start | bytes 24584 | tf_op jit(solution)/shard_map/ppermute | solution.py:87
  102.6 4.8 %collective-permute-start.10 = (f32[8,512]{1,0:T(8,128)S(1)}, f32[8,512]{1,0:T(8,128)S(1)}, u32[]{:S(2)}, u32[]{:S(2)}) collective-permute-start(f32[8,512]{1,0:T(8,128)S(1)} %maximum_select_fusion.1), channel_id=1, source_target_pairs={{0,128},{16,144},{32,160},{48,176},{64,192},{80,208},{96,224},{112... | collective-permute-start | bytes 49160 | tf_op jit(solution)/shard_map/ppermute | solution.py:87
  111.8 0.7 copy-start.4
  120.0 1.4 %slice-start = ((bf16[2,2048,384]{2,1,0:T(8,128)(2,1)}), bf16[1,2048,384]{2,1,0:T(8,128)(2,1)S(1)}, s32[]{:S(2)}) async-start(bf16[2,2048,384]{2,1,0:T(8,128)(2,1)} %all-gather.3.cloned.1.call-done), calls=%async_computation.1 | async-start | bytes 3145728 | tf_op jit(solution)/shard_map/slice | solution.py:145
Sparse Core Ops, SparseCore 0:
  9.1 110.8 all-gather.2

commit v6 on v5

--- a/solution.py
+++ b/solution.py
@@ -16,13 +16,17 @@
 EPS = 1e-06
 
 
-def attn_kernel(sel_ref, q_ref, kn_ref, vn_ref, kf_ref, vf_ref, o_ref, kc_ref, vc_ref, *, q_blocks, slots):
+def attn_kernel(
+    sel_ref, q_ref, kn_ref, vn_ref, kf_ref, vf_ref, fs_ref, g_ref, o_ref, kfn_ref, kc_ref, vc_ref,
+    *, q_blocks, slots,
+):
     scale = 1.0 / math.sqrt(HD)
+    kfn_ref[...] = (kf_ref[0].astype(jnp.float32) * fs_ref[...] * g_ref[...]).astype(jnp.bfloat16)
     for b in range(q_blocks):
         for j in range(slots):
             use_near = sel_ref[0, b, j] == 1
             rows = pl.ds(j * BLK, BLK)
-            kc_ref[rows, :] = jnp.where(use_near, kn_ref[sel_ref[1, b, j]], kf_ref[sel_ref[2, b, j]])
+            kc_ref[rows, :] = jnp.where(use_near, kn_ref[sel_ref[1, b, j]], kfn_ref[sel_ref[2, b, j]])
             vc_ref[rows, :] = jnp.where(
                 use_near, vn_ref[sel_ref[1, b, j]], vf_ref[0, sel_ref[2, b, j]]
             )
@@ -41,13 +45,13 @@
         o_ref[pl.ds(b * BLK, BLK), :] = (acc / total).astype(o_ref.dtype)
 
 
-def sparse_attend(sel, qn, kn_near, v_near, kn_first, first):
+def sparse_attend(sel, qn, kn_near, v_near, first, first_scale, gain_k):
     tok_rows, width = qn.shape
     heads = width // HD
     q_blocks = tok_rows // BLK
     slots = sel.shape[2]
     n_near = kn_near.shape[0]
-    n_first = kn_first.shape[0]
+    n_first = first.shape[1]
     kernel = functools.partial(attn_kernel, q_blocks=q_blocks, slots=slots)
     grid_spec = pltpu.PrefetchScalarGridSpec(
         num_scalar_prefetch=1,
@@ -56,11 +60,14 @@
             pl.BlockSpec((tok_rows, HD), lambda h, sel_ref: (0, h)),
             pl.BlockSpec((n_near, BLK, HD), lambda h, sel_ref: (0, 0, h)),
             pl.BlockSpec((n_near, BLK, HD), lambda h, sel_ref: (0, 0, h)),
-            pl.BlockSpec((n_first, BLK, HD), lambda h, sel_ref: (0, 0, h)),
+            pl.BlockSpec((1, n_first, BLK, HD), lambda h, sel_ref: (0, 0, 0, h)),
             pl.BlockSpec((1, n_first, BLK, HD), lambda h, sel_ref: (1, 0, 0, h)),
+            pl.BlockSpec((n_first, BLK, 1), lambda h, sel_ref: (0, 0, 0)),
+            pl.BlockSpec((1, HD), lambda h, sel_ref: (0, h)),
         ],
         out_specs=pl.BlockSpec((tok_rows, HD), lambda h, sel_ref: (0, h)),
         scratch_shapes=[
+            pltpu.VMEM((n_first, BLK, HD), jnp.bfloat16),
             pltpu.VMEM((slots * BLK, HD), jnp.bfloat16),
             pltpu.VMEM((slots * BLK, HD), jnp.bfloat16),
         ],
@@ -76,7 +83,7 @@
             transcendentals=q_blocks * slots * heads * BLK * BLK,
             bytes_accessed=2 * (2 * tok_rows * width + 2 * (n_near + n_first) * BLK * width),
         ),
-    )(sel, qn, kn_near, v_near, kn_first, first)
+    )(sel, qn, kn_near, v_near, first, first, first_scale, gain_k.reshape(1, width))
 
 
 def xor_gather(piece, n_frame, frame_pos):
@@ -142,7 +149,6 @@
     v_near = jnp.concatenate(
         [near[d][1].reshape(blocks - 1, BLK, width) for d in offsets], axis=0
     )
-    kn_first = (first[0].astype(jnp.float32) * first_scale * gain_k).astype(jnp.bfloat16)
 
     q_tiles = lax.dynamic_slice_in_dim(tiles, frame_pos * blocks, blocks, 0)
     key_slab = q_tiles // blocks
@@ -152,7 +158,7 @@
     near_idx = jnp.clip((dist + NEAR) * (blocks - 1) + within - 1, 0, len(offsets) * (blocks - 1) - 1)
     first_idx = jnp.clip(key_slab, 0, n_frame - 1)
     sel = jnp.stack([near_ok.astype(jnp.int32), near_idx, first_idx]).astype(jnp.int32)
-    return sparse_attend(sel, q_norm, kn_near, v_near, kn_first, first)
+    return sparse_attend(sel, q_norm, kn_near, v_near, first, first_scale, gain_k)
 
 
 def solution(mesh):

time: 140 us -> 139 us (level)
  the two profiles are of different devices: /device:TPU:2 before, /device:TPU:64 now
where the time goes in v6:
time: 139 us; the launch traced here: 138 us
  waiting for transfers between devices  56.2 us (40%)
  starting transfers between devices  42.5 us (31%)
  between operations  13.8 us (10%)
  Pallas kernels  12.2 us (9%)
  local copies, waits for them, and re-layouts  8.57 us (6%)
  other arithmetic  4.73 us (3%)
    ppermute x4, waiting for transfers between devices, xor_gather(): got = lax.ppermute(held, 'frame', perm)  50 us
    ppermute x4, starting transfers between devices, xor_gather(): got = lax.ppermute(held, 'frame', perm)  17.3 us
    ppermute x4, starting transfers between devices, body(): near[d] = lax.ppermute(tail, 'frame', perms[d])  15.1 us
    pallas_call x1, Pallas kernels, sparse_attend(): pl.pallas_call(kernel, grid_spec=grid_spec, out_shape=jax.ShapeDtypeStruc...  12.2 us
    ppermute x3, starting transfers between devices, xor_sum(): x = x + lax.ppermute(x, axis, perm)  10.2 us
    ppermute x3, waiting for transfers between devices, xor_sum(): x = x + lax.ppermute(x, axis, perm)  6.12 us
    slice x5, local copies, waits for them, and re-layouts, body(): near[d][1].reshape(blocks - 1, BLK, width)  4.48 us
    another operation x2, other arithmetic, body(): kv_raw = jnp.stack([k_proj, v_proj])  3.7 us
  transfers between devices with their start and end apart: 12, of which 7 were waited for; matrix products, arithmetic and copies ran while one was open for 7% of the time, Pallas kernels for 0%

profile of v6, /device:TPU:64, one launch (start us, length us, event | category | flops | bytes accessed | tf_op | source)
XLA Modules:
  0.0 138.0 jit_solution(12218864064620506618)
XLA Ops:
  6.5 1.7 %pad_maximum_fusion = bf16[2,128,384]{2,1,0:T(8,128)(2,1)} fusion(bf16[1,512,384]{2,1,0:T(8,128)(2,1)} %bitcast.29, bf16[1,512,384]{2,1,0:T(8,128)(2,1)} %bitcast.26), kind=kLoop, calls=%fused_computation.11 | loop fusion | flops 393216 | bytes 983040 | tf_op jit(solution)/shard_map/stack | solution.py:122
  8.3 2.0 %fusion.3 = bf16[2,384,384]{2,1,0:T(8,128)(2,1)} fusion(bf16[1,512,384]{2,1,0:T(8,128)(2,1)} %bitcast.27, bf16[1,512,384]{2,1,0:T(8,128)(2,1)} %bitcast.30), kind=kLoop, calls=%fused_computation.10 | loop fusion | flops 294912 | bytes 1376256 | tf_op jit(solution)/shard_map/stack | solution.py:122
  10.3 5.2 %collective-permute-start.3 = (bf16[2,384,384]{2,1,0:T(8,128)(2,1)}, bf16[2,384,384]{2,1,0:T(8,128)(2,1)}, u32[]{:S(2)}, u32[]{:S(2)}) collective-permute-start(bf16[2,384,384]{2,1,0:T(8,128)(2,1)} %fusion.3), channel_id=1, source_target_pairs={{0,32},{16,48},{32,64},{48,80},{64,96},{80,112},{96,128},{112,144}... | collective-permute-start | bytes 1769480 | tf_op jit(solution)/shard_map/ppermute | solution.py:127
  15.5 2.6 %collective-permute-start.4 = (bf16[2,384,384]{2,1,0:T(8,128)(2,1)}, bf16[2,384,384]{2,1,0:T(8,128)(2,1)}, u32[]{:S(2)}, u32[]{:S(2)}) collective-permute-start(bf16[2,384,384]{2,1,0:T(8,128)(2,1)} %fusion.3), channel_id=1, source_target_pairs={{0,16},{16,32},{32,48},{48,64},{64,80},{80,96},{96,112},{112,128},... | collective-permute-start | bytes 1769480 | tf_op jit(solution)/shard_map/ppermute | solution.py:127
  18.1 5.4 %collective-permute-start.5 = (bf16[2,384,384]{2,1,0:T(8,128)(2,1)}, bf16[2,384,384]{2,1,0:T(8,128)(2,1)}, u32[]{:S(2)}, u32[]{:S(2)}) collective-permute-start(bf16[2,384,384]{2,1,0:T(8,128)(2,1)} %fusion.3), channel_id=1, source_target_pairs={{16,0},{32,16},{48,32},{64,48},{80,64},{96,80},{112,96},{128,112},... | collective-permute-start | bytes 1769480 | tf_op jit(solution)/shard_map/ppermute | solution.py:127
  23.5 1.9 %collective-permute-start.6 = (bf16[2,384,384]{2,1,0:T(8,128)(2,1)}, bf16[2,384,384]{2,1,0:T(8,128)(2,1)}, u32[]{:S(2)}, u32[]{:S(2)}) collective-permute-start(bf16[2,384,384]{2,1,0:T(8,128)(2,1)} %fusion.3), channel_id=1, source_target_pairs={{32,0},{48,16},{64,32},{80,48},{96,64},{112,80},{128,96},{144,112}... | collective-permute-start | bytes 1769480 | tf_op jit(solution)/shard_map/ppermute | solution.py:127
  25.4 0.2 multiply_reduce_fusion
  25.6 0.2 fusion
  25.8 1.6 %collective-permute-start = (f32[2,512]{1,0:T(2,128)S(1)}, f32[2,512]{1,0:T(2,128)S(1)}, u32[]{:S(2)}, u32[]{:S(2)}) collective-permute-start(f32[2,512]{1,0:T(2,128)S(1)} %pad_maximum_fusion.1), channel_id=1, source_target_pairs={{0,2},{2,0},{4,6},{6,4},{8,10},{10,8},{12,14},{14,12},{1,3},{3,1},... | collective-permute-start | bytes 12296 | tf_op jit(solution)/shard_map/ppermute | solution.py:107
  27.4 0.1 copy.17
  27.5 1.9 %collective-permute-done = f32[2,512]{1,0:T(2,128)S(1)} collective-permute-done((f32[2,512]{1,0:T(2,128)S(1)}, f32[2,512]{1,0:T(2,128)S(1)}, u32[]{:S(2)}, u32[]{:S(2)}) %collective-permute-start) | collective-permute-done | bytes 4128 | tf_op jit(solution)/shard_map/ppermute | solution.py:107
  29.5 3.1 %collective-permute-start.1 = (f32[2,512]{1,0:T(2,128)S(1)}, f32[2,512]{1,0:T(2,128)S(1)}, u32[]{:S(2)}, u32[]{:S(2)}) collective-permute-start(f32[2,512]{1,0:T(2,128)S(1)} %fusion.13), channel_id=1, source_target_pairs={{0,4},{2,6},{4,0},{6,2},{8,12},{10,14},{12,8},{14,10},{1,5},{3,7},... | collective-permute-start | bytes 12296 | tf_op jit(solution)/shard_map/ppermute | solution.py:107
  32.6 2.1 %collective-permute-done.1 = f32[2,512]{1,0:T(2,128)S(1)} collective-permute-done((f32[2,512]{1,0:T(2,128)S(1)}, f32[2,512]{1,0:T(2,128)S(1)}, u32[]{:S(2)}, u32[]{:S(2)}) %collective-permute-start.1) | collective-permute-done | bytes 4128 | tf_op jit(solution)/shard_map/ppermute | solution.py:107
  34.7 5.5 %collective-permute-start.2 = (f32[2,512]{1,0:T(2,128)S(1)}, f32[2,512]{1,0:T(2,128)S(1)}, u32[]{:S(2)}, u32[]{:S(2)}) collective-permute-start(f32[2,512]{1,0:T(2,128)S(1)} %fusion.19), channel_id=1, source_target_pairs={{0,8},{2,10},{4,12},{6,14},{8,0},{10,2},{12,4},{14,6},{1,9},{3,11}... | collective-permute-start | bytes 12296 | tf_op jit(solution)/shard_map/ppermute | solution.py:107
  40.2 2.1 %collective-permute-done.2 = f32[2,512]{1,0:T(2,128)S(1)} collective-permute-done((f32[2,512]{1,0:T(2,128)S(1)}, f32[2,512]{1,0:T(2,128)S(1)}, u32[]{:S(2)}, u32[]{:S(2)}) %collective-permute-start.2) | collective-permute-done | bytes 4128 | tf_op jit(solution)/shard_map/ppermute | solution.py:107
  42.3 0.9 collective-permute-start.7
  43.3 39.0 %collective-permute-done.7 = f32[1,512]{1,0:T(1,128)S(1)} collective-permute-done((f32[1,512]{1,0:T(1,128)S(1)}, f32[1,512]{1,0:T(1,128)S(1)}, u32[]{:S(2)}, u32[]{:S(2)}) %collective-permute-start.7) | collective-permute-done | bytes 2080 | tf_op jit(solution)/shard_map/ppermute | solution.py:94
  82.5 5.1 %collective-permute-done.8 = f32[2,512]{1,0:T(2,128)S(1)} collective-permute-done((f32[2,512]{1,0:T(2,128)S(1)}, f32[2,512]{1,0:T(2,128)S(1)}, u32[]{:S(2)}, u32[]{:S(2)}) %collective-permute-start.8) | collective-permute-done | bytes 4128 | tf_op jit(solution)/shard_map/ppermute | solution.py:94
  87.5 16.1 %collective-permute-start.9 = (f32[4,512]{1,0:T(4,128)S(1)}, f32[4,512]{1,0:T(4,128)S(1)}, u32[]{:S(2)}, u32[]{:S(2)}) collective-permute-start(f32[4,512]{1,0:T(4,128)S(1)} %maximum_select_fusion.2), channel_id=1, source_target_pairs={{0,64},{16,80},{32,96},{48,112},{64,0},{80,16},{96,32},{112,48},{1... | collective-permute-start | bytes 24584 | tf_op jit(solution)/shard_map/ppermute | solution.py:94
  103.8 1.5 %collective-permute-done.9 = f32[4,512]{1,0:T(4,128)S(1)} collective-permute-done((f32[4,512]{1,0:T(4,128)S(1)}, f32[4,512]{1,0:T(4,128)S(1)}, u32[]{:S(2)}, u32[]{:S(2)}) %collective-permute-start.9) | collective-permute-done | bytes 8224 | tf_op jit(solution)/shard_map/ppermute | solution.py:94
  105.4 0.2 fusion.2.q_ref
  105.6 4.4 %collective-permute-done.10 = f32[8,512]{1,0:T(8,128)S(1)} collective-permute-done((f32[8,512]{1,0:T(8,128)S(1)}, f32[8,512]{1,0:T(8,128)S(1)}, u32[]{:S(2)}, u32[]{:S(2)}) %collective-permute-start.10) | collective-permute-done | bytes 16416 | tf_op jit(solution)/shard_map/ppermute | solution.py:94
  110.0 0.6 gather_fusion
  110.6 0.4 copy.16.fs_ref
  111.0 1.1 fusion.17
  112.2 1.1 fusion.16
  113.5 1.1 fusion.15
  114.7 1.1 fusion.14
  116.1 1.1 copy-done.1
  117.2 0.4 multiply_convert_fusion.kn_ref
  117.6 1.4 copy-done.2
  119.0 12.2 %shard_map.73 = bf16[512,384]{1,0:T(8,128)(2,1)} custom-call(s32[3,4,12]{2,1,0:T(4,128)S(1)} %pad_add_fusion.sel_ref, bf16[512,384]{1,0:T(8,128)(2,1)S(1)} %fusion.2.q_ref, bf16[15,128,384]{2,1,0:T(8,128)(2,1)S(1)} %multiply_convert_fusion.kn_ref, bf16[15,128,384]{2,1,0:T(8,128)(2,1)S(1)} %copy-done.2, bf16[2,16,128,384]{3,2,1,0:T(8,128)(2,1)} %bitcast.24, ...), custom_call_target="tpu_custom_call" | custom-call | flops 1207959552 | bytes 6881280 | tf_op jit(solution)/shard_map/pallas_call | solution.py:76
  (56 shorter events, 1.0 us)
Async XLA Ops:
  6.5 20.8 %copy-start = (s32[64,12]{0,1:T(8,128)S(1)}, s32[64,12]{0,1:T(8,128)}, u32[]{:S(2)}) copy-start(s32[64,12]{0,1:T(8,128)} %param.12) | copy-start | bytes 9220
  6.5 18.9 %copy-start.3 = (bf16[512,384]{1,0:T(8,128)(2,1)S(1)}, bf16[512,384]{1,0:T(8,128)(2,1)}, u32[]{:S(2)}) copy-start(bf16[512,384]{1,0:T(8,128)(2,1)} %param.8) | copy-start | bytes 1179652
  6.5 111.1 %all-gather.3.cloned.1.call-start = ((), (), s32[]{:S(2)}) async-start(), calls=%async_computation | async-start | bytes 3342336 | tf_op jit(solution)/shard_map/all_gather | solution.py:123
  6.5 19.0 %copy-start.5 = (bf16[512,384]{1,0:T(8,128)(2,1)S(1)}, bf16[512,384]{1,0:T(8,128)(2,1)}, u32[]{:S(2)}) copy-start(bf16[512,384]{1,0:T(8,128)(2,1)} %param.7) | copy-start | bytes 1179652
  8.3 35.0 %copy-start.8 = (s32[5]{0:T(128)S(1)}, s32[5]{0:T(128)}, u32[]{:S(2)}) copy-start(s32[5]{0:T(128)} %constant.121.clone) | copy-start | bytes 64
  8.3 95.4 %copy-start.4 = (bf16[512,384]{1,0:T(8,128)(2,1)S(1)}, bf16[512,384]{1,0:T(8,128)(2,1)}, u32[]{:S(2)}) copy-start(bf16[512,384]{1,0:T(8,128)(2,1)} %param.9) | copy-start | bytes 1179652
  10.3 93.5 %copy-start.6 = (f32[384]{0:T(512)S(1)}, f32[384]{0:T(512)}, u32[]{:S(2)}) copy-start(f32[384]{0:T(512)} %param.11) | copy-start | bytes 4612
  10.3 95.1 %copy-start.7 = (f32[384]{0:T(512)S(1)}, f32[384]{0:T(512)}, u32[]{:S(2)}) copy-start(f32[384]{0:T(512)} %param.10) | copy-start | bytes 4612
  10.3 100.7 %collective-permute-start.3 = (bf16[2,384,384]{2,1,0:T(8,128)(2,1)}, bf16[2,384,384]{2,1,0:T(8,128)(2,1)}, u32[]{:S(2)}, u32[]{:S(2)}) collective-permute-start(bf16[2,384,384]{2,1,0:T(8,128)(2,1)} %fusion.3), channel_id=1, source_target_pairs={{0,32},{16,48},{32,64},{48,80},{64,96},{80,112},{96,128},{112,144}... | collective-permute-start | bytes 1769480 | tf_op jit(solution)/shard_map/ppermute | solution.py:127
  15.5 96.7 %collective-permute-start.4 = (bf16[2,384,384]{2,1,0:T(8,128)(2,1)}, bf16[2,384,384]{2,1,0:T(8,128)(2,1)}, u32[]{:S(2)}, u32[]{:S(2)}) collective-permute-start(bf16[2,384,384]{2,1,0:T(8,128)(2,1)} %fusion.3), channel_id=1, source_target_pairs={{0,16},{16,32},{32,48},{48,64},{64,80},{80,96},{96,112},{112,128},... | collective-permute-start | bytes 1769480 | tf_op jit(solution)/shard_map/ppermute | solution.py:127
  18.1 95.3 %collective-permute-start.5 = (bf16[2,384,384]{2,1,0:T(8,128)(2,1)}, bf16[2,384,384]{2,1,0:T(8,128)(2,1)}, u32[]{:S(2)}, u32[]{:S(2)}) collective-permute-start(bf16[2,384,384]{2,1,0:T(8,128)(2,1)} %fusion.3), channel_id=1, source_target_pairs={{16,0},{32,16},{48,32},{64,48},{80,64},{96,80},{112,96},{128,112},... | collective-permute-start | bytes 1769480 | tf_op jit(solution)/shard_map/ppermute | solution.py:127
  23.5 91.2 %collective-permute-start.6 = (bf16[2,384,384]{2,1,0:T(8,128)(2,1)}, bf16[2,384,384]{2,1,0:T(8,128)(2,1)}, u32[]{:S(2)}, u32[]{:S(2)}) collective-permute-start(bf16[2,384,384]{2,1,0:T(8,128)(2,1)} %fusion.3), channel_id=1, source_target_pairs={{32,0},{48,16},{64,32},{80,48},{96,64},{112,80},{128,96},{144,112}... | collective-permute-start | bytes 1769480 | tf_op jit(solution)/shard_map/ppermute | solution.py:127
  25.8 3.7 %collective-permute-start = (f32[2,512]{1,0:T(2,128)S(1)}, f32[2,512]{1,0:T(2,128)S(1)}, u32[]{:S(2)}, u32[]{:S(2)}) collective-permute-start(f32[2,512]{1,0:T(2,128)S(1)} %pad_maximum_fusion.1), channel_id=1, source_target_pairs={{0,2},{2,0},{4,6},{6,4},{8,10},{10,8},{12,14},{14,12},{1,3},{3,1},... | collective-permute-start | bytes 12296 | tf_op jit(solution)/shard_map/ppermute | solution.py:107
  29.5 5.2 %collective-permute-start.1 = (f32[2,512]{1,0:T(2,128)S(1)}, f32[2,512]{1,0:T(2,128)S(1)}, u32[]{:S(2)}, u32[]{:S(2)}) collective-permute-start(f32[2,512]{1,0:T(2,128)S(1)} %fusion.13), channel_id=1, source_target_pairs={{0,4},{2,6},{4,0},{6,2},{8,12},{10,14},{12,8},{14,10},{1,5},{3,7},... | collective-permute-start | bytes 12296 | tf_op jit(solution)/shard_map/ppermute | solution.py:107
  34.7 7.6 %collective-permute-start.2 = (f32[2,512]{1,0:T(2,128)S(1)}, f32[2,512]{1,0:T(2,128)S(1)}, u32[]{:S(2)}, u32[]{:S(2)}) collective-permute-start(f32[2,512]{1,0:T(2,128)S(1)} %fusion.19), channel_id=1, source_target_pairs={{0,8},{2,10},{4,12},{6,14},{8,0},{10,2},{12,4},{14,6},{1,9},{3,11}... | collective-permute-start | bytes 12296 | tf_op jit(solution)/shard_map/ppermute | solution.py:107
  42.3 40.0 %collective-permute-start.7 = (f32[1,512]{1,0:T(1,128)S(1)}, f32[1,512]{1,0:T(1,128)S(1)}, u32[]{:S(2)}, u32[]{:S(2)}) collective-permute-start(f32[1,512]{1,0:T(1,128)S(1)} %get-tuple-element.13), channel_id=1, source_target_pairs={{0,16},{16,0},{32,48},{48,32},{64,80},{80,64},{96,112},{112,96},{1... | collective-permute-start | bytes 6152 | tf_op jit(solution)/shard_map/ppermute | solution.py:94
  82.3 5.2 %collective-permute-start.8 = (f32[2,512]{1,0:T(2,128)S(1)}, f32[2,512]{1,0:T(2,128)S(1)}, u32[]{:S(2)}, u32[]{:S(2)}) collective-permute-start(f32[2,512]{1,0:T(2,128)S(1)} %maximum_select_fusion.3), channel_id=1, source_target_pairs={{0,32},{16,48},{32,0},{48,16},{64,96},{80,112},{96,64},{112,80},{1... | collective-permute-start | bytes 12296 | tf_op jit(solution)/shard_map/ppermute | solution.py:94
  87.5 17.8 %collective-permute-start.9 = (f32[4,512]{1,0:T(4,128)S(1)}, f32[4,512]{1,0:T(4,128)S(1)}, u32[]{:S(2)}, u32[]{:S(2)}) collective-permute-start(f32[4,512]{1,0:T(4,128)S(1)} %maximum_select_fusion.2), channel_id=1, source_target_pairs={{0,64},{16,80},{32,96},{48,112},{64,0},{80,16},{96,32},{112,48},{1... | collective-permute-start | bytes 24584 | tf_op jit(solution)/shard_map/ppermute | solution.py:94
  105.3 4.7 %collective-permute-start.10 = (f32[8,512]{1,0:T(8,128)S(1)}, f32[8,512]{1,0:T(8,128)S(1)}, u32[]{:S(2)}, u32[]{:S(2)}) collective-permute-start(f32[8,512]{1,0:T(8,128)S(1)} %maximum_select_fusion.1), channel_id=1, source_target_pairs={{0,128},{16,144},{32,160},{48,176},{64,192},{80,208},{96,224},{112... | collective-permute-start | bytes 49160 | tf_op jit(solution)/shard_map/ppermute | solution.py:94
  116.0 1.1 copy-start.1
  117.6 1.4 copy-start.2
Sparse Core Ops, SparseCore 0:
  9.1 102.6 all-gather.2

commit v7 on v5

--- a/solution.py
+++ b/solution.py
@@ -14,6 +14,8 @@
 NEAR = 2
 
 EPS = 1e-06
+FRAME = ("zl", "y")
+Y_SIZE = 4
 
 
 def attn_kernel(sel_ref, q_ref, kn_ref, vn_ref, kf_ref, vf_ref, o_ref, kc_ref, vc_ref, *, q_blocks, slots):
@@ -84,7 +86,7 @@
     bit = 1
     while bit < n_frame:
         perm = [(i, i ^ bit) for i in range(n_frame)]
-        got = lax.ppermute(held, "frame", perm)
+        got = lax.ppermute(held, FRAME, perm)
         upper = (frame_pos // bit) % 2 == 1
         held = jnp.where(
             upper, jnp.concatenate([got, held], axis=0), jnp.concatenate([held, got], axis=0)
@@ -105,7 +107,7 @@
 def body(q_proj, k_proj, v_proj, gain_q, gain_k, tiles, *, n_frame, n_tensor):
     tok_rows, width = q_proj.shape
     blocks = tok_rows // BLK
-    frame_pos = lax.axis_index("frame")
+    frame_pos = lax.axis_index("zl") * lax.axis_size("y") + lax.axis_index("y")
     full_width = width * lax.axis_size("tensor")
     offsets = list(range(-NEAR, NEAR + 1))
     perms = {
@@ -113,11 +115,13 @@
     }
 
     kv_raw = jnp.stack([k_proj, v_proj])
-    first = lax.all_gather(kv_raw[:, :BLK], "frame", axis=1, tiled=False)
+    first = lax.all_gather(kv_raw[:, :BLK], "y", axis=1, tiled=False)
+    first = lax.all_gather(first, "zl", axis=1, tiled=False)
+    first = first.reshape(2, n_frame, BLK, width)
     tail = kv_raw[:, BLK:]
     near = {0: tail}
     for d in perms:
-        near[d] = lax.ppermute(tail, "frame", perms[d])
+        near[d] = lax.ppermute(tail, FRAME, perms[d])
 
     q_wide = q_proj.astype(jnp.float32)
     k_wide = k_proj.astype(jnp.float32)
@@ -156,17 +160,22 @@
 
 
 def solution(mesh):
+    n_frame, n_tensor, n_dp = (mesh.shape[a] for a in ("frame", "tensor", "dp"))
+    assert mesh.axis_names == ("frame", "tensor", "dp") and n_frame % Y_SIZE == 0
+    split = jax.sharding.Mesh(
+        mesh.devices.reshape(n_frame // Y_SIZE, Y_SIZE, n_tensor, n_dp), ("zl", "y", "tensor", "dp")
+    )
     return jax.shard_map(
         functools.partial(body, n_frame=mesh.shape["frame"], n_tensor=mesh.shape["tensor"]),
-        mesh=mesh,
+        mesh=split,
         in_specs=(
-            P(("dp", "frame"), "tensor"),
-            P(("dp", "frame"), "tensor"),
-            P(("dp", "frame"), "tensor"),
+            P(("dp", "zl", "y"), "tensor"),
+            P(("dp", "zl", "y"), "tensor"),
+            P(("dp", "zl", "y"), "tensor"),
             P("tensor"),
             P("tensor"),
             P("dp", None),
         ),
-        out_specs=P(("dp", "frame"), "tensor"),
+        out_specs=P(("dp", "zl", "y"), "tensor"),
         check_vma=False,
     )

time: 140 us -> 165 us (1.18)
  the two profiles are of different devices: /device:TPU:2 before, /device:TPU:64 now
where the time goes in v7:
time: 165 us; the launch traced here: 164 us
  waiting for transfers between devices  50.7 us (31%)
  blocking collectives  50.3 us (30%)
  starting transfers between devices  29 us (18%)
  between operations  13.8 us (8%)
  Pallas kernels  11 us (7%)
  other arithmetic  4.94 us (3%)
  local copies, waits for them, and re-layouts  4.02 us (2%)
    all_gather x1, blocking collectives, body(): first = lax.all_gather(kv_raw[:, :BLK], 'y', axis=1, tiled=False)  50.3 us
    all_gather x1, waiting for transfers between devices, body(): first = lax.all_gather(first, 'zl', axis=1, tiled=False)  32.6 us
    ppermute x4, starting transfers between devices, body(): near[d] = lax.ppermute(tail, FRAME, perms[d])  15 us
    ppermute x4, waiting for transfers between devices, xor_gather(): got = lax.ppermute(held, FRAME, perm)  14.3 us
    pallas_call x1, Pallas kernels, sparse_attend(): pl.pallas_call(kernel, grid_spec=grid_spec, out_shape=jax.ShapeDtypeStruc...  11 us
    ppermute x3, starting transfers between devices, xor_sum(): x = x + lax.ppermute(x, axis, perm)  10.6 us
    ppermute x3, waiting for transfers between devices, xor_sum(): x = x + lax.ppermute(x, axis, perm)  3.7 us
    ppermute x4, starting transfers between devices, xor_gather(): got = lax.ppermute(held, FRAME, perm)  3.4 us
  transfers between devices with their start and end apart: 12, of which 7 were waited for; matrix products, arithmetic and copies ran while one was open for 3% of the time, Pallas kernels for 0%

profile of v7, /device:TPU:64, one launch (start us, length us, event | category | flops | bytes accessed | tf_op | source)
XLA Modules:
  0.0 163.8 jit_solution(1053512971001670258)
XLA Ops:
  6.6 2.0 %fusion.5 = bf16[2,384,384]{2,1,0:T(8,128)(2,1)} fusion(bf16[1,512,384]{2,1,0:T(8,128)(2,1)} %bitcast.27, bf16[1,512,384]{2,1,0:T(8,128)(2,1)} %bitcast.31), kind=kLoop, calls=%fused_computation.14 | loop fusion | flops 294912 | bytes 1376256 | tf_op jit(solution)/shard_map/stack | solution.py:117
  8.6 5.1 %collective-permute-start.3 = (bf16[2,384,384]{2,1,0:T(8,128)(2,1)}, bf16[2,384,384]{2,1,0:T(8,128)(2,1)S(1)}, u32[]{:S(2)}, u32[]{:S(2)}) collective-permute-start(bf16[2,384,384]{2,1,0:T(8,128)(2,1)} %fusion.5), channel_id=1, source_target_pairs={{0,32},{16,48},{32,64},{48,80},{64,96},{80,112},{96,128},{112,144}... | collective-permute-start | bytes 1769480 | tf_op jit(solution)/shard_map/ppermute | solution.py:124
  13.7 2.6 %collective-permute-start.4 = (bf16[2,384,384]{2,1,0:T(8,128)(2,1)}, bf16[2,384,384]{2,1,0:T(8,128)(2,1)}, u32[]{:S(2)}, u32[]{:S(2)}) collective-permute-start(bf16[2,384,384]{2,1,0:T(8,128)(2,1)} %fusion.5), channel_id=1, source_target_pairs={{0,16},{16,32},{32,48},{48,64},{64,80},{80,96},{96,112},{112,128},... | collective-permute-start | bytes 1769480 | tf_op jit(solution)/shard_map/ppermute | solution.py:124
  16.3 5.4 %collective-permute-start.5 = (bf16[2,384,384]{2,1,0:T(8,128)(2,1)}, bf16[2,384,384]{2,1,0:T(8,128)(2,1)}, u32[]{:S(2)}, u32[]{:S(2)}) collective-permute-start(bf16[2,384,384]{2,1,0:T(8,128)(2,1)} %fusion.5), channel_id=1, source_target_pairs={{16,0},{32,16},{48,32},{64,48},{80,64},{96,80},{112,96},{128,112},... | collective-permute-start | bytes 1769480 | tf_op jit(solution)/shard_map/ppermute | solution.py:124
  21.7 1.9 %collective-permute-start.6 = (bf16[2,384,384]{2,1,0:T(8,128)(2,1)}, bf16[2,384,384]{2,1,0:T(8,128)(2,1)S(1)}, u32[]{:S(2)}, u32[]{:S(2)}) collective-permute-start(bf16[2,384,384]{2,1,0:T(8,128)(2,1)} %fusion.5), channel_id=1, source_target_pairs={{32,0},{48,16},{64,32},{80,48},{96,64},{112,80},{128,96},{144,112}... | collective-permute-start | bytes 1769480 | tf_op jit(solution)/shard_map/ppermute | solution.py:124
  23.6 0.2 multiply_reduce_fusion
  23.8 0.2 fusion.2
  24.0 1.6 collective-permute-start
  25.6 50.3 %all-gather = bf16[2,512,384]{2,1,0:T(8,128)(2,1)} all-gather(bf16[2,128,384]{2,1,0:T(8,128)(2,1)S(1)} %pad_maximum_fusion), channel_id=2, replica_groups=mesh['zl'=4,'y'=4,'tensor'=8,'dp'=2] {'y'}, dimensions={1}, use_global_device_ids=true | all-gather | bytes 983040 | tf_op jit(solution)/shard_map/all_gather | solution.py:118
  75.9 0.1 constant_dynamic-slice_fusion
  76.0 0.1 copy.12
  76.1 3.1 %collective-permute-start.1 = (f32[2,512]{1,0:T(2,128)S(1)}, f32[2,512]{1,0:T(2,128)S(1)}, u32[]{:S(2)}, u32[]{:S(2)}) collective-permute-start(f32[2,512]{1,0:T(2,128)S(1)} %fusion.14), channel_id=1, source_target_pairs={{0,4},{2,6},{4,0},{6,2},{8,12},{10,14},{12,8},{14,10},{1,5},{3,7},... | collective-permute-start | bytes 12296 | tf_op jit(solution)/shard_map/ppermute | solution.py:102
  79.2 2.1 %collective-permute-done.1 = f32[2,512]{1,0:T(2,128)S(1)} collective-permute-done((f32[2,512]{1,0:T(2,128)S(1)}, f32[2,512]{1,0:T(2,128)S(1)}, u32[]{:S(2)}, u32[]{:S(2)}) %collective-permute-start.1) | collective-permute-done | bytes 4128 | tf_op jit(solution)/shard_map/ppermute | solution.py:102
  81.3 6.0 %collective-permute-start.2 = (f32[2,512]{1,0:T(2,128)S(1)}, f32[2,512]{1,0:T(2,128)S(1)}, u32[]{:S(2)}, u32[]{:S(2)}) collective-permute-start(f32[2,512]{1,0:T(2,128)S(1)} %fusion.20), channel_id=1, source_target_pairs={{0,8},{2,10},{4,12},{6,14},{8,0},{10,2},{12,4},{14,6},{1,9},{3,11}... | collective-permute-start | bytes 12296 | tf_op jit(solution)/shard_map/ppermute | solution.py:102
  87.3 1.6 collective-permute-done.2
  88.9 0.1 collective-permute-start.7
  89.1 3.5 %collective-permute-done.7 = f32[1,512]{1,0:T(1,128)S(1)} collective-permute-done((f32[1,512]{1,0:T(1,128)S(1)}, f32[1,512]{1,0:T(1,128)S(1)}, u32[]{:S(2)}, u32[]{:S(2)}) %collective-permute-start.7) | collective-permute-done | bytes 2080 | tf_op jit(solution)/shard_map/ppermute | solution.py:89
  92.6 1.5 collective-permute-start.8
  94.2 3.6 %collective-permute-done.8 = f32[2,512]{1,0:T(2,128)S(1)} collective-permute-done((f32[2,512]{1,0:T(2,128)S(1)}, f32[2,512]{1,0:T(2,128)S(1)}, u32[]{:S(2)}, u32[]{:S(2)}) %collective-permute-start.8) | collective-permute-done | bytes 4128 | tf_op jit(solution)/shard_map/ppermute | solution.py:89
  97.8 0.1 collective-permute-start.9
  98.1 3.8 %collective-permute-done.9 = f32[4,512]{1,0:T(4,128)S(1)} collective-permute-done((f32[4,512]{1,0:T(4,128)S(1)}, f32[4,512]{1,0:T(4,128)S(1)}, u32[]{:S(2)}, u32[]{:S(2)}) %collective-permute-start.9) | collective-permute-done | bytes 8224 | tf_op jit(solution)/shard_map/ppermute | solution.py:89
  101.9 1.7 %collective-permute-start.10 = (f32[8,512]{1,0:T(8,128)S(1)}, f32[8,512]{1,0:T(8,128)S(1)}, u32[]{:S(2)}, u32[]{:S(2)}) collective-permute-start(f32[8,512]{1,0:T(8,128)S(1)} %maximum_select_fusion.1), channel_id=1, source_target_pairs={{0,128},{16,144},{32,160},{48,176},{64,192},{80,208},{96,224},{112... | collective-permute-start | bytes 49160 | tf_op jit(solution)/shard_map/ppermute | solution.py:89
  103.5 0.2 fusion.4.q_ref
  103.7 3.4 %collective-permute-done.10 = f32[8,512]{1,0:T(8,128)S(1)} collective-permute-done((f32[8,512]{1,0:T(8,128)S(1)}, f32[8,512]{1,0:T(8,128)S(1)}, u32[]{:S(2)}, u32[]{:S(2)}) %collective-permute-start.10) | collective-permute-done | bytes 16416 | tf_op jit(solution)/shard_map/ppermute | solution.py:89
  107.1 0.6 gather_fusion
  107.8 1.1 fusion.17
  109.1 1.1 fusion.16
  110.6 0.4 copy-done.4
  111.0 0.4 multiply_convert_fusion.kn_ref
  111.5 32.6 %all-gather.4.cloned.1.call-done.vf_ref = bf16[2,16,128,384]{3,2,1,0:T(8,128)(2,1)} async-done(((bf16[2,4,128,384]{3,2,1,0:T(8,128)(2,1)}), bf16[2,16,128,384]{3,2,1,0:T(8,128)(2,1)}) %all-gather.4.cloned.1.call-update) | async-done | bytes 3145744 | tf_op jit(solution)/shard_map/all_gather | solution.py:119
  144.1 1.8 %fusion.1.kf_ref = bf16[16,128,384]{2,1,0:T(8,128)(2,1)S(1)} fusion(bf16[2,16,128,384]{3,2,1,0:T(8,128)(2,1)} %all-gather.4.cloned.1.call-done.vf_ref, f32[384]{0:T(512)S(1)} %copy-done.4, f32[16,128]{1,0:T(8,128)S(1)} %fusion.9), kind=kLoop, calls=%fused_computation.3 | loop fusion | flops 3145728 | bytes 3155456 | tf_op jit(solution)/shard_map/convert_element_type | solution.py:149
  145.9 11.0 %shard_map.73 = bf16[512,384]{1,0:T(8,128)(2,1)} custom-call(s32[3,4,12]{2,1,0:T(4,128)S(1)} %pad_add_fusion.sel_ref, bf16[512,384]{1,0:T(8,128)(2,1)S(1)} %fusion.4.q_ref, bf16[15,128,384]{2,1,0:T(8,128)(2,1)S(1)} %multiply_convert_fusion.kn_ref, bf16[15,128,384]{2,1,0:T(8,128)(2,1)S(1)} %constant_dynamic-update-slice_fusion.5.vn_ref, ...), custom_call_target="tpu_custom_call" | custom-call | flops 1207959552 | bytes 6881280 | tf_op jit(solution)/shard_map/pallas_call | solution.py:71
  (52 shorter events, 0.9 us)
Async XLA Ops:
  6.5 69.4 %copy-start = (s32[64,12]{0,1:T(8,128)S(1)}, s32[64,12]{0,1:T(8,128)}, u32[]{:S(2)}) copy-start(s32[64,12]{0,1:T(8,128)} %param.12) | copy-start | bytes 9220
  6.5 17.1 %copy-start.1 = (bf16[512,384]{1,0:T(8,128)(2,1)S(1)}, bf16[512,384]{1,0:T(8,128)(2,1)}, u32[]{:S(2)}) copy-start(bf16[512,384]{1,0:T(8,128)(2,1)} %param.8) | copy-start | bytes 1179652
  6.5 19.0 %copy-start.2 = (bf16[512,384]{1,0:T(8,128)(2,1)S(1)}, bf16[512,384]{1,0:T(8,128)(2,1)}, u32[]{:S(2)}) copy-start(bf16[512,384]{1,0:T(8,128)(2,1)} %param.9) | copy-start | bytes 1179652
  6.5 17.3 %copy-start.3 = (bf16[512,384]{1,0:T(8,128)(2,1)S(1)}, bf16[512,384]{1,0:T(8,128)(2,1)}, u32[]{:S(2)}) copy-start(bf16[512,384]{1,0:T(8,128)(2,1)} %param.7) | copy-start | bytes 1179652
  6.5 137.5 %all-gather.4.cloned.1.call-start = ((), (), s32[]{:S(2)}) async-start(), calls=%async_computation | async-start | bytes 3932160 | tf_op jit(solution)/shard_map/all_gather | solution.py:119
  8.6 99.0 %collective-permute-start.3 = (bf16[2,384,384]{2,1,0:T(8,128)(2,1)}, bf16[2,384,384]{2,1,0:T(8,128)(2,1)S(1)}, u32[]{:S(2)}, u32[]{:S(2)}) collective-permute-start(bf16[2,384,384]{2,1,0:T(8,128)(2,1)} %fusion.5), channel_id=1, source_target_pairs={{0,32},{16,48},{32,64},{48,80},{64,96},{80,112},{96,128},{112,144}... | collective-permute-start | bytes 1769480 | tf_op jit(solution)/shard_map/ppermute | solution.py:124
  13.7 94.1 %collective-permute-start.4 = (bf16[2,384,384]{2,1,0:T(8,128)(2,1)}, bf16[2,384,384]{2,1,0:T(8,128)(2,1)}, u32[]{:S(2)}, u32[]{:S(2)}) collective-permute-start(bf16[2,384,384]{2,1,0:T(8,128)(2,1)} %fusion.5), channel_id=1, source_target_pairs={{0,16},{16,32},{32,48},{48,64},{64,80},{80,96},{96,112},{112,128},... | collective-permute-start | bytes 1769480 | tf_op jit(solution)/shard_map/ppermute | solution.py:124
  16.3 92.8 %collective-permute-start.5 = (bf16[2,384,384]{2,1,0:T(8,128)(2,1)}, bf16[2,384,384]{2,1,0:T(8,128)(2,1)}, u32[]{:S(2)}, u32[]{:S(2)}) collective-permute-start(bf16[2,384,384]{2,1,0:T(8,128)(2,1)} %fusion.5), channel_id=1, source_target_pairs={{16,0},{32,16},{48,32},{64,48},{80,64},{96,80},{112,96},{128,112},... | collective-permute-start | bytes 1769480 | tf_op jit(solution)/shard_map/ppermute | solution.py:124
  21.7 88.6 %collective-permute-start.6 = (bf16[2,384,384]{2,1,0:T(8,128)(2,1)}, bf16[2,384,384]{2,1,0:T(8,128)(2,1)S(1)}, u32[]{:S(2)}, u32[]{:S(2)}) collective-permute-start(bf16[2,384,384]{2,1,0:T(8,128)(2,1)} %fusion.5), channel_id=1, source_target_pairs={{32,0},{48,16},{64,32},{80,48},{96,64},{112,80},{128,96},{144,112}... | collective-permute-start | bytes 1769480 | tf_op jit(solution)/shard_map/ppermute | solution.py:124
  24.0 65.1 %copy-start.6 = (s32[5]{0:T(128)S(1)}, s32[5]{0:T(128)}, u32[]{:S(2)}) copy-start(s32[5]{0:T(128)} %constant.126.clone) | copy-start | bytes 64
  24.0 52.1 %collective-permute-start = (f32[2,512]{1,0:T(2,128)S(1)}, f32[2,512]{1,0:T(2,128)S(1)}, u32[]{:S(2)}, u32[]{:S(2)}) collective-permute-start(f32[2,512]{1,0:T(2,128)S(1)} %pad_maximum_fusion.1), channel_id=1, source_target_pairs={{0,2},{2,0},{4,6},{6,4},{8,10},{10,8},{12,14},{14,12},{1,3},{3,1},... | collective-permute-start | bytes 12296 | tf_op jit(solution)/shard_map/ppermute | solution.py:102
  25.6 78.0 %copy-start.5 = (f32[384]{0:T(512)S(1)}, f32[384]{0:T(512)}, u32[]{:S(2)}) copy-start(f32[384]{0:T(512)} %param.10) | copy-start | bytes 4612
  76.1 5.2 %collective-permute-start.1 = (f32[2,512]{1,0:T(2,128)S(1)}, f32[2,512]{1,0:T(2,128)S(1)}, u32[]{:S(2)}, u32[]{:S(2)}) collective-permute-start(f32[2,512]{1,0:T(2,128)S(1)} %fusion.14), channel_id=1, source_target_pairs={{0,4},{2,6},{4,0},{6,2},{8,12},{10,14},{12,8},{14,10},{1,5},{3,7},... | collective-permute-start | bytes 12296 | tf_op jit(solution)/shard_map/ppermute | solution.py:102
  81.3 7.6 %collective-permute-start.2 = (f32[2,512]{1,0:T(2,128)S(1)}, f32[2,512]{1,0:T(2,128)S(1)}, u32[]{:S(2)}, u32[]{:S(2)}) collective-permute-start(f32[2,512]{1,0:T(2,128)S(1)} %fusion.20), channel_id=1, source_target_pairs={{0,8},{2,10},{4,12},{6,14},{8,0},{10,2},{12,4},{14,6},{1,9},{3,11}... | collective-permute-start | bytes 12296 | tf_op jit(solution)/shard_map/ppermute | solution.py:102
  88.9 3.7 %collective-permute-start.7 = (f32[1,512]{1,0:T(1,128)S(1)}, f32[1,512]{1,0:T(1,128)S(1)}, u32[]{:S(2)}, u32[]{:S(2)}) collective-permute-start(f32[1,512]{1,0:T(1,128)S(1)} %get-tuple-element.13), channel_id=1, source_target_pairs={{0,16},{16,0},{32,48},{48,32},{64,80},{80,64},{96,112},{112,96},{1... | collective-permute-start | bytes 6152 | tf_op jit(solution)/shard_map/ppermute | solution.py:89
  92.6 5.2 %collective-permute-start.8 = (f32[2,512]{1,0:T(2,128)S(1)}, f32[2,512]{1,0:T(2,128)S(1)}, u32[]{:S(2)}, u32[]{:S(2)}) collective-permute-start(f32[2,512]{1,0:T(2,128)S(1)} %maximum_select_fusion.3), channel_id=1, source_target_pairs={{0,32},{16,48},{32,0},{48,16},{64,96},{80,112},{96,64},{112,80},{1... | collective-permute-start | bytes 12296 | tf_op jit(solution)/shard_map/ppermute | solution.py:89
  97.8 4.0 %collective-permute-start.9 = (f32[4,512]{1,0:T(4,128)S(1)}, f32[4,512]{1,0:T(4,128)S(1)}, u32[]{:S(2)}, u32[]{:S(2)}) collective-permute-start(f32[4,512]{1,0:T(4,128)S(1)} %maximum_select_fusion.2), channel_id=1, source_target_pairs={{0,64},{16,80},{32,96},{48,112},{64,0},{80,16},{96,32},{112,48},{1... | collective-permute-start | bytes 24584 | tf_op jit(solution)/shard_map/ppermute | solution.py:89
  101.9 5.2 %collective-permute-start.10 = (f32[8,512]{1,0:T(8,128)S(1)}, f32[8,512]{1,0:T(8,128)S(1)}, u32[]{:S(2)}, u32[]{:S(2)}) collective-permute-start(f32[8,512]{1,0:T(8,128)S(1)} %maximum_select_fusion.1), channel_id=1, source_target_pairs={{0,128},{16,144},{32,160},{48,176},{64,192},{80,208},{96,224},{112... | collective-permute-start | bytes 49160 | tf_op jit(solution)/shard_map/ppermute | solution.py:89
  110.3 0.7 copy-start.4
Sparse Core Ops, SparseCore 0:
  76.0 68.0 all-gather.3

commit v8 on v5

--- a/solution.py
+++ b/solution.py
@@ -14,24 +14,28 @@
 NEAR = 2
 
 EPS = 1e-06
+LOG2E = 1.4426950408889634
 
 
 def attn_kernel(sel_ref, q_ref, kn_ref, vn_ref, kf_ref, vf_ref, o_ref, kc_ref, vc_ref, *, q_blocks, slots):
     scale = 1.0 / math.sqrt(HD)
+    cols = pl.ds(pl.multiple_of(pl.program_id(0) * HD, HD), HD)
     for b in range(q_blocks):
         for j in range(slots):
             use_near = sel_ref[0, b, j] == 1
             rows = pl.ds(j * BLK, BLK)
-            kc_ref[rows, :] = jnp.where(use_near, kn_ref[sel_ref[1, b, j]], kf_ref[sel_ref[2, b, j]])
+            kc_ref[rows, :] = jnp.where(
+                use_near, kn_ref[sel_ref[1, b, j], :, cols], kf_ref[sel_ref[2, b, j]]
+            )
             vc_ref[rows, :] = jnp.where(
-                use_near, vn_ref[sel_ref[1, b, j]], vf_ref[0, sel_ref[2, b, j]]
+                use_near, vn_ref[sel_ref[1, b, j], :, cols], vf_ref[0, sel_ref[2, b, j]]
             )
         qh = q_ref[pl.ds(b * BLK, BLK), :]
         s = lax.dot_general(
             kc_ref[...], qh, (((1,), (1,)), ((), ())), preferred_element_type=jnp.float32
         ) * scale
         top = jnp.max(s, axis=0, keepdims=True)
-        w = jnp.exp(s - top)
+        w = jnp.exp2((s - top) * LOG2E)
         total = jnp.sum(w, axis=0, keepdims=True)
         acc = lax.dot_general(
             w.astype(jnp.bfloat16), vc_ref[...], (((0,), (0,)), ((), ())),
@@ -54,8 +58,8 @@
         grid=(heads,),
         in_specs=[
             pl.BlockSpec((tok_rows, HD), lambda h, sel_ref: (0, h)),
-            pl.BlockSpec((n_near, BLK, HD), lambda h, sel_ref: (0, 0, h)),
-            pl.BlockSpec((n_near, BLK, HD), lambda h, sel_ref: (0, 0, h)),
+            pl.BlockSpec(memory_space=pltpu.VMEM),
+            pl.BlockSpec(memory_space=pltpu.VMEM),
             pl.BlockSpec((n_first, BLK, HD), lambda h, sel_ref: (0, 0, h)),
             pl.BlockSpec((1, n_first, BLK, HD), lambda h, sel_ref: (1, 0, 0, h)),
         ],

time: 140 us -> 140 us (level)
  no operation moved by 1% of the time
where the time goes in v8:
time: 140 us
  starting transfers between devices  59.5 us (42%)
  waiting for transfers between devices  43.8 us (31%)
  between operations  13.8 us (10%)
  Pallas kernels  10.9 us (8%)
  local copies, waits for them, and re-layouts  6.47 us (5%)
  other arithmetic  5.17 us (4%)
    ppermute x4, starting transfers between devices, xor_gather(): got = lax.ppermute(held, 'frame', perm)  34.5 us
    ppermute x4, waiting for transfers between devices, xor_gather(): got = lax.ppermute(held, 'frame', perm)  30.6 us
    ppermute x4, starting transfers between devices, body(): near[d] = lax.ppermute(tail, 'frame', perms[d])  13.5 us
    ppermute x3, starting transfers between devices, xor_sum(): x = x + lax.ppermute(x, axis, perm)  11.5 us
    pallas_call x1, Pallas kernels, sparse_attend(): pl.pallas_call(kernel, grid_spec=grid_spec, out_shape=jax.ShapeDtypeStruc...  10.9 us
    all_gather x1, waiting for transfers between devices, body(): first = lax.all_gather(kv_raw[:, :BLK], 'frame', axis=1, tiled=False)  7.15 us
    ppermute x3, waiting for transfers between devices, xor_sum(): x = x + lax.ppermute(x, axis, perm)  6.01 us
    another operation x2, other arithmetic, body(): kv_raw = jnp.stack([k_proj, v_proj])  3.7 us
  transfers between devices with their start and end apart: 12, of which 8 were waited for; matrix products, arithmetic and copies ran while one was open for 5% of the time, Pallas kernels for 0%

profile of v8, /device:TPU:2, one launch (start us, length us, event | category | flops | bytes accessed | tf_op | source)
XLA Modules:
  0.0 139.7 jit_solution(504850326511513362)
XLA Ops:
  6.5 1.7 %pad_maximum_fusion = bf16[2,128,384]{2,1,0:T(8,128)(2,1)} fusion(bf16[1,512,384]{2,1,0:T(8,128)(2,1)} %bitcast.29, bf16[1,512,384]{2,1,0:T(8,128)(2,1)} %bitcast.26), kind=kLoop, calls=%fused_computation.14 | loop fusion | flops 393216 | bytes 983040 | tf_op jit(solution)/shard_map/stack | solution.py:119
  8.3 2.0 %fusion.5 = bf16[2,384,384]{2,1,0:T(8,128)(2,1)} fusion(bf16[1,512,384]{2,1,0:T(8,128)(2,1)} %bitcast.27, bf16[1,512,384]{2,1,0:T(8,128)(2,1)} %bitcast.30), kind=kLoop, calls=%fused_computation.13 | loop fusion | flops 294912 | bytes 1376256 | tf_op jit(solution)/shard_map/stack | solution.py:119
  10.3 1.4 %collective-permute-start.6 = (bf16[2,384,384]{2,1,0:T(8,128)(2,1)}, bf16[2,384,384]{2,1,0:T(8,128)(2,1)}, u32[]{:S(2)}, u32[]{:S(2)}) collective-permute-start(bf16[2,384,384]{2,1,0:T(8,128)(2,1)} %fusion.5), channel_id=1, source_target_pairs={{32,0},{48,16},{64,32},{80,48},{96,64},{112,80},{128,96},{144,112}... | collective-permute-start | bytes 1769480 | tf_op jit(solution)/shard_map/ppermute | solution.py:124
  11.7 1.3 collective-permute-start.5
  13.0 5.4 %collective-permute-start.4 = (bf16[2,384,384]{2,1,0:T(8,128)(2,1)}, bf16[2,384,384]{2,1,0:T(8,128)(2,1)}, u32[]{:S(2)}, u32[]{:S(2)}) collective-permute-start(bf16[2,384,384]{2,1,0:T(8,128)(2,1)} %fusion.5), channel_id=1, source_target_pairs={{0,16},{16,32},{32,48},{48,64},{64,80},{80,96},{96,112},{112,128},... | collective-permute-start | bytes 1769480 | tf_op jit(solution)/shard_map/ppermute | solution.py:124
  18.4 5.4 %collective-permute-start.3 = (bf16[2,384,384]{2,1,0:T(8,128)(2,1)}, bf16[2,384,384]{2,1,0:T(8,128)(2,1)S(1)}, u32[]{:S(2)}, u32[]{:S(2)}) collective-permute-start(bf16[2,384,384]{2,1,0:T(8,128)(2,1)} %fusion.5), channel_id=1, source_target_pairs={{0,32},{16,48},{32,64},{48,80},{64,96},{80,112},{96,128},{112,144}... | collective-permute-start | bytes 1769480 | tf_op jit(solution)/shard_map/ppermute | solution.py:124
  23.8 0.2 multiply_reduce_fusion
  24.0 0.2 fusion.2
  24.2 2.2 %collective-permute-start = (f32[2,512]{1,0:T(2,128)S(1)}, f32[2,512]{1,0:T(2,128)S(1)}, u32[]{:S(2)}, u32[]{:S(2)}) collective-permute-start(f32[2,512]{1,0:T(2,128)S(1)} %pad_maximum_fusion.1), channel_id=1, source_target_pairs={{0,2},{2,0},{4,6},{6,4},{8,10},{10,8},{12,14},{14,12},{1,3},{3,1},... | collective-permute-start | bytes 12296 | tf_op jit(solution)/shard_map/ppermute | solution.py:104
  26.4 0.1 copy.12
  26.5 1.4 %collective-permute-done = f32[2,512]{1,0:T(2,128)S(1)} collective-permute-done((f32[2,512]{1,0:T(2,128)S(1)}, f32[2,512]{1,0:T(2,128)S(1)}, u32[]{:S(2)}, u32[]{:S(2)}) %collective-permute-start) | collective-permute-done | bytes 4128 | tf_op jit(solution)/shard_map/ppermute | solution.py:104
  27.9 2.2 %collective-permute-start.1 = (f32[2,512]{1,0:T(2,128)S(1)}, f32[2,512]{1,0:T(2,128)S(1)}, u32[]{:S(2)}, u32[]{:S(2)}) collective-permute-start(f32[2,512]{1,0:T(2,128)S(1)} %fusion.14), channel_id=1, source_target_pairs={{0,4},{2,6},{4,0},{6,2},{8,12},{10,14},{12,8},{14,10},{1,5},{3,7},... | collective-permute-start | bytes 12296 | tf_op jit(solution)/shard_map/ppermute | solution.py:104
  30.1 3.0 %collective-permute-done.1 = f32[2,512]{1,0:T(2,128)S(1)} collective-permute-done((f32[2,512]{1,0:T(2,128)S(1)}, f32[2,512]{1,0:T(2,128)S(1)}, u32[]{:S(2)}, u32[]{:S(2)}) %collective-permute-start.1) | collective-permute-done | bytes 4128 | tf_op jit(solution)/shard_map/ppermute | solution.py:104
  33.1 7.2 %collective-permute-start.2 = (f32[2,512]{1,0:T(2,128)S(1)}, f32[2,512]{1,0:T(2,128)S(1)}, u32[]{:S(2)}, u32[]{:S(2)}) collective-permute-start(f32[2,512]{1,0:T(2,128)S(1)} %fusion.20), channel_id=1, source_target_pairs={{0,8},{2,10},{4,12},{6,14},{8,0},{10,2},{12,4},{14,6},{1,9},{3,11}... | collective-permute-start | bytes 12296 | tf_op jit(solution)/shard_map/ppermute | solution.py:104
  40.4 1.6 %collective-permute-done.2 = f32[2,512]{1,0:T(2,128)S(1)} collective-permute-done((f32[2,512]{1,0:T(2,128)S(1)}, f32[2,512]{1,0:T(2,128)S(1)}, u32[]{:S(2)}, u32[]{:S(2)}) %collective-permute-start.2) | collective-permute-done | bytes 4128 | tf_op jit(solution)/shard_map/ppermute | solution.py:104
  42.0 3.6 %collective-permute-start.7 = (f32[1,512]{1,0:T(1,128)S(1)}, f32[1,512]{1,0:T(1,128)S(1)}, u32[]{:S(2)}, u32[]{:S(2)}) collective-permute-start(f32[1,512]{1,0:T(1,128)S(1)} %get-tuple-element.13), channel_id=1, source_target_pairs={{0,16},{16,0},{32,48},{48,32},{64,80},{80,64},{96,112},{112,96},{1... | collective-permute-start | bytes 6152 | tf_op jit(solution)/shard_map/ppermute | solution.py:91
  45.6 21.0 %collective-permute-done.7 = f32[1,512]{1,0:T(1,128)S(1)} collective-permute-done((f32[1,512]{1,0:T(1,128)S(1)}, f32[1,512]{1,0:T(1,128)S(1)}, u32[]{:S(2)}, u32[]{:S(2)}) %collective-permute-start.7) | collective-permute-done | bytes 2080 | tf_op jit(solution)/shard_map/ppermute | solution.py:91
  66.6 30.7 %collective-permute-start.8 = (f32[2,512]{1,0:T(2,128)S(1)}, f32[2,512]{1,0:T(2,128)S(1)}, u32[]{:S(2)}, u32[]{:S(2)}) collective-permute-start(f32[2,512]{1,0:T(2,128)S(1)} %maximum_select_fusion.3), channel_id=1, source_target_pairs={{0,32},{16,48},{32,0},{48,16},{64,96},{80,112},{96,64},{112,80},{1... | collective-permute-start | bytes 12296 | tf_op jit(solution)/shard_map/ppermute | solution.py:91
  97.3 1.6 %collective-permute-done.8 = f32[2,512]{1,0:T(2,128)S(1)} collective-permute-done((f32[2,512]{1,0:T(2,128)S(1)}, f32[2,512]{1,0:T(2,128)S(1)}, u32[]{:S(2)}, u32[]{:S(2)}) %collective-permute-start.8) | collective-permute-done | bytes 4128 | tf_op jit(solution)/shard_map/ppermute | solution.py:91
  99.1 3.5 %collective-permute-done.9 = f32[4,512]{1,0:T(4,128)S(1)} collective-permute-done((f32[4,512]{1,0:T(4,128)S(1)}, f32[4,512]{1,0:T(4,128)S(1)}, u32[]{:S(2)}, u32[]{:S(2)}) %collective-permute-start.9) | collective-permute-done | bytes 8224 | tf_op jit(solution)/shard_map/ppermute | solution.py:91
  102.7 0.2 fusion.4.q_ref
  102.9 4.5 %collective-permute-done.10 = f32[8,512]{1,0:T(8,128)S(1)} collective-permute-done((f32[8,512]{1,0:T(8,128)S(1)}, f32[8,512]{1,0:T(8,128)S(1)}, u32[]{:S(2)}, u32[]{:S(2)}) %collective-permute-start.10) | collective-permute-done | bytes 16416 | tf_op jit(solution)/shard_map/ppermute | solution.py:91
  107.5 0.6 gather_fusion
  108.2 1.1 fusion.17
  109.5 1.1 fusion.16
  110.7 1.1 fusion.15
  112.1 0.4 copy-done.4
  112.5 0.4 multiply_convert_fusion.kn_ref
  112.9 7.2 %all-gather.3.cloned.1.call-done = bf16[2,2048,384]{2,1,0:T(8,128)(2,1)} async-done(((bf16[2,128,384]{2,1,0:T(8,128)(2,1)}), bf16[2,2048,384]{2,1,0:T(8,128)(2,1)}) %all-gather.3.cloned.1.call-update) | async-done | bytes 3145744 | tf_op jit(solution)/shard_map/all_gather | solution.py:120
  120.0 1.4 %slice-done = bf16[1,2048,384]{2,1,0:T(8,128)(2,1)S(1)} async-done(((bf16[2,2048,384]{2,1,0:T(8,128)(2,1)}), bf16[1,2048,384]{2,1,0:T(8,128)(2,1)S(1)}, s32[]{:S(2)}) %slice-start) | async-done | bytes 1572888 | tf_op jit(solution)/shard_map/slice | solution.py:149
  121.5 0.4 fusion.1.kf_ref
  121.9 10.9 %shard_map.73 = bf16[512,384]{1,0:T(8,128)(2,1)} custom-call(s32[3,4,12]{2,1,0:T(4,128)S(1)} %pad_add_fusion.sel_ref, bf16[512,384]{1,0:T(8,128)(2,1)S(1)} %fusion.4.q_ref, bf16[15,128,384]{2,1,0:T(8,128)(2,1)S(1)} %multiply_convert_fusion.kn_ref, bf16[15,128,384]{2,1,0:T(8,128)(2,1)S(1)} %constant_dynamic-update-slice_fusion.5.vn_ref, ...), custom_call_target="tpu_custom_call" | custom-call | flops 1207959552 | bytes 6881280 | tf_op jit(solution)/shard_map/pallas_call | solution.py:73
  (53 shorter events, 1.0 us)
Async XLA Ops:
  6.5 19.8 %copy-start = (s32[64,12]{0,1:T(8,128)S(1)}, s32[64,12]{0,1:T(8,128)}, u32[]{:S(2)}) copy-start(s32[64,12]{0,1:T(8,128)} %param.12) | copy-start | bytes 9220
  6.5 17.3 %copy-start.1 = (bf16[512,384]{1,0:T(8,128)(2,1)S(1)}, bf16[512,384]{1,0:T(8,128)(2,1)}, u32[]{:S(2)}) copy-start(bf16[512,384]{1,0:T(8,128)(2,1)} %param.8) | copy-start | bytes 1179652
  6.5 113.5 %all-gather.3.cloned.1.call-start = ((), (), s32[]{:S(2)}) async-start(), calls=%async_computation | async-start | bytes 3342336 | tf_op jit(solution)/shard_map/all_gather | solution.py:120
  6.5 17.4 %copy-start.3 = (bf16[512,384]{1,0:T(8,128)(2,1)S(1)}, bf16[512,384]{1,0:T(8,128)(2,1)}, u32[]{:S(2)}) copy-start(bf16[512,384]{1,0:T(8,128)(2,1)} %param.7) | copy-start | bytes 1179652
  8.3 37.3 %copy-start.6 = (s32[5]{0:T(128)S(1)}, s32[5]{0:T(128)}, u32[]{:S(2)}) copy-start(s32[5]{0:T(128)} %constant.121.clone) | copy-start | bytes 64
  8.3 90.8 %copy-start.2 = (bf16[512,384]{1,0:T(8,128)(2,1)S(1)}, bf16[512,384]{1,0:T(8,128)(2,1)}, u32[]{:S(2)}) copy-start(bf16[512,384]{1,0:T(8,128)(2,1)} %param.9) | copy-start | bytes 1179652
  10.3 92.5 %copy-start.5 = (f32[384]{0:T(512)S(1)}, f32[384]{0:T(512)}, u32[]{:S(2)}) copy-start(f32[384]{0:T(512)} %param.10) | copy-start | bytes 4612
  10.3 100.4 %collective-permute-start.6 = (bf16[2,384,384]{2,1,0:T(8,128)(2,1)}, bf16[2,384,384]{2,1,0:T(8,128)(2,1)}, u32[]{:S(2)}, u32[]{:S(2)}) collective-permute-start(bf16[2,384,384]{2,1,0:T(8,128)(2,1)} %fusion.5), channel_id=1, source_target_pairs={{32,0},{48,16},{64,32},{80,48},{96,64},{112,80},{128,96},{144,112}... | collective-permute-start | bytes 1769480 | tf_op jit(solution)/shard_map/ppermute | solution.py:124
  11.7 97.8 %collective-permute-start.5 = (bf16[2,384,384]{2,1,0:T(8,128)(2,1)}, bf16[2,384,384]{2,1,0:T(8,128)(2,1)}, u32[]{:S(2)}, u32[]{:S(2)}) collective-permute-start(bf16[2,384,384]{2,1,0:T(8,128)(2,1)} %fusion.5), channel_id=1, source_target_pairs={{16,0},{32,16},{48,32},{64,48},{80,64},{96,80},{112,96},{128,112},... | collective-permute-start | bytes 1769480 | tf_op jit(solution)/shard_map/ppermute | solution.py:124
  13.0 95.2 %collective-permute-start.4 = (bf16[2,384,384]{2,1,0:T(8,128)(2,1)}, bf16[2,384,384]{2,1,0:T(8,128)(2,1)}, u32[]{:S(2)}, u32[]{:S(2)}) collective-permute-start(bf16[2,384,384]{2,1,0:T(8,128)(2,1)} %fusion.5), channel_id=1, source_target_pairs={{0,16},{16,32},{32,48},{48,64},{64,80},{80,96},{96,112},{112,128},... | collective-permute-start | bytes 1769480 | tf_op jit(solution)/shard_map/ppermute | solution.py:124
  18.4 89.7 %collective-permute-start.3 = (bf16[2,384,384]{2,1,0:T(8,128)(2,1)}, bf16[2,384,384]{2,1,0:T(8,128)(2,1)S(1)}, u32[]{:S(2)}, u32[]{:S(2)}) collective-permute-start(bf16[2,384,384]{2,1,0:T(8,128)(2,1)} %fusion.5), channel_id=1, source_target_pairs={{0,32},{16,48},{32,64},{48,80},{64,96},{80,112},{96,128},{112,144}... | collective-permute-start | bytes 1769480 | tf_op jit(solution)/shard_map/ppermute | solution.py:124
  24.2 3.7 %collective-permute-start = (f32[2,512]{1,0:T(2,128)S(1)}, f32[2,512]{1,0:T(2,128)S(1)}, u32[]{:S(2)}, u32[]{:S(2)}) collective-permute-start(f32[2,512]{1,0:T(2,128)S(1)} %pad_maximum_fusion.1), channel_id=1, source_target_pairs={{0,2},{2,0},{4,6},{6,4},{8,10},{10,8},{12,14},{14,12},{1,3},{3,1},... | collective-permute-start | bytes 12296 | tf_op jit(solution)/shard_map/ppermute | solution.py:104
  27.9 5.2 %collective-permute-start.1 = (f32[2,512]{1,0:T(2,128)S(1)}, f32[2,512]{1,0:T(2,128)S(1)}, u32[]{:S(2)}, u32[]{:S(2)}) collective-permute-start(f32[2,512]{1,0:T(2,128)S(1)} %fusion.14), channel_id=1, source_target_pairs={{0,4},{2,6},{4,0},{6,2},{8,12},{10,14},{12,8},{14,10},{1,5},{3,7},... | collective-permute-start | bytes 12296 | tf_op jit(solution)/shard_map/ppermute | solution.py:104
  33.1 8.8 %collective-permute-start.2 = (f32[2,512]{1,0:T(2,128)S(1)}, f32[2,512]{1,0:T(2,128)S(1)}, u32[]{:S(2)}, u32[]{:S(2)}) collective-permute-start(f32[2,512]{1,0:T(2,128)S(1)} %fusion.20), channel_id=1, source_target_pairs={{0,8},{2,10},{4,12},{6,14},{8,0},{10,2},{12,4},{14,6},{1,9},{3,11}... | collective-permute-start | bytes 12296 | tf_op jit(solution)/shard_map/ppermute | solution.py:104
  42.0 24.6 %collective-permute-start.7 = (f32[1,512]{1,0:T(1,128)S(1)}, f32[1,512]{1,0:T(1,128)S(1)}, u32[]{:S(2)}, u32[]{:S(2)}) collective-permute-start(f32[1,512]{1,0:T(1,128)S(1)} %get-tuple-element.13), channel_id=1, source_target_pairs={{0,16},{16,0},{32,48},{48,32},{64,80},{80,64},{96,112},{112,96},{1... | collective-permute-start | bytes 6152 | tf_op jit(solution)/shard_map/ppermute | solution.py:91
  66.6 32.3 %collective-permute-start.8 = (f32[2,512]{1,0:T(2,128)S(1)}, f32[2,512]{1,0:T(2,128)S(1)}, u32[]{:S(2)}, u32[]{:S(2)}) collective-permute-start(f32[2,512]{1,0:T(2,128)S(1)} %maximum_select_fusion.3), channel_id=1, source_target_pairs={{0,32},{16,48},{32,0},{48,16},{64,96},{80,112},{96,64},{112,80},{1... | collective-permute-start | bytes 12296 | tf_op jit(solution)/shard_map/ppermute | solution.py:91
  98.9 3.8 %collective-permute-start.9 = (f32[4,512]{1,0:T(4,128)S(1)}, f32[4,512]{1,0:T(4,128)S(1)}, u32[]{:S(2)}, u32[]{:S(2)}) collective-permute-start(f32[4,512]{1,0:T(4,128)S(1)} %maximum_select_fusion.2), channel_id=1, source_target_pairs={{0,64},{16,80},{32,96},{48,112},{64,0},{80,16},{96,32},{112,48},{1... | collective-permute-start | bytes 24584 | tf_op jit(solution)/shard_map/ppermute | solution.py:91
  102.6 4.8 %collective-permute-start.10 = (f32[8,512]{1,0:T(8,128)S(1)}, f32[8,512]{1,0:T(8,128)S(1)}, u32[]{:S(2)}, u32[]{:S(2)}) collective-permute-start(f32[8,512]{1,0:T(8,128)S(1)} %maximum_select_fusion.1), channel_id=1, source_target_pairs={{0,128},{16,144},{32,160},{48,176},{64,192},{80,208},{96,224},{112... | collective-permute-start | bytes 49160 | tf_op jit(solution)/shard_map/ppermute | solution.py:91
  111.8 0.7 copy-start.4
  120.0 1.4 %slice-start = ((bf16[2,2048,384]{2,1,0:T(8,128)(2,1)}), bf16[1,2048,384]{2,1,0:T(8,128)(2,1)S(1)}, s32[]{:S(2)}) async-start(bf16[2,2048,384]{2,1,0:T(8,128)(2,1)} %all-gather.3.cloned.1.call-done), calls=%async_computation.1 | async-start | bytes 3145728 | tf_op jit(solution)/shard_map/slice | solution.py:149
Sparse Core Ops, SparseCore 0:
  9.1 110.8 all-gather.2

commit v9 on v8

--- a/solution.py
+++ b/solution.py
@@ -14,7 +14,6 @@
 NEAR = 2
 
 EPS = 1e-06
-LOG2E = 1.4426950408889634
 
 
 def attn_kernel(sel_ref, q_ref, kn_ref, vn_ref, kf_ref, vf_ref, o_ref, kc_ref, vc_ref, *, q_blocks, slots):
@@ -28,14 +27,14 @@
                 use_near, kn_ref[sel_ref[1, b, j], :, cols], kf_ref[sel_ref[2, b, j]]
             )
             vc_ref[rows, :] = jnp.where(
-                use_near, vn_ref[sel_ref[1, b, j], :, cols], vf_ref[0, sel_ref[2, b, j]]
+                use_near, vn_ref[sel_ref[1, b, j], :, cols], vf_ref[sel_ref[2, b, j], 0]
             )
         qh = q_ref[pl.ds(b * BLK, BLK), :]
         s = lax.dot_general(
             kc_ref[...], qh, (((1,), (1,)), ((), ())), preferred_element_type=jnp.float32
         ) * scale
         top = jnp.max(s, axis=0, keepdims=True)
-        w = jnp.exp2((s - top) * LOG2E)
+        w = jnp.exp(s - top)
         total = jnp.sum(w, axis=0, keepdims=True)
         acc = lax.dot_general(
             w.astype(jnp.bfloat16), vc_ref[...], (((0,), (0,)), ((), ())),
@@ -61,7 +60,7 @@
             pl.BlockSpec(memory_space=pltpu.VMEM),
             pl.BlockSpec(memory_space=pltpu.VMEM),
             pl.BlockSpec((n_first, BLK, HD), lambda h, sel_ref: (0, 0, h)),
-            pl.BlockSpec((1, n_first, BLK, HD), lambda h, sel_ref: (1, 0, 0, h)),
+            pl.BlockSpec((n_first, 1, BLK, HD), lambda h, sel_ref: (0, 1, 0, h)),
         ],
         out_specs=pl.BlockSpec((tok_rows, HD), lambda h, sel_ref: (0, h)),
         scratch_shapes=[
@@ -116,9 +115,10 @@
         d: [(i, i - d) for i in range(n_frame) if 0 <= i - d < n_frame] for d in offsets if d != 0
     }
 
-    kv_raw = jnp.stack([k_proj, v_proj])
-    first = lax.all_gather(kv_raw[:, :BLK], "frame", axis=1, tiled=False)
-    tail = kv_raw[:, BLK:]
+    kv_first = jnp.concatenate([k_proj[:BLK], v_proj[:BLK]], axis=0)
+    first = lax.all_gather(kv_first, "frame", axis=0, tiled=False)
+    first = first.reshape(n_frame, 2, BLK, width)
+    tail = jnp.stack([k_proj[BLK:], v_proj[BLK:]])
     near = {0: tail}
     for d in perms:
         near[d] = lax.ppermute(tail, "frame", perms[d])
@@ -146,7 +146,7 @@
     v_near = jnp.concatenate(
         [near[d][1].reshape(blocks - 1, BLK, width) for d in offsets], axis=0
     )
-    kn_first = (first[0].astype(jnp.float32) * first_scale * gain_k).astype(jnp.bfloat16)
+    kn_first = (first[:, 0].astype(jnp.float32) * first_scale * gain_k).astype(jnp.bfloat16)
 
     q_tiles = lax.dynamic_slice_in_dim(tiles, frame_pos * blocks, blocks, 0)
     key_slab = q_tiles // blocks

time: 140 us -> 137 us (0.979)
  the two profiles are of different devices: /device:TPU:2 before, /device:TPU:64 now
where the time goes in v9:
time: 137 us; the launch traced here: 134 us
  waiting for transfers between devices  55.5 us (41%)
  starting transfers between devices  42.7 us (31%)
  between operations  13.8 us (10%)
  Pallas kernels  10.8 us (8%)
  local copies, waits for them, and re-layouts  7.98 us (6%)
  other arithmetic  3.65 us (3%)
    ppermute x4, waiting for transfers between devices, xor_gather(): got = lax.ppermute(held, 'frame', perm)  49.3 us
    ppermute x4, starting transfers between devices, xor_gather(): got = lax.ppermute(held, 'frame', perm)  17.5 us
    ppermute x4, starting transfers between devices, body(): near[d] = lax.ppermute(tail, 'frame', perms[d])  15 us
    pallas_call x1, Pallas kernels, sparse_attend(): pl.pallas_call(kernel, grid_spec=grid_spec, out_shape=jax.ShapeDtypeStruc...  10.8 us
    ppermute x3, starting transfers between devices, xor_sum(): x = x + lax.ppermute(x, axis, perm)  10.2 us
    ppermute x3, waiting for transfers between devices, xor_sum(): x = x + lax.ppermute(x, axis, perm)  6.12 us
    slice x4, local copies, waits for them, and re-layouts, body(): near[d][1].reshape(blocks - 1, BLK, width)  3.4 us
  transfers between devices with their start and end apart: 12, of which 7 were waited for; matrix products, arithmetic and copies ran while one was open for 5% of the time, Pallas kernels for 0%

profile of v9, /device:TPU:64, one launch (start us, length us, event | category | flops | bytes accessed | tf_op | source)
XLA Modules:
  0.0 134.3 jit_solution(2063260114705806768)
XLA Ops:
  6.5 1.0 slice.65
  7.5 0.9 slice.64
  8.4 0.7 pad_maximum_fusion.1
  9.1 1.1 fusion.18
  10.4 5.1 %collective-permute-start.3 = (bf16[2,384,384]{2,1,0:T(8,128)(2,1)S(1)}, bf16[2,384,384]{2,1,0:T(8,128)(2,1)S(1)}, u32[]{:S(2)}, u32[]{:S(2)}) collective-permute-start(bf16[2,384,384]{2,1,0:T(8,128)(2,1)S(1)} %pad_maximum_fusion), channel_id=1, source_target_pairs={{0,32},{16,48},{32,64},{48,80},{64,96},{80,112},{96,128},{112,144}... | collective-permute-start | bytes 1769480 | tf_op jit(solution)/shard_map/ppermute | solution.py:124
  15.5 2.6 %collective-permute-start.4 = (bf16[2,384,384]{2,1,0:T(8,128)(2,1)S(1)}, bf16[2,384,384]{2,1,0:T(8,128)(2,1)}, u32[]{:S(2)}, u32[]{:S(2)}) collective-permute-start(bf16[2,384,384]{2,1,0:T(8,128)(2,1)S(1)} %pad_maximum_fusion), channel_id=1, source_target_pairs={{0,16},{16,32},{32,48},{48,64},{64,80},{80,96},{96,112},{112,128},... | collective-permute-start | bytes 1769480 | tf_op jit(solution)/shard_map/ppermute | solution.py:124
  18.1 5.4 %collective-permute-start.5 = (bf16[2,384,384]{2,1,0:T(8,128)(2,1)S(1)}, bf16[2,384,384]{2,1,0:T(8,128)(2,1)}, u32[]{:S(2)}, u32[]{:S(2)}) collective-permute-start(bf16[2,384,384]{2,1,0:T(8,128)(2,1)S(1)} %pad_maximum_fusion), channel_id=1, source_target_pairs={{16,0},{32,16},{48,32},{64,48},{80,64},{96,80},{112,96},{128,112},... | collective-permute-start | bytes 1769480 | tf_op jit(solution)/shard_map/ppermute | solution.py:124
  23.5 1.9 %collective-permute-start.6 = (bf16[2,384,384]{2,1,0:T(8,128)(2,1)S(1)}, bf16[2,384,384]{2,1,0:T(8,128)(2,1)}, u32[]{:S(2)}, u32[]{:S(2)}) collective-permute-start(bf16[2,384,384]{2,1,0:T(8,128)(2,1)S(1)} %pad_maximum_fusion), channel_id=1, source_target_pairs={{32,0},{48,16},{64,32},{80,48},{96,64},{112,80},{128,96},{144,112}... | collective-permute-start | bytes 1769480 | tf_op jit(solution)/shard_map/ppermute | solution.py:124
  25.4 0.2 multiply_reduce_fusion
  25.6 0.2 fusion.2
  25.7 1.6 %collective-permute-start = (f32[2,512]{1,0:T(2,128)S(1)}, f32[2,512]{1,0:T(2,128)S(1)}, u32[]{:S(2)}, u32[]{:S(2)}) collective-permute-start(f32[2,512]{1,0:T(2,128)S(1)} %pad_maximum_fusion.2), channel_id=1, source_target_pairs={{0,2},{2,0},{4,6},{6,4},{8,10},{10,8},{12,14},{14,12},{1,3},{3,1},... | collective-permute-start | bytes 12296 | tf_op jit(solution)/shard_map/ppermute | solution.py:103
  27.4 0.1 copy.12
  27.5 1.9 %collective-permute-done = f32[2,512]{1,0:T(2,128)S(1)} collective-permute-done((f32[2,512]{1,0:T(2,128)S(1)}, f32[2,512]{1,0:T(2,128)S(1)}, u32[]{:S(2)}, u32[]{:S(2)}) %collective-permute-start) | collective-permute-done | bytes 4128 | tf_op jit(solution)/shard_map/ppermute | solution.py:103
  29.4 3.1 %collective-permute-start.1 = (f32[2,512]{1,0:T(2,128)S(1)}, f32[2,512]{1,0:T(2,128)S(1)}, u32[]{:S(2)}, u32[]{:S(2)}) collective-permute-start(f32[2,512]{1,0:T(2,128)S(1)} %fusion.13), channel_id=1, source_target_pairs={{0,4},{2,6},{4,0},{6,2},{8,12},{10,14},{12,8},{14,10},{1,5},{3,7},... | collective-permute-start | bytes 12296 | tf_op jit(solution)/shard_map/ppermute | solution.py:103
  32.6 2.1 %collective-permute-done.1 = f32[2,512]{1,0:T(2,128)S(1)} collective-permute-done((f32[2,512]{1,0:T(2,128)S(1)}, f32[2,512]{1,0:T(2,128)S(1)}, u32[]{:S(2)}, u32[]{:S(2)}) %collective-permute-start.1) | collective-permute-done | bytes 4128 | tf_op jit(solution)/shard_map/ppermute | solution.py:103
  34.6 5.5 %collective-permute-start.2 = (f32[2,512]{1,0:T(2,128)S(1)}, f32[2,512]{1,0:T(2,128)S(1)}, u32[]{:S(2)}, u32[]{:S(2)}) collective-permute-start(f32[2,512]{1,0:T(2,128)S(1)} %fusion.21), channel_id=1, source_target_pairs={{0,8},{2,10},{4,12},{6,14},{8,0},{10,2},{12,4},{14,6},{1,9},{3,11}... | collective-permute-start | bytes 12296 | tf_op jit(solution)/shard_map/ppermute | solution.py:103
  40.1 2.1 %collective-permute-done.2 = f32[2,512]{1,0:T(2,128)S(1)} collective-permute-done((f32[2,512]{1,0:T(2,128)S(1)}, f32[2,512]{1,0:T(2,128)S(1)}, u32[]{:S(2)}, u32[]{:S(2)}) %collective-permute-start.2) | collective-permute-done | bytes 4128 | tf_op jit(solution)/shard_map/ppermute | solution.py:103
  42.3 0.9 collective-permute-start.7
  43.2 38.1 %collective-permute-done.7 = f32[1,512]{1,0:T(1,128)S(1)} collective-permute-done((f32[1,512]{1,0:T(1,128)S(1)}, f32[1,512]{1,0:T(1,128)S(1)}, u32[]{:S(2)}, u32[]{:S(2)}) %collective-permute-start.7) | collective-permute-done | bytes 2080 | tf_op jit(solution)/shard_map/ppermute | solution.py:90
  81.5 5.1 %collective-permute-done.8 = f32[2,512]{1,0:T(2,128)S(1)} collective-permute-done((f32[2,512]{1,0:T(2,128)S(1)}, f32[2,512]{1,0:T(2,128)S(1)}, u32[]{:S(2)}, u32[]{:S(2)}) %collective-permute-start.8) | collective-permute-done | bytes 4128 | tf_op jit(solution)/shard_map/ppermute | solution.py:90
  86.6 16.4 %collective-permute-start.9 = (f32[4,512]{1,0:T(4,128)S(1)}, f32[4,512]{1,0:T(4,128)S(1)}, u32[]{:S(2)}, u32[]{:S(2)}) collective-permute-start(f32[4,512]{1,0:T(4,128)S(1)} %maximum_select_fusion.2), channel_id=1, source_target_pairs={{0,64},{16,80},{32,96},{48,112},{64,0},{80,16},{96,32},{112,48},{1... | collective-permute-start | bytes 24584 | tf_op jit(solution)/shard_map/ppermute | solution.py:90
  103.0 1.6 %collective-permute-done.9 = f32[4,512]{1,0:T(4,128)S(1)} collective-permute-done((f32[4,512]{1,0:T(4,128)S(1)}, f32[4,512]{1,0:T(4,128)S(1)}, u32[]{:S(2)}, u32[]{:S(2)}) %collective-permute-start.9) | collective-permute-done | bytes 8224 | tf_op jit(solution)/shard_map/ppermute | solution.py:90
  104.8 0.2 fusion.4.q_ref
  104.9 4.5 %collective-permute-done.10 = f32[8,512]{1,0:T(8,128)S(1)} collective-permute-done((f32[8,512]{1,0:T(8,128)S(1)}, f32[8,512]{1,0:T(8,128)S(1)}, u32[]{:S(2)}, u32[]{:S(2)}) %collective-permute-start.10) | collective-permute-done | bytes 16416 | tf_op jit(solution)/shard_map/ppermute | solution.py:90
  109.4 0.6 gather_fusion
  110.2 1.1 fusion.16
  111.4 1.1 fusion.15
  112.6 1.1 fusion.14
  114.0 0.4 copy-done.3
  114.4 0.4 multiply_convert_fusion.kn_ref
  114.9 1.9 %fusion.1.kf_ref = bf16[16,128,384]{2,1,0:T(8,128)(2,1)S(1)} fusion(bf16[16,2,128,384]{3,2,1,0:T(8,128)(2,1)} %bitcast.29, f32[384]{0:T(512)S(1)} %copy-done.3, f32[16,128]{1,0:T(8,128)S(1)} %fusion.8), kind=kLoop, calls=%fused_computation.3 | loop fusion | flops 3145728 | bytes 3155456 | tf_op jit(solution)/shard_map/convert_element_type | solution.py:149
  116.7 10.8 %shard_map.73 = bf16[512,384]{1,0:T(8,128)(2,1)} custom-call(s32[3,4,12]{2,1,0:T(4,128)S(1)} %pad_add_fusion.sel_ref, bf16[512,384]{1,0:T(8,128)(2,1)S(1)} %fusion.4.q_ref, bf16[15,128,384]{2,1,0:T(8,128)(2,1)S(1)} %multiply_convert_fusion.kn_ref, bf16[15,128,384]{2,1,0:T(8,128)(2,1)S(1)} %constant_dynamic-update-slice_fusion.5.vn_ref, ...), custom_call_target="tpu_custom_call" | custom-call | flops 1207959552 | bytes 6881280 | tf_op jit(solution)/shard_map/pallas_call | solution.py:72
  (51 shorter events, 1.1 us)
Async XLA Ops:
  6.5 20.8 %copy-start = (s32[64,12]{0,1:T(8,128)S(1)}, s32[64,12]{0,1:T(8,128)}, u32[]{:S(2)}) copy-start(s32[64,12]{0,1:T(8,128)} %param.12) | copy-start | bytes 9220
  6.5 3.7 %copy-start.1 = (bf16[512,384]{1,0:T(8,128)(2,1)S(1)}, bf16[512,384]{1,0:T(8,128)(2,1)}, u32[]{:S(2)}) copy-start(bf16[512,384]{1,0:T(8,128)(2,1)} %param.8) | copy-start | bytes 1179652
  6.5 108.3 %all-gather.3.cloned.1.call-start = ((), (), s32[]{:S(2)}) async-start(), calls=%async_computation | async-start | bytes 3342336 | tf_op jit(solution)/shard_map/all_gather | solution.py:119
  9.1 16.4 %copy-start.2 = (bf16[512,384]{1,0:T(8,128)(2,1)S(1)}, bf16[512,384]{1,0:T(8,128)(2,1)}, u32[]{:S(2)}) copy-start(bf16[512,384]{1,0:T(8,128)(2,1)} %param.7) | copy-start | bytes 1179652
  10.2 33.0 %copy-start.5 = (s32[5]{0:T(128)S(1)}, s32[5]{0:T(128)}, u32[]{:S(2)}) copy-start(s32[5]{0:T(128)} %constant.121.clone) | copy-start | bytes 64
  10.2 94.5 %copy-start.4 = (f32[384]{0:T(512)S(1)}, f32[384]{0:T(512)}, u32[]{:S(2)}) copy-start(f32[384]{0:T(512)} %param.10) | copy-start | bytes 4612
  10.4 99.6 %collective-permute-start.3 = (bf16[2,384,384]{2,1,0:T(8,128)(2,1)S(1)}, bf16[2,384,384]{2,1,0:T(8,128)(2,1)S(1)}, u32[]{:S(2)}, u32[]{:S(2)}) collective-permute-start(bf16[2,384,384]{2,1,0:T(8,128)(2,1)S(1)} %pad_maximum_fusion), channel_id=1, source_target_pairs={{0,32},{16,48},{32,64},{48,80},{64,96},{80,112},{96,128},{112,144}... | collective-permute-start | bytes 1769480 | tf_op jit(solution)/shard_map/ppermute | solution.py:124
  15.5 94.7 %collective-permute-start.4 = (bf16[2,384,384]{2,1,0:T(8,128)(2,1)S(1)}, bf16[2,384,384]{2,1,0:T(8,128)(2,1)}, u32[]{:S(2)}, u32[]{:S(2)}) collective-permute-start(bf16[2,384,384]{2,1,0:T(8,128)(2,1)S(1)} %pad_maximum_fusion), channel_id=1, source_target_pairs={{0,16},{16,32},{32,48},{48,64},{64,80},{80,96},{96,112},{112,128},... | collective-permute-start | bytes 1769480 | tf_op jit(solution)/shard_map/ppermute | solution.py:124
  18.1 93.3 %collective-permute-start.5 = (bf16[2,384,384]{2,1,0:T(8,128)(2,1)S(1)}, bf16[2,384,384]{2,1,0:T(8,128)(2,1)}, u32[]{:S(2)}, u32[]{:S(2)}) collective-permute-start(bf16[2,384,384]{2,1,0:T(8,128)(2,1)S(1)} %pad_maximum_fusion), channel_id=1, source_target_pairs={{16,0},{32,16},{48,32},{64,48},{80,64},{96,80},{112,96},{128,112},... | collective-permute-start | bytes 1769480 | tf_op jit(solution)/shard_map/ppermute | solution.py:124
  23.5 89.1 %collective-permute-start.6 = (bf16[2,384,384]{2,1,0:T(8,128)(2,1)S(1)}, bf16[2,384,384]{2,1,0:T(8,128)(2,1)}, u32[]{:S(2)}, u32[]{:S(2)}) collective-permute-start(bf16[2,384,384]{2,1,0:T(8,128)(2,1)S(1)} %pad_maximum_fusion), channel_id=1, source_target_pairs={{32,0},{48,16},{64,32},{80,48},{96,64},{112,80},{128,96},{144,112}... | collective-permute-start | bytes 1769480 | tf_op jit(solution)/shard_map/ppermute | solution.py:124
  25.7 3.7 %collective-permute-start = (f32[2,512]{1,0:T(2,128)S(1)}, f32[2,512]{1,0:T(2,128)S(1)}, u32[]{:S(2)}, u32[]{:S(2)}) collective-permute-start(f32[2,512]{1,0:T(2,128)S(1)} %pad_maximum_fusion.2), channel_id=1, source_target_pairs={{0,2},{2,0},{4,6},{6,4},{8,10},{10,8},{12,14},{14,12},{1,3},{3,1},... | collective-permute-start | bytes 12296 | tf_op jit(solution)/shard_map/ppermute | solution.py:103
  29.4 5.2 %collective-permute-start.1 = (f32[2,512]{1,0:T(2,128)S(1)}, f32[2,512]{1,0:T(2,128)S(1)}, u32[]{:S(2)}, u32[]{:S(2)}) collective-permute-start(f32[2,512]{1,0:T(2,128)S(1)} %fusion.13), channel_id=1, source_target_pairs={{0,4},{2,6},{4,0},{6,2},{8,12},{10,14},{12,8},{14,10},{1,5},{3,7},... | collective-permute-start | bytes 12296 | tf_op jit(solution)/shard_map/ppermute | solution.py:103
  34.6 7.6 %collective-permute-start.2 = (f32[2,512]{1,0:T(2,128)S(1)}, f32[2,512]{1,0:T(2,128)S(1)}, u32[]{:S(2)}, u32[]{:S(2)}) collective-permute-start(f32[2,512]{1,0:T(2,128)S(1)} %fusion.21), channel_id=1, source_target_pairs={{0,8},{2,10},{4,12},{6,14},{8,0},{10,2},{12,4},{14,6},{1,9},{3,11}... | collective-permute-start | bytes 12296 | tf_op jit(solution)/shard_map/ppermute | solution.py:103
  42.3 39.1 %collective-permute-start.7 = (f32[1,512]{1,0:T(1,128)S(1)}, f32[1,512]{1,0:T(1,128)S(1)}, u32[]{:S(2)}, u32[]{:S(2)}) collective-permute-start(f32[1,512]{1,0:T(1,128)S(1)} %get-tuple-element.17), channel_id=1, source_target_pairs={{0,16},{16,0},{32,48},{48,32},{64,80},{80,64},{96,112},{112,96},{1... | collective-permute-start | bytes 6152 | tf_op jit(solution)/shard_map/ppermute | solution.py:90
  81.4 5.2 %collective-permute-start.8 = (f32[2,512]{1,0:T(2,128)S(1)}, f32[2,512]{1,0:T(2,128)S(1)}, u32[]{:S(2)}, u32[]{:S(2)}) collective-permute-start(f32[2,512]{1,0:T(2,128)S(1)} %maximum_select_fusion.3), channel_id=1, source_target_pairs={{0,32},{16,48},{32,0},{48,16},{64,96},{80,112},{96,64},{112,80},{1... | collective-permute-start | bytes 12296 | tf_op jit(solution)/shard_map/ppermute | solution.py:90
  86.6 18.0 %collective-permute-start.9 = (f32[4,512]{1,0:T(4,128)S(1)}, f32[4,512]{1,0:T(4,128)S(1)}, u32[]{:S(2)}, u32[]{:S(2)}) collective-permute-start(f32[4,512]{1,0:T(4,128)S(1)} %maximum_select_fusion.2), channel_id=1, source_target_pairs={{0,64},{16,80},{32,96},{48,112},{64,0},{80,16},{96,32},{112,48},{1... | collective-permute-start | bytes 24584 | tf_op jit(solution)/shard_map/ppermute | solution.py:90
  104.7 4.8 %collective-permute-start.10 = (f32[8,512]{1,0:T(8,128)S(1)}, f32[8,512]{1,0:T(8,128)S(1)}, u32[]{:S(2)}, u32[]{:S(2)}) collective-permute-start(f32[8,512]{1,0:T(8,128)S(1)} %maximum_select_fusion.1), channel_id=1, source_target_pairs={{0,128},{16,144},{32,160},{48,176},{64,192},{80,208},{96,224},{112... | collective-permute-start | bytes 49160 | tf_op jit(solution)/shard_map/ppermute | solution.py:90
  113.7 0.7 copy-start.3
Sparse Core Ops, SparseCore 0:
  9.3 102.3 all-gather.2

commit v10 on v8

--- a/solution.py
+++ b/solution.py
@@ -14,7 +14,6 @@
 NEAR = 2
 
 EPS = 1e-06
-LOG2E = 1.4426950408889634
 
 
 def attn_kernel(sel_ref, q_ref, kn_ref, vn_ref, kf_ref, vf_ref, o_ref, kc_ref, vc_ref, *, q_blocks, slots):
@@ -24,18 +23,25 @@
         for j in range(slots):
             use_near = sel_ref[0, b, j] == 1
             rows = pl.ds(j * BLK, BLK)
-            kc_ref[rows, :] = jnp.where(
-                use_near, kn_ref[sel_ref[1, b, j], :, cols], kf_ref[sel_ref[2, b, j]]
-            )
-            vc_ref[rows, :] = jnp.where(
-                use_near, vn_ref[sel_ref[1, b, j], :, cols], vf_ref[0, sel_ref[2, b, j]]
-            )
+            ni = sel_ref[1, b, j]
+            fi = sel_ref[2, b, j]
+
+            @pl.when(use_near)
+            def _():
+                kc_ref[rows, :] = kn_ref[ni, :, cols]
+                vc_ref[rows, :] = vn_ref[ni, :, cols]
+
+            @pl.when(jnp.logical_not(use_near))
+            def _():
+                kc_ref[rows, :] = kf_ref[fi, :, cols]
+                vc_ref[rows, :] = vf_ref[0, fi]
+
         qh = q_ref[pl.ds(b * BLK, BLK), :]
         s = lax.dot_general(
             kc_ref[...], qh, (((1,), (1,)), ((), ())), preferred_element_type=jnp.float32
         ) * scale
         top = jnp.max(s, axis=0, keepdims=True)
-        w = jnp.exp2((s - top) * LOG2E)
+        w = jnp.exp(s - top)
         total = jnp.sum(w, axis=0, keepdims=True)
         acc = lax.dot_general(
             w.astype(jnp.bfloat16), vc_ref[...], (((0,), (0,)), ((), ())),
@@ -60,7 +66,7 @@
             pl.BlockSpec((tok_rows, HD), lambda h, sel_ref: (0, h)),
             pl.BlockSpec(memory_space=pltpu.VMEM),
             pl.BlockSpec(memory_space=pltpu.VMEM),
-            pl.BlockSpec((n_first, BLK, HD), lambda h, sel_ref: (0, 0, h)),
+            pl.BlockSpec(memory_space=pltpu.VMEM),
             pl.BlockSpec((1, n_first, BLK, HD), lambda h, sel_ref: (1, 0, 0, h)),
         ],
         out_specs=pl.BlockSpec((tok_rows, HD), lambda h, sel_ref: (0, h)),

time: 140 us -> 144 us (1.029)
  Pallas kernels: 10.9 us -> 15 us
    pallas_call x1, Pallas kernels: 10.9 us -> 15 us  [sparse_attend(): pl.pallas_call(kernel, grid_spec=grid_spec, out_shape=jax.ShapeDtypeStruc...]
where the time goes in v10:
time: 144 us
  starting transfers between devices  59.5 us (41%)
  waiting for transfers between devices  43.8 us (30%)
  Pallas kernels  15 us (10%)
  between operations  13.8 us (10%)
  local copies, waits for them, and re-layouts  6.47 us (4%)
  other arithmetic  5.17 us (4%)
    ppermute x4, starting transfers between devices, xor_gather(): got = lax.ppermute(held, 'frame', perm)  34.5 us
    ppermute x4, waiting for transfers between devices, xor_gather(): got = lax.ppermute(held, 'frame', perm)  30.6 us
    pallas_call x1, Pallas kernels, sparse_attend(): pl.pallas_call(kernel, grid_spec=grid_spec, out_shape=jax.ShapeDtypeStruc...  15 us
    ppermute x4, starting transfers between devices, body(): near[d] = lax.ppermute(tail, 'frame', perms[d])  13.5 us
    ppermute x3, starting transfers between devices, xor_sum(): x = x + lax.ppermute(x, axis, perm)  11.5 us
    all_gather x1, waiting for transfers between devices, body(): first = lax.all_gather(kv_raw[:, :BLK], 'frame', axis=1, tiled=False)  7.15 us
    ppermute x3, waiting for transfers between devices, xor_sum(): x = x + lax.ppermute(x, axis, perm)  6.01 us
    another operation x2, other arithmetic, body(): kv_raw = jnp.stack([k_proj, v_proj])  3.7 us
  transfers between devices with their start and end apart: 12, of which 8 were waited for; matrix products, arithmetic and copies ran while one was open for 5% of the time, Pallas kernels for 0%

profile of v10, /device:TPU:2, one launch (start us, length us, event | category | flops | bytes accessed | tf_op | source)
XLA Modules:
  0.0 143.7 jit_solution(6730327100055222456)
XLA Ops:
  6.5 1.7 %pad_maximum_fusion = bf16[2,128,384]{2,1,0:T(8,128)(2,1)} fusion(bf16[1,512,384]{2,1,0:T(8,128)(2,1)} %bitcast.29, bf16[1,512,384]{2,1,0:T(8,128)(2,1)} %bitcast.26), kind=kLoop, calls=%fused_computation.14 | loop fusion | flops 393216 | bytes 983040 | tf_op jit(solution)/shard_map/stack | solution.py:125
  8.3 2.0 %fusion.5 = bf16[2,384,384]{2,1,0:T(8,128)(2,1)} fusion(bf16[1,512,384]{2,1,0:T(8,128)(2,1)} %bitcast.27, bf16[1,512,384]{2,1,0:T(8,128)(2,1)} %bitcast.30), kind=kLoop, calls=%fused_computation.13 | loop fusion | flops 294912 | bytes 1376256 | tf_op jit(solution)/shard_map/stack | solution.py:125
  10.3 1.4 collective-permute-start.6
  11.7 1.3 collective-permute-start.5
  13.0 5.4 %collective-permute-start.4 = (bf16[2,384,384]{2,1,0:T(8,128)(2,1)}, bf16[2,384,384]{2,1,0:T(8,128)(2,1)}, u32[]{:S(2)}, u32[]{:S(2)}) collective-permute-start(bf16[2,384,384]{2,1,0:T(8,128)(2,1)} %fusion.5), channel_id=1, source_target_pairs={{0,16},{16,32},{32,48},{48,64},{64,80},{80,96},{96,112},{112,128},... | collective-permute-start | bytes 1769480 | tf_op jit(solution)/shard_map/ppermute | solution.py:130
  18.4 5.4 %collective-permute-start.3 = (bf16[2,384,384]{2,1,0:T(8,128)(2,1)}, bf16[2,384,384]{2,1,0:T(8,128)(2,1)S(1)}, u32[]{:S(2)}, u32[]{:S(2)}) collective-permute-start(bf16[2,384,384]{2,1,0:T(8,128)(2,1)} %fusion.5), channel_id=1, source_target_pairs={{0,32},{16,48},{32,64},{48,80},{64,96},{80,112},{96,128},{112,144}... | collective-permute-start | bytes 1769480 | tf_op jit(solution)/shard_map/ppermute | solution.py:130
  23.8 0.2 multiply_reduce_fusion
  24.0 0.2 fusion.2
  24.2 2.2 %collective-permute-start = (f32[2,512]{1,0:T(2,128)S(1)}, f32[2,512]{1,0:T(2,128)S(1)}, u32[]{:S(2)}, u32[]{:S(2)}) collective-permute-start(f32[2,512]{1,0:T(2,128)S(1)} %pad_maximum_fusion.1), channel_id=1, source_target_pairs={{0,2},{2,0},{4,6},{6,4},{8,10},{10,8},{12,14},{14,12},{1,3},{3,1},... | collective-permute-start | bytes 12296 | tf_op jit(solution)/shard_map/ppermute | solution.py:110
  26.4 0.1 copy.12
  26.5 1.4 collective-permute-done
  27.9 2.2 %collective-permute-start.1 = (f32[2,512]{1,0:T(2,128)S(1)}, f32[2,512]{1,0:T(2,128)S(1)}, u32[]{:S(2)}, u32[]{:S(2)}) collective-permute-start(f32[2,512]{1,0:T(2,128)S(1)} %fusion.14), channel_id=1, source_target_pairs={{0,4},{2,6},{4,0},{6,2},{8,12},{10,14},{12,8},{14,10},{1,5},{3,7},... | collective-permute-start | bytes 12296 | tf_op jit(solution)/shard_map/ppermute | solution.py:110
  30.1 3.0 %collective-permute-done.1 = f32[2,512]{1,0:T(2,128)S(1)} collective-permute-done((f32[2,512]{1,0:T(2,128)S(1)}, f32[2,512]{1,0:T(2,128)S(1)}, u32[]{:S(2)}, u32[]{:S(2)}) %collective-permute-start.1) | collective-permute-done | bytes 4128 | tf_op jit(solution)/shard_map/ppermute | solution.py:110
  33.1 7.2 %collective-permute-start.2 = (f32[2,512]{1,0:T(2,128)S(1)}, f32[2,512]{1,0:T(2,128)S(1)}, u32[]{:S(2)}, u32[]{:S(2)}) collective-permute-start(f32[2,512]{1,0:T(2,128)S(1)} %fusion.20), channel_id=1, source_target_pairs={{0,8},{2,10},{4,12},{6,14},{8,0},{10,2},{12,4},{14,6},{1,9},{3,11}... | collective-permute-start | bytes 12296 | tf_op jit(solution)/shard_map/ppermute | solution.py:110
  40.4 1.6 %collective-permute-done.2 = f32[2,512]{1,0:T(2,128)S(1)} collective-permute-done((f32[2,512]{1,0:T(2,128)S(1)}, f32[2,512]{1,0:T(2,128)S(1)}, u32[]{:S(2)}, u32[]{:S(2)}) %collective-permute-start.2) | collective-permute-done | bytes 4128 | tf_op jit(solution)/shard_map/ppermute | solution.py:110
  42.0 3.6 %collective-permute-start.7 = (f32[1,512]{1,0:T(1,128)S(1)}, f32[1,512]{1,0:T(1,128)S(1)}, u32[]{:S(2)}, u32[]{:S(2)}) collective-permute-start(f32[1,512]{1,0:T(1,128)S(1)} %get-tuple-element.13), channel_id=1, source_target_pairs={{0,16},{16,0},{32,48},{48,32},{64,80},{80,64},{96,112},{112,96},{1... | collective-permute-start | bytes 6152 | tf_op jit(solution)/shard_map/ppermute | solution.py:97
  45.6 21.0 %collective-permute-done.7 = f32[1,512]{1,0:T(1,128)S(1)} collective-permute-done((f32[1,512]{1,0:T(1,128)S(1)}, f32[1,512]{1,0:T(1,128)S(1)}, u32[]{:S(2)}, u32[]{:S(2)}) %collective-permute-start.7) | collective-permute-done | bytes 2080 | tf_op jit(solution)/shard_map/ppermute | solution.py:97
  66.6 30.7 %collective-permute-start.8 = (f32[2,512]{1,0:T(2,128)S(1)}, f32[2,512]{1,0:T(2,128)S(1)}, u32[]{:S(2)}, u32[]{:S(2)}) collective-permute-start(f32[2,512]{1,0:T(2,128)S(1)} %maximum_select_fusion.3), channel_id=1, source_target_pairs={{0,32},{16,48},{32,0},{48,16},{64,96},{80,112},{96,64},{112,80},{1... | collective-permute-start | bytes 12296 | tf_op jit(solution)/shard_map/ppermute | solution.py:97
  97.3 1.6 %collective-permute-done.8 = f32[2,512]{1,0:T(2,128)S(1)} collective-permute-done((f32[2,512]{1,0:T(2,128)S(1)}, f32[2,512]{1,0:T(2,128)S(1)}, u32[]{:S(2)}, u32[]{:S(2)}) %collective-permute-start.8) | collective-permute-done | bytes 4128 | tf_op jit(solution)/shard_map/ppermute | solution.py:97
  99.1 3.5 %collective-permute-done.9 = f32[4,512]{1,0:T(4,128)S(1)} collective-permute-done((f32[4,512]{1,0:T(4,128)S(1)}, f32[4,512]{1,0:T(4,128)S(1)}, u32[]{:S(2)}, u32[]{:S(2)}) %collective-permute-start.9) | collective-permute-done | bytes 8224 | tf_op jit(solution)/shard_map/ppermute | solution.py:97
  102.7 0.2 fusion.4.q_ref
  102.9 4.5 %collective-permute-done.10 = f32[8,512]{1,0:T(8,128)S(1)} collective-permute-done((f32[8,512]{1,0:T(8,128)S(1)}, f32[8,512]{1,0:T(8,128)S(1)}, u32[]{:S(2)}, u32[]{:S(2)}) %collective-permute-start.10) | collective-permute-done | bytes 16416 | tf_op jit(solution)/shard_map/ppermute | solution.py:97
  107.5 0.6 gather_fusion
  108.2 1.1 fusion.17
  109.5 1.1 fusion.16
  110.7 1.1 fusion.15
  112.1 0.4 copy-done.4
  112.5 0.4 multiply_convert_fusion.kn_ref
  112.9 7.2 %all-gather.3.cloned.1.call-done = bf16[2,2048,384]{2,1,0:T(8,128)(2,1)} async-done(((bf16[2,128,384]{2,1,0:T(8,128)(2,1)}), bf16[2,2048,384]{2,1,0:T(8,128)(2,1)}) %all-gather.3.cloned.1.call-update) | async-done | bytes 3145744 | tf_op jit(solution)/shard_map/all_gather | solution.py:126
  120.0 1.4 slice-done
  121.5 0.4 fusion.1.kf_ref
  121.9 15.0 %shard_map.73 = bf16[512,384]{1,0:T(8,128)(2,1)} custom-call(s32[3,4,12]{2,1,0:T(4,128)S(1)} %pad_add_fusion.sel_ref, bf16[512,384]{1,0:T(8,128)(2,1)S(1)} %fusion.4.q_ref, bf16[15,128,384]{2,1,0:T(8,128)(2,1)S(1)} %multiply_convert_fusion.kn_ref, bf16[15,128,384]{2,1,0:T(8,128)(2,1)S(1)} %constant_dynamic-update-slice_fusion.5.vn_ref, ...), custom_call_target="tpu_custom_call" | custom-call | flops 1207959552 | bytes 6881280 | tf_op jit(solution)/shard_map/pallas_call | solution.py:79
  (53 shorter events, 1.0 us)
Async XLA Ops:
  6.5 19.8 %copy-start = (s32[64,12]{0,1:T(8,128)S(1)}, s32[64,12]{0,1:T(8,128)}, u32[]{:S(2)}) copy-start(s32[64,12]{0,1:T(8,128)} %param.12) | copy-start | bytes 9220
  6.5 17.3 %copy-start.1 = (bf16[512,384]{1,0:T(8,128)(2,1)S(1)}, bf16[512,384]{1,0:T(8,128)(2,1)}, u32[]{:S(2)}) copy-start(bf16[512,384]{1,0:T(8,128)(2,1)} %param.8) | copy-start | bytes 1179652
  6.5 113.5 %all-gather.3.cloned.1.call-start = ((), (), s32[]{:S(2)}) async-start(), calls=%async_computation | async-start | bytes 3342336 | tf_op jit(solution)/shard_map/all_gather | solution.py:126
  6.5 17.4 %copy-start.3 = (bf16[512,384]{1,0:T(8,128)(2,1)S(1)}, bf16[512,384]{1,0:T(8,128)(2,1)}, u32[]{:S(2)}) copy-start(bf16[512,384]{1,0:T(8,128)(2,1)} %param.7) | copy-start | bytes 1179652
  8.3 37.3 %copy-start.6 = (s32[5]{0:T(128)S(1)}, s32[5]{0:T(128)}, u32[]{:S(2)}) copy-start(s32[5]{0:T(128)} %constant.121.clone) | copy-start | bytes 64
  8.3 90.8 %copy-start.2 = (bf16[512,384]{1,0:T(8,128)(2,1)S(1)}, bf16[512,384]{1,0:T(8,128)(2,1)}, u32[]{:S(2)}) copy-start(bf16[512,384]{1,0:T(8,128)(2,1)} %param.9) | copy-start | bytes 1179652
  10.3 92.5 %copy-start.5 = (f32[384]{0:T(512)S(1)}, f32[384]{0:T(512)}, u32[]{:S(2)}) copy-start(f32[384]{0:T(512)} %param.10) | copy-start | bytes 4612
  10.3 100.4 %collective-permute-start.6 = (bf16[2,384,384]{2,1,0:T(8,128)(2,1)}, bf16[2,384,384]{2,1,0:T(8,128)(2,1)}, u32[]{:S(2)}, u32[]{:S(2)}) collective-permute-start(bf16[2,384,384]{2,1,0:T(8,128)(2,1)} %fusion.5), channel_id=1, source_target_pairs={{32,0},{48,16},{64,32},{80,48},{96,64},{112,80},{128,96},{144,112}... | collective-permute-start | bytes 1769480 | tf_op jit(solution)/shard_map/ppermute | solution.py:130
  11.7 97.8 %collective-permute-start.5 = (bf16[2,384,384]{2,1,0:T(8,128)(2,1)}, bf16[2,384,384]{2,1,0:T(8,128)(2,1)}, u32[]{:S(2)}, u32[]{:S(2)}) collective-permute-start(bf16[2,384,384]{2,1,0:T(8,128)(2,1)} %fusion.5), channel_id=1, source_target_pairs={{16,0},{32,16},{48,32},{64,48},{80,64},{96,80},{112,96},{128,112},... | collective-permute-start | bytes 1769480 | tf_op jit(solution)/shard_map/ppermute | solution.py:130
  13.0 95.2 %collective-permute-start.4 = (bf16[2,384,384]{2,1,0:T(8,128)(2,1)}, bf16[2,384,384]{2,1,0:T(8,128)(2,1)}, u32[]{:S(2)}, u32[]{:S(2)}) collective-permute-start(bf16[2,384,384]{2,1,0:T(8,128)(2,1)} %fusion.5), channel_id=1, source_target_pairs={{0,16},{16,32},{32,48},{48,64},{64,80},{80,96},{96,112},{112,128},... | collective-permute-start | bytes 1769480 | tf_op jit(solution)/shard_map/ppermute | solution.py:130
  18.4 89.7 %collective-permute-start.3 = (bf16[2,384,384]{2,1,0:T(8,128)(2,1)}, bf16[2,384,384]{2,1,0:T(8,128)(2,1)S(1)}, u32[]{:S(2)}, u32[]{:S(2)}) collective-permute-start(bf16[2,384,384]{2,1,0:T(8,128)(2,1)} %fusion.5), channel_id=1, source_target_pairs={{0,32},{16,48},{32,64},{48,80},{64,96},{80,112},{96,128},{112,144}... | collective-permute-start | bytes 1769480 | tf_op jit(solution)/shard_map/ppermute | solution.py:130
  24.2 3.7 %collective-permute-start = (f32[2,512]{1,0:T(2,128)S(1)}, f32[2,512]{1,0:T(2,128)S(1)}, u32[]{:S(2)}, u32[]{:S(2)}) collective-permute-start(f32[2,512]{1,0:T(2,128)S(1)} %pad_maximum_fusion.1), channel_id=1, source_target_pairs={{0,2},{2,0},{4,6},{6,4},{8,10},{10,8},{12,14},{14,12},{1,3},{3,1},... | collective-permute-start | bytes 12296 | tf_op jit(solution)/shard_map/ppermute | solution.py:110
  27.9 5.2 %collective-permute-start.1 = (f32[2,512]{1,0:T(2,128)S(1)}, f32[2,512]{1,0:T(2,128)S(1)}, u32[]{:S(2)}, u32[]{:S(2)}) collective-permute-start(f32[2,512]{1,0:T(2,128)S(1)} %fusion.14), channel_id=1, source_target_pairs={{0,4},{2,6},{4,0},{6,2},{8,12},{10,14},{12,8},{14,10},{1,5},{3,7},... | collective-permute-start | bytes 12296 | tf_op jit(solution)/shard_map/ppermute | solution.py:110
  33.1 8.8 %collective-permute-start.2 = (f32[2,512]{1,0:T(2,128)S(1)}, f32[2,512]{1,0:T(2,128)S(1)}, u32[]{:S(2)}, u32[]{:S(2)}) collective-permute-start(f32[2,512]{1,0:T(2,128)S(1)} %fusion.20), channel_id=1, source_target_pairs={{0,8},{2,10},{4,12},{6,14},{8,0},{10,2},{12,4},{14,6},{1,9},{3,11}... | collective-permute-start | bytes 12296 | tf_op jit(solution)/shard_map/ppermute | solution.py:110
  42.0 24.6 %collective-permute-start.7 = (f32[1,512]{1,0:T(1,128)S(1)}, f32[1,512]{1,0:T(1,128)S(1)}, u32[]{:S(2)}, u32[]{:S(2)}) collective-permute-start(f32[1,512]{1,0:T(1,128)S(1)} %get-tuple-element.13), channel_id=1, source_target_pairs={{0,16},{16,0},{32,48},{48,32},{64,80},{80,64},{96,112},{112,96},{1... | collective-permute-start | bytes 6152 | tf_op jit(solution)/shard_map/ppermute | solution.py:97
  66.6 32.3 %collective-permute-start.8 = (f32[2,512]{1,0:T(2,128)S(1)}, f32[2,512]{1,0:T(2,128)S(1)}, u32[]{:S(2)}, u32[]{:S(2)}) collective-permute-start(f32[2,512]{1,0:T(2,128)S(1)} %maximum_select_fusion.3), channel_id=1, source_target_pairs={{0,32},{16,48},{32,0},{48,16},{64,96},{80,112},{96,64},{112,80},{1... | collective-permute-start | bytes 12296 | tf_op jit(solution)/shard_map/ppermute | solution.py:97
  98.9 3.8 %collective-permute-start.9 = (f32[4,512]{1,0:T(4,128)S(1)}, f32[4,512]{1,0:T(4,128)S(1)}, u32[]{:S(2)}, u32[]{:S(2)}) collective-permute-start(f32[4,512]{1,0:T(4,128)S(1)} %maximum_select_fusion.2), channel_id=1, source_target_pairs={{0,64},{16,80},{32,96},{48,112},{64,0},{80,16},{96,32},{112,48},{1... | collective-permute-start | bytes 24584 | tf_op jit(solution)/shard_map/ppermute | solution.py:97
  102.6 4.8 %collective-permute-start.10 = (f32[8,512]{1,0:T(8,128)S(1)}, f32[8,512]{1,0:T(8,128)S(1)}, u32[]{:S(2)}, u32[]{:S(2)}) collective-permute-start(f32[8,512]{1,0:T(8,128)S(1)} %maximum_select_fusion.1), channel_id=1, source_target_pairs={{0,128},{16,144},{32,160},{48,176},{64,192},{80,208},{96,224},{112... | collective-permute-start | bytes 49160 | tf_op jit(solution)/shard_map/ppermute | solution.py:97
  111.8 0.7 copy-start.4
  120.0 1.4 slice-start
Sparse Core Ops, SparseCore 0:
  9.1 110.8 all-gather.2

commit v11 on v8

--- a/solution.py
+++ b/solution.py
@@ -14,28 +14,31 @@
 NEAR = 2
 
 EPS = 1e-06
-LOG2E = 1.4426950408889634
 
 
-def attn_kernel(sel_ref, q_ref, kn_ref, vn_ref, kf_ref, vf_ref, o_ref, kc_ref, vc_ref, *, q_blocks, slots):
+def attn_kernel(
+    sel_ref, q_ref, kn_ref, vn_ref, kf_ref, vf_ref, o_ref, kc_ref, vc_ref, kb_ref, vb_ref,
+    *, q_blocks, slots,
+):
     scale = 1.0 / math.sqrt(HD)
     cols = pl.ds(pl.multiple_of(pl.program_id(0) * HD, HD), HD)
+    n_near = kn_ref.shape[0]
+    n_first = kf_ref.shape[0]
+    kb_ref[pl.ds(0, n_near)] = kn_ref[:, :, cols]
+    vb_ref[pl.ds(0, n_near)] = vn_ref[:, :, cols]
+    kb_ref[pl.ds(n_near, n_first)] = kf_ref[...]
+    vb_ref[pl.ds(n_near, n_first)] = vf_ref[0]
     for b in range(q_blocks):
         for j in range(slots):
-            use_near = sel_ref[0, b, j] == 1
             rows = pl.ds(j * BLK, BLK)
-            kc_ref[rows, :] = jnp.where(
-                use_near, kn_ref[sel_ref[1, b, j], :, cols], kf_ref[sel_ref[2, b, j]]
-            )
-            vc_ref[rows, :] = jnp.where(
-                use_near, vn_ref[sel_ref[1, b, j], :, cols], vf_ref[0, sel_ref[2, b, j]]
-            )
+            kc_ref[rows, :] = kb_ref[sel_ref[b, j]]
+            vc_ref[rows, :] = vb_ref[sel_ref[b, j]]
         qh = q_ref[pl.ds(b * BLK, BLK), :]
         s = lax.dot_general(
             kc_ref[...], qh, (((1,), (1,)), ((), ())), preferred_element_type=jnp.float32
         ) * scale
         top = jnp.max(s, axis=0, keepdims=True)
-        w = jnp.exp2((s - top) * LOG2E)
+        w = jnp.exp(s - top)
         total = jnp.sum(w, axis=0, keepdims=True)
         acc = lax.dot_general(
             w.astype(jnp.bfloat16), vc_ref[...], (((0,), (0,)), ((), ())),
@@ -49,7 +52,7 @@
     tok_rows, width = qn.shape
     heads = width // HD
     q_blocks = tok_rows // BLK
-    slots = sel.shape[2]
+    slots = sel.shape[1]
     n_near = kn_near.shape[0]
     n_first = kn_first.shape[0]
     kernel = functools.partial(attn_kernel, q_blocks=q_blocks, slots=slots)
@@ -67,6 +70,8 @@
         scratch_shapes=[
             pltpu.VMEM((slots * BLK, HD), jnp.bfloat16),
             pltpu.VMEM((slots * BLK, HD), jnp.bfloat16),
+            pltpu.VMEM((n_near + n_first, BLK, HD), jnp.bfloat16),
+            pltpu.VMEM((n_near + n_first, BLK, HD), jnp.bfloat16),
         ],
     )
     flops = 4 * q_blocks * slots * heads * BLK * BLK * HD
@@ -155,7 +160,7 @@
     near_ok = (jnp.abs(dist) <= NEAR) & (within > 0)
     near_idx = jnp.clip((dist + NEAR) * (blocks - 1) + within - 1, 0, len(offsets) * (blocks - 1) - 1)
     first_idx = jnp.clip(key_slab, 0, n_frame - 1)
-    sel = jnp.stack([near_ok.astype(jnp.int32), near_idx, first_idx]).astype(jnp.int32)
+    sel = jnp.where(near_ok, near_idx, len(offsets) * (blocks - 1) + first_idx).astype(jnp.int32)
     return sparse_attend(sel, q_norm, kn_near, v_near, kn_first, first)
 
 

time: 140 us -> 144 us (1.029)
  the two profiles are of different devices: /device:TPU:2 before, /device:TPU:24 now
where the time goes in v11:
time: 144 us
  waiting for transfers between devices  82 us (57%)
  starting transfers between devices  26.4 us (18%)
  between operations  13.9 us (10%)
  Pallas kernels  10 us (7%)
  local copies, waits for them, and re-layouts  6.46 us (4%)
  other arithmetic  5.09 us (4%)
    ppermute x3, waiting for transfers between devices, xor_sum(): x = x + lax.ppermute(x, axis, perm)  65.4 us
    ppermute x4, waiting for transfers between devices, xor_gather(): got = lax.ppermute(held, 'frame', perm)  16.5 us
    ppermute x4, starting transfers between devices, body(): near[d] = lax.ppermute(tail, 'frame', perms[d])  14.1 us
    ppermute x3, starting transfers between devices, xor_sum(): x = x + lax.ppermute(x, axis, perm)  12 us
    pallas_call x1, Pallas kernels, sparse_attend(): pl.pallas_call(kernel, grid_spec=grid_spec, out_shape=jax.ShapeDtypeStruc...  10 us
    slice x5, local copies, waits for them, and re-layouts, body(): near[d][1].reshape(blocks - 1, BLK, width)  3.43 us
  transfers between devices with their start and end apart: 12, of which 6 were waited for; matrix products, arithmetic and copies ran while one was open for 5% of the time, Pallas kernels for 0%

profile of v11, /device:TPU:24, one launch (start us, length us, event | category | flops | bytes accessed | tf_op | source)
XLA Modules:
  0.0 143.9 jit_solution(4066023156211310639)
XLA Ops:
  6.6 1.7 %pad_maximum_fusion = bf16[2,128,384]{2,1,0:T(8,128)(2,1)} fusion(bf16[1,512,384]{2,1,0:T(8,128)(2,1)} %bitcast.23, bf16[1,512,384]{2,1,0:T(8,128)(2,1)} %bitcast.20), kind=kLoop, calls=%fused_computation.14 | loop fusion | flops 393216 | bytes 983040 | tf_op jit(solution)/shard_map/stack | solution.py:124
  8.3 1.1 multiply_reduce_fusion
  9.5 0.2 fusion.2
  9.7 1.6 %collective-permute-start = (f32[2,512]{1,0:T(2,128)S(1)}, f32[2,512]{1,0:T(2,128)S(1)}, u32[]{:S(2)}, u32[]{:S(2)}) collective-permute-start(f32[2,512]{1,0:T(2,128)S(1)} %pad_maximum_fusion.1), channel_id=1, source_target_pairs={{0,2},{2,0},{4,6},{6,4},{8,10},{10,8},{12,14},{14,12},{1,3},{3,1},... | collective-permute-start | bytes 12296 | tf_op jit(solution)/shard_map/ppermute | solution.py:109
  11.3 2.1 %collective-permute-done = f32[2,512]{1,0:T(2,128)S(1)} collective-permute-done((f32[2,512]{1,0:T(2,128)S(1)}, f32[2,512]{1,0:T(2,128)S(1)}, u32[]{:S(2)}, u32[]{:S(2)}) %collective-permute-start) | collective-permute-done | bytes 4128 | tf_op jit(solution)/shard_map/ppermute | solution.py:109
  13.4 3.1 %collective-permute-start.1 = (f32[2,512]{1,0:T(2,128)S(1)}, f32[2,512]{1,0:T(2,128)S(1)}, u32[]{:S(2)}, u32[]{:S(2)}) collective-permute-start(f32[2,512]{1,0:T(2,128)S(1)} %fusion.15), channel_id=1, source_target_pairs={{0,4},{2,6},{4,0},{6,2},{8,12},{10,14},{12,8},{14,10},{1,5},{3,7},... | collective-permute-start | bytes 12296 | tf_op jit(solution)/shard_map/ppermute | solution.py:109
  16.5 0.9 fusion.5
  17.4 3.1 %collective-permute-start.6 = (bf16[2,384,384]{2,1,0:T(8,128)(2,1)}, bf16[2,384,384]{2,1,0:T(8,128)(2,1)}, u32[]{:S(2)}, u32[]{:S(2)}) collective-permute-start(bf16[2,384,384]{2,1,0:T(8,128)(2,1)} %fusion.5), channel_id=1, source_target_pairs={{32,0},{48,16},{64,32},{80,48},{96,64},{112,80},{128,96},{144,112}... | collective-permute-start | bytes 1769480 | tf_op jit(solution)/shard_map/ppermute | solution.py:129
  20.5 1.9 %collective-permute-start.5 = (bf16[2,384,384]{2,1,0:T(8,128)(2,1)}, bf16[2,384,384]{2,1,0:T(8,128)(2,1)}, u32[]{:S(2)}, u32[]{:S(2)}) collective-permute-start(bf16[2,384,384]{2,1,0:T(8,128)(2,1)} %fusion.5), channel_id=1, source_target_pairs={{16,0},{32,16},{48,32},{64,48},{80,64},{96,80},{112,96},{128,112},... | collective-permute-start | bytes 1769480 | tf_op jit(solution)/shard_map/ppermute | solution.py:129
  22.5 6.0 %collective-permute-start.4 = (bf16[2,384,384]{2,1,0:T(8,128)(2,1)}, bf16[2,384,384]{2,1,0:T(8,128)(2,1)}, u32[]{:S(2)}, u32[]{:S(2)}) collective-permute-start(bf16[2,384,384]{2,1,0:T(8,128)(2,1)} %fusion.5), channel_id=1, source_target_pairs={{0,16},{16,32},{32,48},{48,64},{64,80},{80,96},{96,112},{112,128},... | collective-permute-start | bytes 1769480 | tf_op jit(solution)/shard_map/ppermute | solution.py:129
  28.5 3.0 %collective-permute-start.3 = (bf16[2,384,384]{2,1,0:T(8,128)(2,1)}, bf16[2,384,384]{2,1,0:T(8,128)(2,1)S(1)}, u32[]{:S(2)}, u32[]{:S(2)}) collective-permute-start(bf16[2,384,384]{2,1,0:T(8,128)(2,1)} %fusion.5), channel_id=1, source_target_pairs={{0,32},{16,48},{32,64},{48,80},{64,96},{80,112},{96,128},{112,144}... | collective-permute-start | bytes 1769480 | tf_op jit(solution)/shard_map/ppermute | solution.py:129
  31.5 7.3 %collective-permute-start.2 = (f32[2,512]{1,0:T(2,128)S(1)}, f32[2,512]{1,0:T(2,128)S(1)}, u32[]{:S(2)}, u32[]{:S(2)}) collective-permute-start(f32[2,512]{1,0:T(2,128)S(1)} %fusion.21), channel_id=1, source_target_pairs={{0,8},{2,10},{4,12},{6,14},{8,0},{10,2},{12,4},{14,6},{1,9},{3,11}... | collective-permute-start | bytes 12296 | tf_op jit(solution)/shard_map/ppermute | solution.py:109
  38.9 0.1 copy.9
  39.0 63.3 %collective-permute-done.2 = f32[2,512]{1,0:T(2,128)S(1)} collective-permute-done((f32[2,512]{1,0:T(2,128)S(1)}, f32[2,512]{1,0:T(2,128)S(1)}, u32[]{:S(2)}, u32[]{:S(2)}) %collective-permute-start.2) | collective-permute-done | bytes 4128 | tf_op jit(solution)/shard_map/ppermute | solution.py:109
  102.3 0.1 collective-permute-start.7
  102.5 3.5 %collective-permute-done.7 = f32[1,512]{1,0:T(1,128)S(1)} collective-permute-done((f32[1,512]{1,0:T(1,128)S(1)}, f32[1,512]{1,0:T(1,128)S(1)}, u32[]{:S(2)}, u32[]{:S(2)}) %collective-permute-start.7) | collective-permute-done | bytes 2080 | tf_op jit(solution)/shard_map/ppermute | solution.py:96
  106.0 0.1 collective-permute-start.8
  106.2 5.0 %collective-permute-done.8 = f32[2,512]{1,0:T(2,128)S(1)} collective-permute-done((f32[2,512]{1,0:T(2,128)S(1)}, f32[2,512]{1,0:T(2,128)S(1)}, u32[]{:S(2)}, u32[]{:S(2)}) %collective-permute-start.8) | collective-permute-done | bytes 4128 | tf_op jit(solution)/shard_map/ppermute | solution.py:96
  111.2 0.1 collective-permute-start.9
  111.5 3.5 %collective-permute-done.9 = f32[4,512]{1,0:T(4,128)S(1)} collective-permute-done((f32[4,512]{1,0:T(4,128)S(1)}, f32[4,512]{1,0:T(4,128)S(1)}, u32[]{:S(2)}, u32[]{:S(2)}) %collective-permute-start.9) | collective-permute-done | bytes 8224 | tf_op jit(solution)/shard_map/ppermute | solution.py:96
  115.0 0.1 collective-permute-start.10
  115.1 0.2 fusion.4.q_ref
  115.3 4.4 %collective-permute-done.10 = f32[8,512]{1,0:T(8,128)S(1)} collective-permute-done((f32[8,512]{1,0:T(8,128)S(1)}, f32[8,512]{1,0:T(8,128)S(1)}, u32[]{:S(2)}, u32[]{:S(2)}) %collective-permute-start.10) | collective-permute-done | bytes 16416 | tf_op jit(solution)/shard_map/ppermute | solution.py:96
  119.7 0.6 gather_fusion
  120.5 1.1 fusion.18
  121.7 1.1 fusion.17
  122.9 1.1 fusion.16
  124.3 0.4 copy-done.4
  124.7 0.4 multiply_convert_fusion.kn_ref
  125.2 1.4 slice-done
  126.6 0.4 fusion.1.kf_ref
  127.0 10.0 %shard_map.73 = bf16[512,384]{1,0:T(8,128)(2,1)} custom-call(s32[4,12]{1,0:T(4,128)S(1)} %add_select_fusion.2.sel_ref, bf16[512,384]{1,0:T(8,128)(2,1)S(1)} %fusion.4.q_ref, bf16[15,128,384]{2,1,0:T(8,128)(2,1)S(1)} %multiply_convert_fusion.kn_ref, bf16[15,128,384]{2,1,0:T(8,128)(2,1)S(1)} %constant_dynamic-update-slice_fusion.5.vn_ref, ...), custom_call_target="tpu_custom_call" | custom-call | flops 1207959552 | bytes 6881280 | tf_op jit(solution)/shard_map/pallas_call | solution.py:78
  (51 shorter events, 0.9 us)
Async XLA Ops:
  6.5 32.3 %copy-start = (s32[64,12]{0,1:T(8,128)S(1)}, s32[64,12]{0,1:T(8,128)}, u32[]{:S(2)}) copy-start(s32[64,12]{0,1:T(8,128)} %param.12) | copy-start | bytes 9220
  6.5 10.0 %copy-start.1 = (bf16[512,384]{1,0:T(8,128)(2,1)S(1)}, bf16[512,384]{1,0:T(8,128)(2,1)}, u32[]{:S(2)}) copy-start(bf16[512,384]{1,0:T(8,128)(2,1)} %param.8) | copy-start | bytes 1179652
  6.5 10.0 %copy-start.2 = (bf16[512,384]{1,0:T(8,128)(2,1)S(1)}, bf16[512,384]{1,0:T(8,128)(2,1)}, u32[]{:S(2)}) copy-start(bf16[512,384]{1,0:T(8,128)(2,1)} %param.9) | copy-start | bytes 1179652
  6.5 3.0 %copy-start.3 = (bf16[512,384]{1,0:T(8,128)(2,1)S(1)}, bf16[512,384]{1,0:T(8,128)(2,1)}, u32[]{:S(2)}) copy-start(bf16[512,384]{1,0:T(8,128)(2,1)} %param.7) | copy-start | bytes 1179652
  6.5 118.6 %all-gather.3.cloned.1.call-start = ((), (), s32[]{:S(2)}) async-start(), calls=%async_computation | async-start | bytes 3342336 | tf_op jit(solution)/shard_map/all_gather | solution.py:125
  8.3 97.8 %copy-start.6 = (s32[5]{0:T(128)S(1)}, s32[5]{0:T(128)}, u32[]{:S(2)}) copy-start(s32[5]{0:T(128)} %constant.122.clone) | copy-start | bytes 64
  9.7 105.4 %copy-start.5 = (f32[384]{0:T(512)S(1)}, f32[384]{0:T(512)}, u32[]{:S(2)}) copy-start(f32[384]{0:T(512)} %param.10) | copy-start | bytes 4612
  9.7 3.7 %collective-permute-start = (f32[2,512]{1,0:T(2,128)S(1)}, f32[2,512]{1,0:T(2,128)S(1)}, u32[]{:S(2)}, u32[]{:S(2)}) collective-permute-start(f32[2,512]{1,0:T(2,128)S(1)} %pad_maximum_fusion.1), channel_id=1, source_target_pairs={{0,2},{2,0},{4,6},{6,4},{8,10},{10,8},{12,14},{14,12},{1,3},{3,1},... | collective-permute-start | bytes 12296 | tf_op jit(solution)/shard_map/ppermute | solution.py:109
  13.4 18.1 %collective-permute-start.1 = (f32[2,512]{1,0:T(2,128)S(1)}, f32[2,512]{1,0:T(2,128)S(1)}, u32[]{:S(2)}, u32[]{:S(2)}) collective-permute-start(f32[2,512]{1,0:T(2,128)S(1)} %fusion.15), channel_id=1, source_target_pairs={{0,4},{2,6},{4,0},{6,2},{8,12},{10,14},{12,8},{14,10},{1,5},{3,7},... | collective-permute-start | bytes 12296 | tf_op jit(solution)/shard_map/ppermute | solution.py:109
  17.4 105.5 %collective-permute-start.6 = (bf16[2,384,384]{2,1,0:T(8,128)(2,1)}, bf16[2,384,384]{2,1,0:T(8,128)(2,1)}, u32[]{:S(2)}, u32[]{:S(2)}) collective-permute-start(bf16[2,384,384]{2,1,0:T(8,128)(2,1)} %fusion.5), channel_id=1, source_target_pairs={{32,0},{48,16},{64,32},{80,48},{96,64},{112,80},{128,96},{144,112}... | collective-permute-start | bytes 1769480 | tf_op jit(solution)/shard_map/ppermute | solution.py:129
  20.5 101.2 %collective-permute-start.5 = (bf16[2,384,384]{2,1,0:T(8,128)(2,1)}, bf16[2,384,384]{2,1,0:T(8,128)(2,1)}, u32[]{:S(2)}, u32[]{:S(2)}) collective-permute-start(bf16[2,384,384]{2,1,0:T(8,128)(2,1)} %fusion.5), channel_id=1, source_target_pairs={{16,0},{32,16},{48,32},{64,48},{80,64},{96,80},{112,96},{128,112},... | collective-permute-start | bytes 1769480 | tf_op jit(solution)/shard_map/ppermute | solution.py:129
  22.5 98.0 %collective-permute-start.4 = (bf16[2,384,384]{2,1,0:T(8,128)(2,1)}, bf16[2,384,384]{2,1,0:T(8,128)(2,1)}, u32[]{:S(2)}, u32[]{:S(2)}) collective-permute-start(bf16[2,384,384]{2,1,0:T(8,128)(2,1)} %fusion.5), channel_id=1, source_target_pairs={{0,16},{16,32},{32,48},{48,64},{64,80},{80,96},{96,112},{112,128},... | collective-permute-start | bytes 1769480 | tf_op jit(solution)/shard_map/ppermute | solution.py:129
  28.5 91.8 %collective-permute-start.3 = (bf16[2,384,384]{2,1,0:T(8,128)(2,1)}, bf16[2,384,384]{2,1,0:T(8,128)(2,1)S(1)}, u32[]{:S(2)}, u32[]{:S(2)}) collective-permute-start(bf16[2,384,384]{2,1,0:T(8,128)(2,1)} %fusion.5), channel_id=1, source_target_pairs={{0,32},{16,48},{32,64},{48,80},{64,96},{80,112},{96,128},{112,144}... | collective-permute-start | bytes 1769480 | tf_op jit(solution)/shard_map/ppermute | solution.py:129
  31.5 70.8 %collective-permute-start.2 = (f32[2,512]{1,0:T(2,128)S(1)}, f32[2,512]{1,0:T(2,128)S(1)}, u32[]{:S(2)}, u32[]{:S(2)}) collective-permute-start(f32[2,512]{1,0:T(2,128)S(1)} %fusion.21), channel_id=1, source_target_pairs={{0,8},{2,10},{4,12},{6,14},{8,0},{10,2},{12,4},{14,6},{1,9},{3,11}... | collective-permute-start | bytes 12296 | tf_op jit(solution)/shard_map/ppermute | solution.py:109
  102.3 3.7 %collective-permute-start.7 = (f32[1,512]{1,0:T(1,128)S(1)}, f32[1,512]{1,0:T(1,128)S(1)}, u32[]{:S(2)}, u32[]{:S(2)}) collective-permute-start(f32[1,512]{1,0:T(1,128)S(1)} %get-tuple-element.13), channel_id=1, source_target_pairs={{0,16},{16,0},{32,48},{48,32},{64,80},{80,64},{96,112},{112,96},{1... | collective-permute-start | bytes 6152 | tf_op jit(solution)/shard_map/ppermute | solution.py:96
  106.0 5.2 %collective-permute-start.8 = (f32[2,512]{1,0:T(2,128)S(1)}, f32[2,512]{1,0:T(2,128)S(1)}, u32[]{:S(2)}, u32[]{:S(2)}) collective-permute-start(f32[2,512]{1,0:T(2,128)S(1)} %maximum_select_fusion.3), channel_id=1, source_target_pairs={{0,32},{16,48},{32,0},{48,16},{64,96},{80,112},{96,64},{112,80},{1... | collective-permute-start | bytes 12296 | tf_op jit(solution)/shard_map/ppermute | solution.py:96
  111.2 3.7 %collective-permute-start.9 = (f32[4,512]{1,0:T(4,128)S(1)}, f32[4,512]{1,0:T(4,128)S(1)}, u32[]{:S(2)}, u32[]{:S(2)}) collective-permute-start(f32[4,512]{1,0:T(4,128)S(1)} %maximum_select_fusion.2), channel_id=1, source_target_pairs={{0,64},{16,80},{32,96},{48,112},{64,0},{80,16},{96,32},{112,48},{1... | collective-permute-start | bytes 24584 | tf_op jit(solution)/shard_map/ppermute | solution.py:96
  115.0 4.7 %collective-permute-start.10 = (f32[8,512]{1,0:T(8,128)S(1)}, f32[8,512]{1,0:T(8,128)S(1)}, u32[]{:S(2)}, u32[]{:S(2)}) collective-permute-start(f32[8,512]{1,0:T(8,128)S(1)} %maximum_select_fusion.1), channel_id=1, source_target_pairs={{0,128},{16,144},{32,160},{48,176},{64,192},{80,208},{96,224},{112... | collective-permute-start | bytes 49160 | tf_op jit(solution)/shard_map/ppermute | solution.py:96
  124.0 0.7 copy-start.4
  125.2 1.4 slice-start
Sparse Core Ops, SparseCore 0:
  9.1 106.3 all-gather.2
